TPU v7x, 256 devices: a whole 4x4x8 slice. The times are simulated.
256 devices in a mesh: lon: 16 (over x, y_lo, core), lat: 16 (over y_hi, z).
Axes of the slice: x: 4, y: 4 (y_hi: 2, y_lo: 2; y = y_hi * 2 + y_lo), z: 8, core: 2. Of those that a mesh axis runs over, the one named last changes fastest.
Arguments:
- height: float32 [3072, 7200], P('lat', 'lon'), may hold values from 0.4 to 1.6
- east_wind: float32 [3072, 7200], P('lat', 'lon'), may hold values from -1.5 to 1.5
- north_wind: float32 [3072, 7200], P('lat', 'lon'), may hold values from -1.5 to 1.5
- cutoffs: int32 [512], replicated, may hold values from 1 to 64
Outputs:
- height_final: float32 [3072, 7200], P('lat', 'lon')
- east_final: float32 [3072, 7200], P('lat', 'lon')
- north_final: float32 [3072, 7200], P('lat', 'lon')
All inputs are finite; a program needn't handle non-finite values.
Results may differ from a plain program's by a relative error of at most 0.0002.
Values sent between devices are 32-bit elements; how exact they have to be, the bound alone decides.
No kernel may reach another device: no remote copies, remote signals or barrier semaphores. Data moves between devices by JAX's collectives and lax.ppermute only.
A program may use at most 128 MiB of HBM per device.

v0:
```python
import math

import jax
import jax.numpy as jnp
from jax import lax
from jax.sharding import PartitionSpec as P

NLON = 7200
LAT_ROWS = 3600
KMAX = 64
STEPS = 2


COURANT = 0.1
OMEGA_RATE = 1.5


def with_halo(value, sides, width, wrap):
    for axis, dim in sides:
        devices, length = (lax.axis_size(axis), value.shape[dim])
        up = [(i, (i + 1) % devices) for i in range(devices if wrap else devices - 1)]
        down = [(j, i) for i, j in up]
        last = lax.slice_in_dim(value, length - width, length, axis=dim)
        first = lax.slice_in_dim(value, 0, width, axis=dim)
        before = lax.ppermute(last, axis, up)
        after = lax.ppermute(first, axis, down)
        value = jnp.concatenate([before, value, after], axis=dim)
    return value


def from_behind(value, axis, by):
    devices = lax.axis_size(axis)
    return lax.ppermute(value, axis, [(i, (i + by) % devices) for i in range(devices)])


def local_table(width):
    waves = jnp.arange(KMAX + 1, dtype=jnp.int32)
    columns = lax.axis_index("lon") * width + jnp.arange(width, dtype=jnp.int32)
    phase = waves[:, None] * columns[None, :] % NLON
    angle = phase.astype(jnp.float32) * (2.0 * math.pi / NLON)
    return jnp.concatenate([jnp.cos(angle), jnp.sin(angle)], axis=0)


def spectral_weights(cut_rows):
    waves = jnp.arange(KMAX + 1, dtype=jnp.int32)
    scale = jnp.where(waves == 0, 1.0 / NLON, 2.0 / NLON).astype(jnp.float32)
    keep = (waves[None, :] <= cut_rows[:, None]).astype(jnp.float32) * scale[None, :]
    return jnp.concatenate([keep, keep], axis=1)


def project(fields, table):
    return jnp.einsum("fnw,kw->fnk", fields, table, precision=lax.Precision.HIGHEST)


def expand(coeffs, table):
    return jnp.einsum("fnk,kw->fnw", coeffs, table, precision=lax.Precision.HIGHEST)


def low_pass(fields, cut_rows, active, table):
    weights = spectral_weights(cut_rows)
    coeffs = lax.psum(project(fields, table), "lon") * weights[None]
    smooth = expand(coeffs, table)
    return jnp.where(active[None, :, None], smooth, fields)


def filter_state(state, cutoffs, table):
    rows_here = state.shape[1]
    lat_count = lax.axis_size("lat")
    lat_index = lax.axis_index("lat")
    filtered_rows = cutoffs.shape[0]
    cut_all = jnp.pad(cutoffs, (0, rows_here * lat_count - filtered_rows))
    global_rows = lat_index * rows_here + jnp.arange(rows_here, dtype=jnp.int32)
    cut_rows = lax.dynamic_slice_in_dim(cut_all, lat_index * rows_here, rows_here, 0)
    return low_pass(state, cut_rows, global_rows < filtered_rows, table)


def tendency(state, cos_all, sinlat, lon_step, lat_step):
    lat_index = lax.axis_index("lat")
    lat_count = lax.axis_size("lat")
    edge_cols = jnp.concatenate([state[:, :, :1], state[:, :, -1:]], axis=2)
    got_cols = with_halo(edge_cols, (("lon", 2),), 1, True)
    west_col = got_cols[:, :, 0:1]
    east_col = got_cols[:, :, 3:4]
    edge_rows = jnp.concatenate([state[:, :1, :], state[:, -1:, :]], axis=1)
    got_rows = with_halo(edge_rows, (("lat", 1),), 1, False)
    flips = jnp.array([1.0, -1.0, -1.0], jnp.float32)
    mirror = from_behind(state[:, 0, :], "lon", lax.axis_size("lon") // 2) * flips[:, None]
    northmost = jnp.where(lat_index == 0, mirror, got_rows[:, 0, :])
    southmost = jnp.where(lat_index == lat_count - 1, state[:, -1, :], got_rows[:, 3, :])
    corner = jnp.zeros((3, 1, 1), jnp.float32)
    top_line = jnp.concatenate([corner, northmost[:, None, :], corner], axis=2)
    bottom_line = jnp.concatenate([corner, southmost[:, None, :], corner], axis=2)
    middle_lines = jnp.concatenate([west_col, state, east_col], axis=2)
    extended = jnp.concatenate([top_line, middle_lines, bottom_line], axis=1)
    east_side = extended[:, 1:-1, 2:]
    west_side = extended[:, 1:-1, :-2]
    north_side = extended[:, :-2, 1:-1]
    south_side = extended[:, 2:, 1:-1]
    cos_north = cos_all[:-2][:, None]
    cos_south = cos_all[2:][:, None]
    coslat = cos_all[1:-1][:, None]

    def zonal_pair(east_value, west_value):
        return (east_value - west_value) * (0.5 / lon_step)

    def north_pair(north_value, south_value):
        return (north_value - south_value) * (0.5 / lat_step)

    height, east, north = (state[0], state[1], state[2])
    inv_cos = 1.0 / coslat
    turning = 2.0 * OMEGA_RATE * sinlat + east * sinlat * inv_cos
    flux_north = north_side[0] * north_side[2] * cos_north
    flux_south = south_side[0] * south_side[2] * cos_south
    rate_height = (
        -(
            zonal_pair(east_side[0] * east_side[1], west_side[0] * west_side[1])
            + north_pair(flux_north, flux_south)
        )
        * inv_cos
    )
    rate_east = (
        -east * zonal_pair(east_side[1], west_side[1]) * inv_cos
        - north * north_pair(north_side[1], south_side[1])
        + turning * north
        - zonal_pair(east_side[0], west_side[0]) * inv_cos
    )
    rate_north = (
        -east * zonal_pair(east_side[2], west_side[2]) * inv_cos
        - north * north_pair(north_side[2], south_side[2])
        - turning * east
        - north_pair(north_side[0], south_side[0])
    )
    return jnp.stack([rate_height, rate_east, rate_north], axis=0)


def shards(height, east_wind, north_wind, cutoffs):
    rows_here = height.shape[0]
    lat_index = lax.axis_index("lat")
    lat_step = math.pi / LAT_ROWS
    lon_step = 2.0 * math.pi / NLON
    time_step = COURANT * lat_step
    first_row = (lat_index * rows_here).astype(jnp.float32)
    index = first_row + jnp.arange(-1, rows_here + 1).astype(jnp.float32)
    cos_all = jnp.abs(jnp.sin((index + 0.5) * lat_step))
    sin_all = jnp.cos((index + 0.5) * lat_step)
    sinlat = sin_all[1:-1][:, None]
    table = local_table(height.shape[1])
    state = jnp.stack([height, east_wind, north_wind], axis=0)
    for step_index in range(STEPS):
        rates = tendency(state, cos_all, sinlat, lon_step, lat_step)
        middle = state + 0.5 * time_step * rates
        rates = tendency(middle, cos_all, sinlat, lon_step, lat_step)
        advanced = state + time_step * rates
        state = filter_state(advanced, cutoffs, table)
    return (state[0], state[1], state[2])


def solution(mesh):
    placed = (P("lat", "lon"), P("lat", "lon"), P("lat", "lon"), P())
    return jax.shard_map(
        shards,
        mesh=mesh,
        in_specs=placed,
        out_specs=(P("lat", "lon"), P("lat", "lon"), P("lat", "lon")),
        check_vma=False,
    )
```

profile of v0, /device:TPU:17, one launch (start us, length us, event | category | flops | bytes accessed | tf_op | source)
XLA Modules:
  0.0 349.9 jit_solution(10091914671788850582)
XLA Ops:
  7.2 1.3 pad_maximum_fusion
  8.6 0.8 fusion.111
  9.4 0.7 collective-permute-start
  10.0 1.1 collective-permute-start.1
  11.7 7.4 %collective-permute-start.4 = (f32[3,1,450]{2,1,0:T(1,128)}, f32[3,1,450]{2,1,0:T(1,128)}, u32[]{:S(2)}, u32[]{:S(2)}) collective-permute-start(f32[3,1,450]{2,1,0:T(1,128)} %get-tuple-element.26), channel_id=1, source_target_pairs={{1,0},{2,1},{3,2},{4,3},{5,4},{6,5},{7,6},{8,7},{9,8},{10,9},{11,1... | collective-permute-start | bytes 16208 | tf_op jit(solution)/shard_map/ppermute | solution.py:26
  19.1 1.3 copy.94
  20.4 2.8 collective-permute-start.2
  23.7 1.9 collective-permute-start.3
  25.7 0.7 broadcast_multiply_fusion
  27.1 0.7 pad_dynamic-slice_fusion
  28.8 3.2 collective-permute-done.3
  32.1 0.8 fusion.96
  33.0 0.7 broadcast_select_fusion
  35.5 3.8 %collective-permute-start.9 = (f32[3,1,450]{2,0,1:T(4,128)S(1)}, f32[3,1,450]{2,0,1:T(4,128)S(1)}, u32[]{:S(2)}, u32[]{:S(2)}) collective-permute-start(f32[3,1,450]{2,0,1:T(4,128)S(1)} %copy.97), channel_id=1, source_target_pairs={{1,0},{2,1},{3,2},{4,3},{5,4},{6,5},{7,6},{8,7},{9,8},{10,9},{11,1... | collective-permute-start | bytes 16208 | tf_op jit(solution)/shard_map/ppermute | solution.py:26
  40.2 1.9 collective-permute-start.8
  42.2 3.7 %collective-permute-start.5 = (f32[3,192,1]{2,1,0:T(8,128)S(1)}, f32[3,192,1]{2,1,0:T(8,128)S(1)}, u32[]{:S(2)}, u32[]{:S(2)}) collective-permute-start(f32[3,192,1]{2,1,0:T(8,128)S(1)} %get-tuple-element.23), channel_id=1, source_target_pairs={{16,0},{32,16},{48,32},{64,48},{80,64},{96,80},{112,96},{128,112},... | collective-permute-start | bytes 6920 | tf_op jit(solution)/shard_map/ppermute | solution.py:26
  46.1 2.3 collective-permute-done.8
  48.6 2.2 collective-permute-done.5
  50.8 2.2 collective-permute-done.6
  53.0 0.8 fusion.77
  53.8 0.8 fusion.56
  54.6 1.5 fusion.50
  56.0 3.2 fusion.89
  59.6 116.2 %all-reduce.4.cloned.1.call-done = f32[3,192,130]{1,2,0:T(8,128)} async-done(((f32[3,192,130]{1,2,0:T(8,128)}), f32[3,192,130]{1,2,0:T(8,128)}) %all-reduce.4.cloned.1.call-update) | async-done | bytes 299536 | tf_op jit(solution)/shard_map/psum | solution.py:61
  175.9 2.7 convolution_select_fusion.1
  178.6 4.9 %collective-permute-start.14 = (f32[3,1,450]{2,0,1:T(4,128)S(1)}, f32[3,1,450]{2,0,1:T(4,128)S(1)}, u32[]{:S(2)}, u32[]{:S(2)}) collective-permute-start(f32[3,1,450]{2,0,1:T(4,128)S(1)} %copy.96), channel_id=1, source_target_pairs={{1,0},{2,1},{3,2},{4,3},{5,4},{6,5},{7,6},{8,7},{9,8},{10,9},{11,1... | collective-permute-start | bytes 16208 | tf_op jit(solution)/shard_map/ppermute | solution.py:26
  183.6 0.7 collective-permute-done.14
  184.3 1.9 collective-permute-start.13
  186.4 3.5 %collective-permute-start.10 = (f32[3,192,1]{2,1,0:T(8,128)S(1)}, f32[3,192,1]{2,1,0:T(8,128)S(1)}, u32[]{:S(2)}, u32[]{:S(2)}) collective-permute-start(f32[3,192,1]{2,1,0:T(8,128)S(1)} %get-tuple-element.19), channel_id=1, source_target_pairs={{16,0},{32,16},{48,32},{64,48},{80,64},{96,80},{112,96},{128,112},... | collective-permute-start | bytes 6920 | tf_op jit(solution)/shard_map/ppermute | solution.py:26
  189.9 2.7 collective-permute-done.13
  193.3 2.3 collective-permute-done.11
  195.6 0.8 fusion.76
  196.5 0.8 fusion.43
  197.2 0.7 fusion.37
  198.2 6.4 %collective-permute-start.19 = (f32[3,1,450]{2,0,1:T(4,128)S(1)}, f32[3,1,450]{2,0,1:T(4,128)S(1)}, u32[]{:S(2)}, u32[]{:S(2)}) collective-permute-start(f32[3,1,450]{2,0,1:T(4,128)S(1)} %copy.95), channel_id=1, source_target_pairs={{1,0},{2,1},{3,2},{4,3},{5,4},{6,5},{7,6},{8,7},{9,8},{10,9},{11,1... | collective-permute-start | bytes 16208 | tf_op jit(solution)/shard_map/ppermute | solution.py:26
  204.6 1.6 collective-permute-start.17
  206.2 1.9 collective-permute-start.18
  208.3 3.4 collective-permute-start.15
  211.6 0.7 collective-permute-start.16
  212.3 2.0 collective-permute-done.18
  214.5 2.2 collective-permute-done.15
  216.7 0.8 fusion.75
  217.6 0.8 fusion.30
  218.3 0.7 fusion.24
  219.0 2.2 fusion.88
  221.3 118.3 %all-reduce.6.cloned.1.call-done = f32[3,192,130]{1,2,0:T(8,128)} async-done(((f32[3,192,130]{1,2,0:T(8,128)}), f32[3,192,130]{1,2,0:T(8,128)}) %all-reduce.6.cloned.1.call-update) | async-done | bytes 299536 | tf_op jit(solution)/shard_map/psum | solution.py:61
  339.6 2.5 convolution_select_fusion
  342.0 1.0 slice_bitcast_fusion
  (87 shorter events, 8.0 us)
Async XLA Ops:
  7.2 168.7 %all-reduce.4.cloned.1.call-start = ((), (), s32[]{:S(2)}) async-start(), calls=%async_computation | async-start | bytes 835584 | tf_op jit(solution)/shard_map/psum | solution.py:61
  8.5 19.8 %copy-start = (f32[192,450]{1,0:T(8,128)S(1)}, f32[192,450]{1,0:T(8,128)}, u32[]{:S(2)}) copy-start(f32[192,450]{1,0:T(8,128)} %param.10) | copy-start | bytes 1036804
  8.6 19.8 %copy-start.1 = (f32[192,450]{1,0:T(8,128)S(1)}, f32[192,450]{1,0:T(8,128)}, u32[]{:S(2)}) copy-start(f32[192,450]{1,0:T(8,128)} %param.9) | copy-start | bytes 1036804
  8.6 19.8 %copy-start.2 = (f32[192,450]{1,0:T(8,128)S(1)}, f32[192,450]{1,0:T(8,128)}, u32[]{:S(2)}) copy-start(f32[192,450]{1,0:T(8,128)} %param.8) | copy-start | bytes 1036804
  9.4 18.9 %collective-permute-start = (f32[3,192,1]{2,1,0:T(8,128)}, f32[3,192,1]{2,1,0:T(8,128)S(1)}, u32[]{:S(2)}, u32[]{:S(2)}) collective-permute-start(f32[3,192,1]{2,1,0:T(8,128)} %get-tuple-element.29), channel_id=1, source_target_pairs={{16,0},{32,16},{48,32},{64,48},{80,64},{96,80},{112,96},{128,112},... | collective-permute-start | bytes 6920 | tf_op jit(solution)/shard_map/ppermute | solution.py:26
  10.0 18.2 %collective-permute-start.1 = (f32[3,192,1]{2,1,0:T(8,128)S(1)}, f32[3,192,1]{2,1,0:T(8,128)S(1)}, u32[]{:S(2)}, u32[]{:S(2)}) collective-permute-start(f32[3,192,1]{2,1,0:T(8,128)S(1)} %get-tuple-element.30), channel_id=1, source_target_pairs={{0,16},{16,32},{32,48},{48,64},{64,80},{80,96},{96,112},{112,128},... | collective-permute-start | bytes 6920 | tf_op jit(solution)/shard_map/ppermute | solution.py:25
  11.7 21.2 %collective-permute-start.4 = (f32[3,1,450]{2,1,0:T(1,128)}, f32[3,1,450]{2,1,0:T(1,128)}, u32[]{:S(2)}, u32[]{:S(2)}) collective-permute-start(f32[3,1,450]{2,1,0:T(1,128)} %get-tuple-element.26), channel_id=1, source_target_pairs={{1,0},{2,1},{3,2},{4,3},{5,4},{6,5},{7,6},{8,7},{9,8},{10,9},{11,1... | collective-permute-start | bytes 16208 | tf_op jit(solution)/shard_map/ppermute | solution.py:26
  20.4 8.4 %collective-permute-start.2 = (f32[3,450]{1,0:T(4,128)}, f32[3,450]{1,0:T(4,128)}, u32[]{:S(2)}, u32[]{:S(2)}) collective-permute-start(f32[3,450]{1,0:T(4,128)} %bitcast.93), channel_id=1, source_target_pairs={{0,128},{16,144},{32,160},{48,176},{64,192},{80,208},{96,224},{112... | collective-permute-start | bytes 16208 | tf_op jit(solution)/shard_map/ppermute | solution.py:33
  23.7 8.3 %collective-permute-start.3 = (f32[3,1,450]{2,0,1:T(4,128)}, f32[3,1,450]{2,0,1:T(4,128)}, u32[]{:S(2)}, u32[]{:S(2)}) collective-permute-start(f32[3,1,450]{2,0,1:T(4,128)} %copy.74), channel_id=1, source_target_pairs={{0,1},{1,2},{2,3},{3,4},{4,5},{5,6},{6,7},{7,8},{8,9},{9,10},{10,1... | collective-permute-start | bytes 16208 | tf_op jit(solution)/shard_map/ppermute | solution.py:25
  28.3 3.8 %copy-start.8 = (f32[3]{0:T(128)S(1)}, f32[3]{0:T(128)}, u32[]{:S(2)}) copy-start(f32[3]{0:T(128)} %constant.57.clone) | copy-start | bytes 40
  28.3 5.4 %copy-start.4 = (f32[192]{0:T(256)S(1)}, f32[192]{0:T(256)}, u32[]{:S(2)}) copy-start(f32[192]{0:T(256)} %get-tuple-element.53) | copy-start | bytes 2308
  28.3 5.4 %copy-start.6 = (f32[192]{0:T(256)S(1)}, f32[192]{0:T(256)}, u32[]{:S(2)}) copy-start(f32[192]{0:T(256)} %get-tuple-element.54) | copy-start | bytes 2308
  35.5 4.6 %collective-permute-start.9 = (f32[3,1,450]{2,0,1:T(4,128)S(1)}, f32[3,1,450]{2,0,1:T(4,128)S(1)}, u32[]{:S(2)}, u32[]{:S(2)}) collective-permute-start(f32[3,1,450]{2,0,1:T(4,128)S(1)} %copy.97), channel_id=1, source_target_pairs={{1,0},{2,1},{3,2},{4,3},{5,4},{6,5},{7,6},{8,7},{9,8},{10,9},{11,1... | collective-permute-start | bytes 16208 | tf_op jit(solution)/shard_map/ppermute | solution.py:26
  39.4 6.7 %collective-permute-start.7 = (f32[3,450]{1,0:T(4,128)S(1)}, f32[3,450]{1,0:T(4,128)S(1)}, u32[]{:S(2)}, u32[]{:S(2)}) collective-permute-start(f32[3,450]{1,0:T(4,128)S(1)} %bitcast.115), channel_id=1, source_target_pairs={{0,128},{16,144},{32,160},{48,176},{64,192},{80,208},{96,224},{112... | collective-permute-start | bytes 16208 | tf_op jit(solution)/shard_map/ppermute | solution.py:33
  40.2 8.3 %collective-permute-start.8 = (f32[3,1,450]{2,0,1:T(4,128)S(1)}, f32[3,1,450]{2,0,1:T(4,128)S(1)}, u32[]{:S(2)}, u32[]{:S(2)}) collective-permute-start(f32[3,1,450]{2,0,1:T(4,128)S(1)} %get-tuple-element.40), channel_id=1, source_target_pairs={{0,1},{1,2},{2,3},{3,4},{4,5},{5,6},{6,7},{7,8},{8,9},{9,10},{10,1... | collective-permute-start | bytes 16208 | tf_op jit(solution)/shard_map/ppermute | solution.py:25
  42.2 8.5 %collective-permute-start.5 = (f32[3,192,1]{2,1,0:T(8,128)S(1)}, f32[3,192,1]{2,1,0:T(8,128)S(1)}, u32[]{:S(2)}, u32[]{:S(2)}) collective-permute-start(f32[3,192,1]{2,1,0:T(8,128)S(1)} %get-tuple-element.23), channel_id=1, source_target_pairs={{16,0},{32,16},{48,32},{64,48},{80,64},{96,80},{112,96},{128,112},... | collective-permute-start | bytes 6920 | tf_op jit(solution)/shard_map/ppermute | solution.py:26
  46.0 7.0 %collective-permute-start.6 = (f32[3,192,1]{2,1,0:T(8,128)S(1)}, f32[3,192,1]{2,1,0:T(8,128)S(1)}, u32[]{:S(2)}, u32[]{:S(2)}) collective-permute-start(f32[3,192,1]{2,1,0:T(8,128)S(1)} %get-tuple-element.24), channel_id=1, source_target_pairs={{0,16},{16,32},{32,48},{48,64},{64,80},{80,96},{96,112},{112,128},... | collective-permute-start | bytes 6920 | tf_op jit(solution)/shard_map/ppermute | solution.py:25
  54.6 1.5 copy-start.3
  56.0 3.4 copy-start.10
  56.0 3.5 copy-start.11
  59.3 280.3 %all-reduce.6.cloned.1.call-start = ((), (), s32[]{:S(2)}) async-start(), calls=%async_computation.1 | async-start | bytes 835584 | tf_op jit(solution)/shard_map/psum | solution.py:61
  178.6 14.1 %copy-start.9 = (f32[3]{0:T(128)S(1)}, f32[3]{0:T(128)}, u32[]{:S(2)}) copy-start(f32[3]{0:T(128)} %constant.57.clone) | copy-start | bytes 40
  178.6 17.0 %copy-start.5 = (f32[192]{0:T(256)S(1)}, f32[192]{0:T(256)}, u32[]{:S(2)}) copy-start(f32[192]{0:T(256)} %get-tuple-element.53) | copy-start | bytes 2308
  178.6 17.0 %copy-start.7 = (f32[192]{0:T(256)S(1)}, f32[192]{0:T(256)}, u32[]{:S(2)}) copy-start(f32[192]{0:T(256)} %get-tuple-element.54) | copy-start | bytes 2308
  178.6 5.7 %collective-permute-start.14 = (f32[3,1,450]{2,0,1:T(4,128)S(1)}, f32[3,1,450]{2,0,1:T(4,128)S(1)}, u32[]{:S(2)}, u32[]{:S(2)}) collective-permute-start(f32[3,1,450]{2,0,1:T(4,128)S(1)} %copy.96), channel_id=1, source_target_pairs={{1,0},{2,1},{3,2},{4,3},{5,4},{6,5},{7,6},{8,7},{9,8},{10,9},{11,1... | collective-permute-start | bytes 16208 | tf_op jit(solution)/shard_map/ppermute | solution.py:26
  183.5 6.4 %collective-permute-start.12 = (f32[3,450]{1,0:T(4,128)S(1)}, f32[3,450]{1,0:T(4,128)S(1)}, u32[]{:S(2)}, u32[]{:S(2)}) collective-permute-start(f32[3,450]{1,0:T(4,128)S(1)} %bitcast.117), channel_id=1, source_target_pairs={{0,128},{16,144},{32,160},{48,176},{64,192},{80,208},{96,224},{112... | collective-permute-start | bytes 16208 | tf_op jit(solution)/shard_map/ppermute | solution.py:33
  184.3 8.4 %collective-permute-start.13 = (f32[3,1,450]{2,0,1:T(4,128)S(1)}, f32[3,1,450]{2,0,1:T(4,128)S(1)}, u32[]{:S(2)}, u32[]{:S(2)}) collective-permute-start(f32[3,1,450]{2,0,1:T(4,128)S(1)} %get-tuple-element.36), channel_id=1, source_target_pairs={{0,1},{1,2},{2,3},{3,4},{4,5},{5,6},{6,7},{7,8},{8,9},{9,10},{10,1... | collective-permute-start | bytes 16208 | tf_op jit(solution)/shard_map/ppermute | solution.py:25
  186.4 6.9 %collective-permute-start.10 = (f32[3,192,1]{2,1,0:T(8,128)S(1)}, f32[3,192,1]{2,1,0:T(8,128)S(1)}, u32[]{:S(2)}, u32[]{:S(2)}) collective-permute-start(f32[3,192,1]{2,1,0:T(8,128)S(1)} %get-tuple-element.19), channel_id=1, source_target_pairs={{16,0},{32,16},{48,32},{64,48},{80,64},{96,80},{112,96},{128,112},... | collective-permute-start | bytes 6920 | tf_op jit(solution)/shard_map/ppermute | solution.py:26
  189.9 5.7 %collective-permute-start.11 = (f32[3,192,1]{2,1,0:T(8,128)S(1)}, f32[3,192,1]{2,1,0:T(8,128)S(1)}, u32[]{:S(2)}, u32[]{:S(2)}) collective-permute-start(f32[3,192,1]{2,1,0:T(8,128)S(1)} %get-tuple-element.20), channel_id=1, source_target_pairs={{0,16},{16,32},{32,48},{48,64},{64,80},{80,96},{96,112},{112,128},... | collective-permute-start | bytes 6920 | tf_op jit(solution)/shard_map/ppermute | solution.py:25
  198.2 8.0 %collective-permute-start.19 = (f32[3,1,450]{2,0,1:T(4,128)S(1)}, f32[3,1,450]{2,0,1:T(4,128)S(1)}, u32[]{:S(2)}, u32[]{:S(2)}) collective-permute-start(f32[3,1,450]{2,0,1:T(4,128)S(1)} %copy.95), channel_id=1, source_target_pairs={{1,0},{2,1},{3,2},{4,3},{5,4},{6,5},{7,6},{8,7},{9,8},{10,9},{11,1... | collective-permute-start | bytes 16208 | tf_op jit(solution)/shard_map/ppermute | solution.py:26
  204.6 7.7 %collective-permute-start.17 = (f32[3,450]{1,0:T(4,128)S(1)}, f32[3,450]{1,0:T(4,128)S(1)}, u32[]{:S(2)}, u32[]{:S(2)}) collective-permute-start(f32[3,450]{1,0:T(4,128)S(1)} %bitcast.116), channel_id=1, source_target_pairs={{0,128},{16,144},{32,160},{48,176},{64,192},{80,208},{96,224},{112... | collective-permute-start | bytes 16208 | tf_op jit(solution)/shard_map/ppermute | solution.py:33
  206.2 8.1 %collective-permute-start.18 = (f32[3,1,450]{2,0,1:T(4,128)S(1)}, f32[3,1,450]{2,0,1:T(4,128)S(1)}, u32[]{:S(2)}, u32[]{:S(2)}) collective-permute-start(f32[3,1,450]{2,0,1:T(4,128)S(1)} %get-tuple-element.32), channel_id=1, source_target_pairs={{0,1},{1,2},{2,3},{3,4},{4,5},{5,6},{6,7},{7,8},{8,9},{9,10},{10,1... | collective-permute-start | bytes 16208 | tf_op jit(solution)/shard_map/ppermute | solution.py:25
  208.3 8.4 %collective-permute-start.15 = (f32[3,192,1]{2,1,0:T(8,128)S(1)}, f32[3,192,1]{2,1,0:T(8,128)S(1)}, u32[]{:S(2)}, u32[]{:S(2)}) collective-permute-start(f32[3,192,1]{2,1,0:T(8,128)S(1)} %get-tuple-element.15), channel_id=1, source_target_pairs={{16,0},{32,16},{48,32},{64,48},{80,64},{96,80},{112,96},{128,112},... | collective-permute-start | bytes 6920 | tf_op jit(solution)/shard_map/ppermute | solution.py:26
  211.6 5.1 %collective-permute-start.16 = (f32[3,192,1]{2,1,0:T(8,128)S(1)}, f32[3,192,1]{2,1,0:T(8,128)S(1)}, u32[]{:S(2)}, u32[]{:S(2)}) collective-permute-start(f32[3,192,1]{2,1,0:T(8,128)S(1)} %get-tuple-element.16), channel_id=1, source_target_pairs={{0,16},{16,32},{32,48},{48,64},{64,80},{80,96},{96,112},{112,128},... | collective-permute-start | bytes 6920 | tf_op jit(solution)/shard_map/ppermute | solution.py:25
Sparse Core Ops, SparseCore 0:
  59.4 116.4 all-reduce.3
  221.4 118.1 all-reduce.5
where the time goes:
time: 352 us; the launch traced here: 350 us
  waiting for transfers between devices  255 us (72%)
  starting transfers between devices  48.3 us (14%)
  other arithmetic  15.6 us (4%)
  between operations  14.5 us (4%)
  matrix products  10.6 us (3%)
  local copies, waits for them, and re-layouts  5.62 us (2%)
    psum x2, waiting for transfers between devices, low_pass(): coeffs = lax.psum(project(fields, table), 'lon') * weights[None]  235 us
    ppermute x8, starting transfers between devices, with_halo(): after = lax.ppermute(first, axis, down)  33.8 us
    ppermute x8, waiting for transfers between devices, with_halo(): before = lax.ppermute(last, axis, up)  14.8 us
    ppermute x8, starting transfers between devices, with_halo(): before = lax.ppermute(last, axis, up)  9.56 us
  transfers between devices with their start and end apart: 22, of which 13 were waited for; matrix products, arithmetic and copies ran while one was open for 2% of the time, Pallas kernels for 0%

commit v1 on v0

--- a/solution.py
+++ b/solution.py
@@ -33,9 +33,10 @@
     return lax.ppermute(value, axis, [(i, (i + by) % devices) for i in range(devices)])
 
 
-def local_table(width):
+def local_table(first, width):
     waves = jnp.arange(KMAX + 1, dtype=jnp.int32)
-    columns = lax.axis_index("lon") * width + jnp.arange(width, dtype=jnp.int32)
+    columns = (lax.axis_index("lon") * NLON // lax.axis_size("lon") + first) % NLON
+    columns = (columns + jnp.arange(width, dtype=jnp.int32)) % NLON
     phase = waves[:, None] * columns[None, :] % NLON
     angle = phase.astype(jnp.float32) * (2.0 * math.pi / NLON)
     return jnp.concatenate([jnp.cos(angle), jnp.sin(angle)], axis=0)
@@ -48,6 +49,12 @@
     return jnp.concatenate([keep, keep], axis=1)
 
 
+def half_turn_signs():
+    waves = jnp.arange(KMAX + 1, dtype=jnp.int32)
+    signs = jnp.where(waves % 2 == 0, 1.0, -1.0).astype(jnp.float32)
+    return jnp.concatenate([signs, signs], axis=0)
+
+
 def project(fields, table):
     return jnp.einsum("fnw,kw->fnk", fields, table, precision=lax.Precision.HIGHEST)
 
@@ -56,14 +63,46 @@
     return jnp.einsum("fnk,kw->fnw", coeffs, table, precision=lax.Precision.HIGHEST)
 
 
-def low_pass(fields, cut_rows, active, table):
+def low_pass(fields, cut_rows, active, table, wide_table, with_halos):
+    devices = lax.axis_size("lon")
+    lon_index = lax.axis_index("lon")
+    count, rows, width = fields.shape
+    share = rows // devices
+    partial = project(fields, table)
+    modes = partial.shape[2]
+    gathered = lax.all_to_all(partial, "lon", split_axis=1, concat_axis=0, tiled=True)
+    reduced = gathered.reshape(devices, count, share, modes).sum(axis=0)
+    payload = [jnp.broadcast_to(reduced.reshape(1, -1), (devices, count * share * modes))]
+    if with_halos:
+        targets = jnp.arange(devices, dtype=jnp.int32)[:, None]
+        to_east = targets == (lon_index + 1) % devices
+        edge = jnp.where(to_east, fields[:, :, -1].reshape(1, -1), fields[:, :, 0].reshape(1, -1))
+        payload += [edge, jnp.broadcast_to(fields[:, 0, :].reshape(1, -1), (devices, count * width))]
+    spread = lax.all_to_all(jnp.concatenate(payload, axis=1), "lon", split_axis=0, concat_axis=0, tiled=True)
+    block = count * share * modes
+    coeffs = spread[:, :block].reshape(devices, count, share, modes)
+    coeffs = jnp.moveaxis(coeffs, 0, 1).reshape(count, rows, modes)
     weights = spectral_weights(cut_rows)
-    coeffs = lax.psum(project(fields, table), "lon") * weights[None]
-    smooth = expand(coeffs, table)
-    return jnp.where(active[None, :, None], smooth, fields)
-
-
-def filter_state(state, cutoffs, table):
+    scaled = coeffs * weights[None]
+    if not with_halos:
+        smooth = expand(scaled, table)
+        return jnp.where(active[None, :, None], smooth, fields), None
+    wide = expand(scaled, wide_table)
+    smooth = wide[:, :, 1:-1]
+    filtered = jnp.where(active[None, :, None], smooth, fields)
+    edges = spread[:, block:block + count * rows].reshape(devices, count, rows)
+    rows_far = spread[:, block + count * rows:].reshape(devices, count, width)
+    west_raw = edges[(lon_index - 1) % devices]
+    east_raw = edges[(lon_index + 1) % devices]
+    far_raw = rows_far[(lon_index + devices // 2) % devices]
+    west = jnp.where(active[None, :], wide[:, :, 0], west_raw)[:, :, None]
+    east = jnp.where(active[None, :], wide[:, :, -1], east_raw)[:, :, None]
+    far_smooth = expand(scaled[:, :1, :] * half_turn_signs()[None, None, :], table)[:, 0, :]
+    far = jnp.where(active[0], far_smooth, far_raw)
+    return filtered, (west, east, far)
+
+
+def filter_state(state, cutoffs, table, wide_table, with_halos):
     rows_here = state.shape[1]
     lat_count = lax.axis_size("lat")
     lat_index = lax.axis_index("lat")
@@ -71,20 +110,24 @@
     cut_all = jnp.pad(cutoffs, (0, rows_here * lat_count - filtered_rows))
     global_rows = lat_index * rows_here + jnp.arange(rows_here, dtype=jnp.int32)
     cut_rows = lax.dynamic_slice_in_dim(cut_all, lat_index * rows_here, rows_here, 0)
-    return low_pass(state, cut_rows, global_rows < filtered_rows, table)
-
-
-def tendency(state, cos_all, sinlat, lon_step, lat_step):
+    return low_pass(state, cut_rows, global_rows < filtered_rows, table, wide_table, with_halos)
+
+
+def tendency(state, cos_all, sinlat, lon_step, lat_step, lon_halos=None):
     lat_index = lax.axis_index("lat")
     lat_count = lax.axis_size("lat")
-    edge_cols = jnp.concatenate([state[:, :, :1], state[:, :, -1:]], axis=2)
-    got_cols = with_halo(edge_cols, (("lon", 2),), 1, True)
-    west_col = got_cols[:, :, 0:1]
-    east_col = got_cols[:, :, 3:4]
+    flips = jnp.array([1.0, -1.0, -1.0], jnp.float32)
+    if lon_halos is None:
+        edge_cols = jnp.concatenate([state[:, :, :1], state[:, :, -1:]], axis=2)
+        got_cols = with_halo(edge_cols, (("lon", 2),), 1, True)
+        west_col = got_cols[:, :, 0:1]
+        east_col = got_cols[:, :, 3:4]
+        mirror = from_behind(state[:, 0, :], "lon", lax.axis_size("lon") // 2)
+    else:
+        west_col, east_col, mirror = lon_halos
+    mirror = mirror * flips[:, None]
     edge_rows = jnp.concatenate([state[:, :1, :], state[:, -1:, :]], axis=1)
     got_rows = with_halo(edge_rows, (("lat", 1),), 1, False)
-    flips = jnp.array([1.0, -1.0, -1.0], jnp.float32)
-    mirror = from_behind(state[:, 0, :], "lon", lax.axis_size("lon") // 2) * flips[:, None]
     northmost = jnp.where(lat_index == 0, mirror, got_rows[:, 0, :])
     southmost = jnp.where(lat_index == lat_count - 1, state[:, -1, :], got_rows[:, 3, :])
     corner = jnp.zeros((3, 1, 1), jnp.float32)
@@ -144,14 +187,18 @@
     cos_all = jnp.abs(jnp.sin((index + 0.5) * lat_step))
     sin_all = jnp.cos((index + 0.5) * lat_step)
     sinlat = sin_all[1:-1][:, None]
-    table = local_table(height.shape[1])
+    width = height.shape[1]
+    table = local_table(0, width)
+    wide_table = local_table(-1, width + 2)
     state = jnp.stack([height, east_wind, north_wind], axis=0)
+    lon_halos = None
     for step_index in range(STEPS):
-        rates = tendency(state, cos_all, sinlat, lon_step, lat_step)
+        rates = tendency(state, cos_all, sinlat, lon_step, lat_step, lon_halos)
         middle = state + 0.5 * time_step * rates
         rates = tendency(middle, cos_all, sinlat, lon_step, lat_step)
         advanced = state + time_step * rates
-        state = filter_state(advanced, cutoffs, table)
+        last = step_index == STEPS - 1
+        state, lon_halos = filter_state(advanced, cutoffs, table, wide_table, not last)
     return (state[0], state[1], state[2])
 
 

time: 352 us -> 169 us (0.48)
  waiting for transfers between devices: 255 us -> 36.7 us
  blocking collectives: 0 us -> 22.7 us
  local copies, waits for them, and re-layouts: 5.62 us -> 23.9 us
  between operations: 14.5 us -> 1.66 us
  other arithmetic: 15.6 us -> 22.5 us
  starting transfers between devices: 48.3 us -> 53.3 us
  matrix products: 10.6 us -> 6.88 us
    psum x2 -> x0, waiting for transfers between devices: 235 us -> none  [low_pass(): coeffs = lax.psum(project(fields, table), 'lon') * weights[None]]
    all_to_all x0 -> x2, blocking collectives: none -> 22.7 us  [the longest x1 12 us: low_pass(): lax.all_to_all(partial, 'lon', split_axis=1, concat_axis=0, tiled=True)]
    all_to_all x0 -> x2, waiting for transfers between devices: none -> 14.4 us  [the longest x1 7.51 us: low_pass(): lax.all_to_all(partial, 'lon', split_axis=1, concat_axis=0, tiled=True)]
    all_to_all x0 -> x2, starting transfers between devices: none -> 10.2 us  [the longest x1 6.4 us: low_pass(): lax.all_to_all(partial, 'lon', split_axis=1, concat_axis=0, tiled=True)]
    unnamed x29 -> x76, local copies, waits for them, and re-layouts: 1.97 us -> 8.49 us
    ppermute x8 -> x7, starting transfers between devices: 33.8 us -> 28.2 us  [with_halo(): after = lax.ppermute(first, axis, down)]
    all_to_all x0 -> x3, other arithmetic: none -> 4.78 us  [the longest x2 3.31 us: low_pass(): lax.all_to_all(partial, 'lon', split_axis=1, concat_axis=0, tiled=True)]
    reshape x0 -> x6, local copies, waits for them, and re-layouts: none -> 4.67 us  [the longest x2 2.36 us: low_pass(): coeffs = spread[:, :block].reshape(devices, count, share, modes)]
  transfers between devices with their start and end apart: 22 -> 19, of which waited for: 13 -> 10; matrix products, arithmetic and copies ran while one was open for 2% -> 5% of each run, Pallas kernels for 0% -> 0%
where the time goes in v1:
time: 169 us; the launch traced here: 168 us
  starting transfers between devices  53.3 us (32%)
  waiting for transfers between devices  36.7 us (22%)
  local copies, waits for them, and re-layouts  23.9 us (14%)
  blocking collectives  22.7 us (13%)
  other arithmetic  22.5 us (13%)
  matrix products  6.88 us (4%)
    ppermute x7, starting transfers between devices, with_halo(): after = lax.ppermute(first, axis, down)  28.2 us
    ppermute x7, waiting for transfers between devices, with_halo(): before = lax.ppermute(last, axis, up)  13.2 us
    all_to_all x1, blocking collectives, low_pass(): lax.all_to_all(partial, 'lon', split_axis=1, concat_axis=0, tiled=True)  12 us
    all_to_all x1, blocking collectives, low_pass(): lax.all_to_all(jnp.concatenate(payload, axis=1), 'lon', split_axis=0, con...  10.7 us
    ppermute x7, starting transfers between devices, with_halo(): before = lax.ppermute(last, axis, up)  10.3 us
    ppermute x7, waiting for transfers between devices, with_halo(): after = lax.ppermute(first, axis, down)  9.1 us
    unnamed x76, local copies, waits for them, and re-layouts  8.49 us
    all_to_all x1, waiting for transfers between devices, low_pass(): lax.all_to_all(partial, 'lon', split_axis=1, concat_axis=0, tiled=True)  7.51 us
  transfers between devices with their start and end apart: 19, of which 10 were waited for; matrix products, arithmetic and copies ran while one was open for 5% of the time, Pallas kernels for 0%

profile of v1, /device:TPU:17, one launch (start us, length us, event | category | flops | bytes accessed | tf_op | source)
XLA Modules:
  0.0 167.6 jit_solution(4173457352512339414)
XLA Ops:
  0.6 1.3 pad_maximum_fusion
  3.6 1.1 collective-permute-start.1
  4.7 7.4 %collective-permute-start.4 = (f32[3,1,450]{2,1,0:T(1,128)S(1)}, f32[3,1,450]{2,1,0:T(1,128)S(1)}, u32[]{:S(2)}, u32[]{:S(2)}) collective-permute-start(f32[3,1,450]{2,1,0:T(1,128)S(1)} %get-tuple-element.28), channel_id=1, source_target_pairs={{1,0},{2,1},{3,2},{4,3},{5,4},{6,5},{7,6},{8,7},{9,8},{10,9},{11,1... | collective-permute-start | bytes 16208 | tf_op jit(solution)/shard_map/ppermute | solution.py:26
  12.1 2.8 %collective-permute-start.2 = (f32[3,450]{1,0:T(4,128)S(1)}, f32[3,450]{1,0:T(4,128)S(1)}, u32[]{:S(2)}, u32[]{:S(2)}) collective-permute-start(f32[3,450]{1,0:T(4,128)S(1)} %bitcast.145), channel_id=1, source_target_pairs={{0,128},{16,144},{32,160},{48,176},{64,192},{80,208},{96,224},{112... | collective-permute-start | bytes 16208 | tf_op jit(solution)/shard_map/ppermute | solution.py:33
  14.9 1.9 %collective-permute-start.3 = (f32[3,1,450]{2,0,1:T(4,128)S(1)}, f32[3,1,450]{2,0,1:T(4,128)S(1)}, u32[]{:S(2)}, u32[]{:S(2)}) collective-permute-start(f32[3,1,450]{2,0,1:T(4,128)S(1)} %copy.170), channel_id=1, source_target_pairs={{0,1},{1,2},{2,3},{3,4},{4,5},{5,6},{6,7},{7,8},{8,9},{9,10},{10,1... | collective-permute-start | bytes 16208 | tf_op jit(solution)/shard_map/ppermute | solution.py:25
  19.2 3.7 %collective-permute-done.3 = f32[3,1,450]{2,0,1:T(4,128)S(1)} collective-permute-done((f32[3,1,450]{2,0,1:T(4,128)S(1)}, f32[3,1,450]{2,0,1:T(4,128)S(1)}, u32[]{:S(2)}, u32[]{:S(2)}) %collective-permute-start.3) | collective-permute-done | bytes 5432 | tf_op jit(solution)/shard_map/ppermute | solution.py:25
  24.9 3.4 %collective-permute-start.9 = (f32[3,1,450]{2,0,1:T(4,128)S(1)}, f32[3,1,450]{2,0,1:T(4,128)S(1)}, u32[]{:S(2)}, u32[]{:S(2)}) collective-permute-start(f32[3,1,450]{2,0,1:T(4,128)S(1)} %copy.198), channel_id=1, source_target_pairs={{1,0},{2,1},{3,2},{4,3},{5,4},{6,5},{7,6},{8,7},{9,8},{10,9},{11,1... | collective-permute-start | bytes 16208 | tf_op jit(solution)/shard_map/ppermute | solution.py:26
  29.3 1.9 %collective-permute-start.8 = (f32[3,1,450]{2,0,1:T(4,128)S(1)}, f32[3,1,450]{2,0,1:T(4,128)S(1)}, u32[]{:S(2)}, u32[]{:S(2)}) collective-permute-start(f32[3,1,450]{2,0,1:T(4,128)S(1)} %get-tuple-element.42), channel_id=1, source_target_pairs={{0,1},{1,2},{2,3},{3,4},{4,5},{5,6},{6,7},{7,8},{8,9},{9,10},{10,1... | collective-permute-start | bytes 16208 | tf_op jit(solution)/shard_map/ppermute | solution.py:25
  31.4 4.0 %collective-permute-start.5 = (f32[3,192,1]{2,1,0:T(8,128)S(1)}, f32[3,192,1]{2,1,0:T(8,128)S(1)}, u32[]{:S(2)}, u32[]{:S(2)}) collective-permute-start(f32[3,192,1]{2,1,0:T(8,128)S(1)} %get-tuple-element.25), channel_id=1, source_target_pairs={{16,0},{32,16},{48,32},{64,48},{80,64},{96,80},{112,96},{128,112},... | collective-permute-start | bytes 6920 | tf_op jit(solution)/shard_map/ppermute | solution.py:26
  35.7 1.6 collective-permute-done.8
  37.5 2.6 %collective-permute-done.5 = f32[3,192,1]{2,1,0:T(8,128)S(1)} collective-permute-done((f32[3,192,1]{2,1,0:T(8,128)S(1)}, f32[3,192,1]{2,1,0:T(8,128)S(1)}, u32[]{:S(2)}, u32[]{:S(2)}) %collective-permute-start.5) | collective-permute-done | bytes 2336 | tf_op jit(solution)/shard_map/ppermute | solution.py:26
  40.2 2.3 %collective-permute-done.6 = f32[3,192,1]{2,1,0:T(8,128)S(1)} collective-permute-done((f32[3,192,1]{2,1,0:T(8,128)S(1)}, f32[3,192,1]{2,1,0:T(8,128)S(1)}, u32[]{:S(2)}, u32[]{:S(2)}) %collective-permute-start.6) | collective-permute-done | bytes 2336 | tf_op jit(solution)/shard_map/ppermute | solution.py:25
  46.0 2.1 %fusion.88 = f32[3,192,130]{1,2,0:T(8,128)} fusion(f32[3,192,450]{2,1,0:T(8,128)S(1)} %fusion.1, f32[65,450]{1,0:T(8,128)S(1)} %get-tuple-element.54, f32[65,450]{1,0:T(8,128)S(1)} %get-tuple-element.53), kind=kOutput, calls=%fused_computation.196 | convolution fusion | flops 404410496 | bytes 1570320 | tf_op jit(solution)/shard_map/fnw,kw->fnk/dot_general | solution.py:59
  48.1 1.4 copy.135
  49.5 1.7 %reshape.320 = f32[16,1,4680]{2,1,0:T(1,128)} reshape(f32[192,3,130]{2,1,0:T(4,128)S(1)} %bitcast.135) | data formatting | bytes 599040
  51.2 6.4 %all-to-all-start = ((f32[16,1,4680]{2,1,0:T(1,128)}), f32[16,1,4680]{2,1,0:T(1,128)S(1)}, u32[]{:S(2)}, u32[]{:S(2)}) async-start(f32[16,1,4680]{2,1,0:T(1,128)} %reshape.320), calls=%async_computation | async-start | bytes 606208 | tf_op jit(solution)/shard_map/all_to_all | solution.py:73
  57.9 7.5 %all-to-all-done = f32[16,1,4680]{2,1,0:T(1,128)S(1)} async-done(((f32[16,1,4680]{2,1,0:T(1,128)}), f32[16,1,4680]{2,1,0:T(1,128)S(1)}, u32[]{:S(2)}, u32[]{:S(2)}) %all-to-all-start) | async-done | bytes 299552 | tf_op jit(solution)/shard_map/all_to_all | solution.py:73
  65.9 1.3 reduce.11
  67.2 0.9 reshape.321
  68.6 1.1 all_to_all.32
  69.7 3.8 %all-to-all-start.1 = ((f32[16,1,6606]{2,1,0:T(1,128)}), f32[16,1,6606]{2,1,0:T(1,128)S(1)}, u32[]{:S(2)}, u32[]{:S(2)}) async-start(f32[16,1,6606]{2,1,0:T(1,128)} %all_to_all.32), calls=%async_computation.1 | async-start | bytes 851968 | tf_op jit(solution)/shard_map/all_to_all | solution.py:81
  74.2 1.3 fusion.97
  75.5 6.9 %all-to-all-done.1 = f32[16,1,6606]{2,1,0:T(1,128)S(1)} async-done(((f32[16,1,6606]{2,1,0:T(1,128)}), f32[16,1,6606]{2,1,0:T(1,128)S(1)}, u32[]{:S(2)}, u32[]{:S(2)}) %all-to-all-start.1) | async-done | bytes 422816 | tf_op jit(solution)/shard_map/all_to_all | solution.py:81
  85.7 1.1 fusion.82
  87.5 6.5 %collective-permute-start.11 = (f32[3,1,450]{2,0,1:T(4,128)S(1)}, f32[3,1,450]{2,0,1:T(4,128)S(1)}, u32[]{:S(2)}, u32[]{:S(2)}) collective-permute-start(f32[3,1,450]{2,0,1:T(4,128)S(1)} %copy.174), channel_id=1, source_target_pairs={{1,0},{2,1},{3,2},{4,3},{5,4},{6,5},{7,6},{8,7},{9,8},{10,9},{11,1... | collective-permute-start | bytes 16208 | tf_op jit(solution)/shard_map/ppermute | solution.py:26
  94.9 1.0 slice_select_fusion.2
  95.9 2.1 %collective-permute-start.10 = (f32[3,1,450]{2,0,1:T(4,128)S(1)}, f32[3,1,450]{2,0,1:T(4,128)S(1)}, u32[]{:S(2)}, u32[]{:S(2)}) collective-permute-start(f32[3,1,450]{2,0,1:T(4,128)S(1)} %get-tuple-element.40), channel_id=1, source_target_pairs={{0,1},{1,2},{2,3},{3,4},{4,5},{5,6},{6,7},{7,8},{8,9},{9,10},{10,1... | collective-permute-start | bytes 16208 | tf_op jit(solution)/shard_map/ppermute | solution.py:25
  98.8 1.0 slice.513
  99.9 4.0 %collective-permute-done.10 = f32[3,1,450]{2,0,1:T(4,128)S(1)} collective-permute-done((f32[3,1,450]{2,0,1:T(4,128)S(1)}, f32[3,1,450]{2,0,1:T(4,128)S(1)}, u32[]{:S(2)}, u32[]{:S(2)}) %collective-permute-start.10) | collective-permute-done | bytes 5432 | tf_op jit(solution)/shard_map/ppermute | solution.py:25
  106.9 3.0 %collective-permute-start.16 = (f32[3,1,450]{2,0,1:T(4,128)S(1)}, f32[3,1,450]{2,0,1:T(4,128)S(1)}, u32[]{:S(2)}, u32[]{:S(2)}) collective-permute-start(f32[3,1,450]{2,0,1:T(4,128)S(1)} %copy.197), channel_id=1, source_target_pairs={{1,0},{2,1},{3,2},{4,3},{5,4},{6,5},{7,6},{8,7},{9,8},{10,9},{11,1... | collective-permute-start | bytes 16208 | tf_op jit(solution)/shard_map/ppermute | solution.py:26
  109.9 1.4 collective-permute-start.14
  111.3 2.3 %collective-permute-start.15 = (f32[3,1,450]{2,0,1:T(4,128)S(1)}, f32[3,1,450]{2,0,1:T(4,128)S(1)}, u32[]{:S(2)}, u32[]{:S(2)}) collective-permute-start(f32[3,1,450]{2,0,1:T(4,128)S(1)} %get-tuple-element.36), channel_id=1, source_target_pairs={{0,1},{1,2},{2,3},{3,4},{4,5},{5,6},{6,7},{7,8},{8,9},{9,10},{10,1... | collective-permute-start | bytes 16208 | tf_op jit(solution)/shard_map/ppermute | solution.py:25
  113.8 3.4 %collective-permute-start.12 = (f32[3,192,1]{2,1,0:T(8,128)S(1)}, f32[3,192,1]{2,1,0:T(8,128)S(1)}, u32[]{:S(2)}, u32[]{:S(2)}) collective-permute-start(f32[3,192,1]{2,1,0:T(8,128)S(1)} %get-tuple-element.19), channel_id=1, source_target_pairs={{16,0},{32,16},{48,32},{64,48},{80,64},{96,80},{112,96},{128,112},... | collective-permute-start | bytes 6920 | tf_op jit(solution)/shard_map/ppermute | solution.py:26
  117.8 1.6 collective-permute-done.15
  119.5 5.7 %collective-permute-done.12 = f32[3,192,1]{2,1,0:T(8,128)S(1)} collective-permute-done((f32[3,192,1]{2,1,0:T(8,128)S(1)}, f32[3,192,1]{2,1,0:T(8,128)S(1)}, u32[]{:S(2)}, u32[]{:S(2)}) %collective-permute-start.12) | collective-permute-done | bytes 2336 | tf_op jit(solution)/shard_map/ppermute | solution.py:26
  127.6 2.2 %fusion.86 = f32[3,192,130]{1,2,0:T(8,128)} fusion(f32[65,450]{1,0:T(8,128)S(1)} %copy-done.6, f32[65,450]{1,0:T(8,128)S(1)} %copy-done.4, f32[3,192,450]{2,1,0:T(8,128)S(1)} %slice_select_fusion, f32[1,192,450]{2,1,0:T(8,128)S(1)} %fusion.26, f32[1,192,450]{2,1,0:T(8,128)S(1)} %fusion.32, f32[1,192,450]{2,1,0:T(8,128)S(1)} %fusion.77), kind=kOutput, calls=%fused_computation.194 | convolution fusion | flops 405447296 | bytes 2607120 | tf_op jit(solution)/shard_map/fnw,kw->fnk/dot_general | solution.py:59
  129.8 1.4 copy.157
  131.1 1.7 %reshape.322 = f32[16,1,4680]{2,1,0:T(1,128)} reshape(f32[192,3,130]{2,1,0:T(4,128)S(1)} %bitcast.137) | data formatting | bytes 599040
  132.9 12.0 %all_to_all.42 = f32[16,1,4680]{2,1,0:T(1,128)S(1)} all-to-all(f32[16,1,4680]{2,1,0:T(1,128)} %reshape.322), channel_id=1, replica_groups=mesh['lon'=16,'lat'=16] {'lon'}, dimensions={0} | all-to-all | bytes 599040 | tf_op jit(solution)/shard_map/all_to_all | solution.py:73
  144.9 2.0 %reduce.12 = f32[16,4680]{1,0:T(8,128)} reduce(f32[16,1,4680]{2,1,0:T(1,128)S(1)} %all_to_all.42, f32[]{:T(128)} %broadcast.357), dimensions={1}, to_apply=%all_to_all.35.reduce_sub_computation | reduce | bytes 599044 | tf_op jit(solution)/shard_map/all_to_all | solution.py:73
  146.9 1.9 %reshape.323 = f32[192,3,130]{2,1,0:T(4,128)S(1)} reshape(f32[16,4680]{1,0:T(8,128)} %reduce.12) | data formatting | bytes 599040
  149.3 10.7 %all_to_all.43 = f32[16,1,4680]{2,1,0:T(1,128)S(1)} all-to-all(f32[16,1,4680]{2,1,0:T(1,128)S(1)} %broadcast_in_dim.157), channel_id=1, replica_groups=mesh['lon'=16,'lat'=16] {'lon'}, dimensions={0} | all-to-all | bytes 599040 | tf_op jit(solution)/shard_map/all_to_all | solution.py:81
  160.0 1.5 reduce.7
  161.5 1.7 reshape.312
  163.1 1.0 copy.159
  164.1 1.2 reshape.313
  165.3 1.2 convolution_select_fusion
  166.6 1.0 slice_bitcast_fusion
  (169 shorter events, 25.1 us)
Async XLA Ops:
  2.0 15.8 %copy-start.30 = (s32[512]{0:T(512)S(1)}, s32[512]{0:T(512)}, u32[]{:S(2)}) copy-start(s32[512]{0:T(512)} %param.11) | copy-start | bytes 6148
  2.0 16.7 %copy-start = (f32[192,450]{1,0:T(8,128)S(1)}, f32[192,450]{1,0:T(8,128)}, u32[]{:S(2)}) copy-start(f32[192,450]{1,0:T(8,128)} %param.10) | copy-start | bytes 1036804
  2.0 16.7 %copy-start.1 = (f32[192,450]{1,0:T(8,128)S(1)}, f32[192,450]{1,0:T(8,128)}, u32[]{:S(2)}) copy-start(f32[192,450]{1,0:T(8,128)} %param.9) | copy-start | bytes 1036804
  2.0 16.7 %copy-start.2 = (f32[192,450]{1,0:T(8,128)S(1)}, f32[192,450]{1,0:T(8,128)}, u32[]{:S(2)}) copy-start(f32[192,450]{1,0:T(8,128)} %param.8) | copy-start | bytes 1036804
  2.9 15.7 %collective-permute-start = (f32[3,192,1]{2,1,0:T(8,128)}, f32[3,192,1]{2,1,0:T(8,128)S(1)}, u32[]{:S(2)}, u32[]{:S(2)}) collective-permute-start(f32[3,192,1]{2,1,0:T(8,128)} %get-tuple-element.31), channel_id=1, source_target_pairs={{16,0},{32,16},{48,32},{64,48},{80,64},{96,80},{112,96},{128,112},... | collective-permute-start | bytes 6920 | tf_op jit(solution)/shard_map/ppermute | solution.py:26
  3.6 15.1 %collective-permute-start.1 = (f32[3,192,1]{2,1,0:T(8,128)}, f32[3,192,1]{2,1,0:T(8,128)S(1)}, u32[]{:S(2)}, u32[]{:S(2)}) collective-permute-start(f32[3,192,1]{2,1,0:T(8,128)} %get-tuple-element.32), channel_id=1, source_target_pairs={{0,16},{16,32},{32,48},{48,64},{64,80},{80,96},{96,112},{112,128},... | collective-permute-start | bytes 6920 | tf_op jit(solution)/shard_map/ppermute | solution.py:25
  4.7 18.4 %collective-permute-start.4 = (f32[3,1,450]{2,1,0:T(1,128)S(1)}, f32[3,1,450]{2,1,0:T(1,128)S(1)}, u32[]{:S(2)}, u32[]{:S(2)}) collective-permute-start(f32[3,1,450]{2,1,0:T(1,128)S(1)} %get-tuple-element.28), channel_id=1, source_target_pairs={{1,0},{2,1},{3,2},{4,3},{5,4},{6,5},{7,6},{8,7},{9,8},{10,9},{11,1... | collective-permute-start | bytes 16208 | tf_op jit(solution)/shard_map/ppermute | solution.py:26
  12.1 7.1 %collective-permute-start.2 = (f32[3,450]{1,0:T(4,128)S(1)}, f32[3,450]{1,0:T(4,128)S(1)}, u32[]{:S(2)}, u32[]{:S(2)}) collective-permute-start(f32[3,450]{1,0:T(4,128)S(1)} %bitcast.145), channel_id=1, source_target_pairs={{0,128},{16,144},{32,160},{48,176},{64,192},{80,208},{96,224},{112... | collective-permute-start | bytes 16208 | tf_op jit(solution)/shard_map/ppermute | solution.py:33
  14.9 8.0 %collective-permute-start.3 = (f32[3,1,450]{2,0,1:T(4,128)S(1)}, f32[3,1,450]{2,0,1:T(4,128)S(1)}, u32[]{:S(2)}, u32[]{:S(2)}) collective-permute-start(f32[3,1,450]{2,0,1:T(4,128)S(1)} %copy.170), channel_id=1, source_target_pairs={{0,1},{1,2},{2,3},{3,4},{4,5},{5,6},{6,7},{7,8},{8,9},{9,10},{10,1... | collective-permute-start | bytes 16208 | tf_op jit(solution)/shard_map/ppermute | solution.py:25
  17.0 25.5 %copy-start.21 = (f32[192]{0:T(256)}, f32[192]{0:T(256)S(1)}, u32[]{:S(2)}) copy-start(f32[192]{0:T(256)S(1)} %get-tuple-element.57) | copy-start | bytes 2308
  17.0 25.5 %copy-start.23 = (f32[192]{0:T(256)}, f32[192]{0:T(256)S(1)}, u32[]{:S(2)}) copy-start(f32[192]{0:T(256)S(1)} %get-tuple-element.58) | copy-start | bytes 2308
  17.0 26.3 %copy-start.19 = (f32[192]{0:T(256)}, f32[192]{0:T(256)S(1)}, u32[]{:S(2)}) copy-start(f32[192]{0:T(256)S(1)} %get-tuple-element.10) | copy-start | bytes 2308
  17.7 28.3 %copy-start.3 = (f32[65,450]{1,0:T(8,128)}, f32[65,450]{1,0:T(8,128)S(1)}, u32[]{:S(2)}) copy-start(f32[65,450]{1,0:T(8,128)S(1)} %get-tuple-element.53) | copy-start | bytes 351004
  17.7 28.3 %copy-start.5 = (f32[65,450]{1,0:T(8,128)}, f32[65,450]{1,0:T(8,128)S(1)}, u32[]{:S(2)}) copy-start(f32[65,450]{1,0:T(8,128)S(1)} %get-tuple-element.54) | copy-start | bytes 351004
  18.6 4.3 %copy-start.28 = (f32[3]{0:T(128)S(1)}, f32[3]{0:T(128)}, u32[]{:S(2)}) copy-start(f32[3]{0:T(128)} %constant.136.clone) | copy-start | bytes 40
  24.9 4.4 %collective-permute-start.9 = (f32[3,1,450]{2,0,1:T(4,128)S(1)}, f32[3,1,450]{2,0,1:T(4,128)S(1)}, u32[]{:S(2)}, u32[]{:S(2)}) collective-permute-start(f32[3,1,450]{2,0,1:T(4,128)S(1)} %copy.198), channel_id=1, source_target_pairs={{1,0},{2,1},{3,2},{4,3},{5,4},{6,5},{7,6},{8,7},{9,8},{10,9},{11,1... | collective-permute-start | bytes 16208 | tf_op jit(solution)/shard_map/ppermute | solution.py:26
  28.3 7.4 %collective-permute-start.7 = (f32[3,450]{1,0:T(4,128)S(1)}, f32[3,450]{1,0:T(4,128)S(1)}, u32[]{:S(2)}, u32[]{:S(2)}) collective-permute-start(f32[3,450]{1,0:T(4,128)S(1)} %bitcast.146), channel_id=1, source_target_pairs={{0,128},{16,144},{32,160},{48,176},{64,192},{80,208},{96,224},{112... | collective-permute-start | bytes 16208 | tf_op jit(solution)/shard_map/ppermute | solution.py:33
  29.3 8.0 %collective-permute-start.8 = (f32[3,1,450]{2,0,1:T(4,128)S(1)}, f32[3,1,450]{2,0,1:T(4,128)S(1)}, u32[]{:S(2)}, u32[]{:S(2)}) collective-permute-start(f32[3,1,450]{2,0,1:T(4,128)S(1)} %get-tuple-element.42), channel_id=1, source_target_pairs={{0,1},{1,2},{2,3},{3,4},{4,5},{5,6},{6,7},{7,8},{8,9},{9,10},{10,1... | collective-permute-start | bytes 16208 | tf_op jit(solution)/shard_map/ppermute | solution.py:25
  31.4 8.7 %collective-permute-start.5 = (f32[3,192,1]{2,1,0:T(8,128)S(1)}, f32[3,192,1]{2,1,0:T(8,128)S(1)}, u32[]{:S(2)}, u32[]{:S(2)}) collective-permute-start(f32[3,192,1]{2,1,0:T(8,128)S(1)} %get-tuple-element.25), channel_id=1, source_target_pairs={{16,0},{32,16},{48,32},{64,48},{80,64},{96,80},{112,96},{128,112},... | collective-permute-start | bytes 6920 | tf_op jit(solution)/shard_map/ppermute | solution.py:26
  35.4 7.1 %collective-permute-start.6 = (f32[3,192,1]{2,1,0:T(8,128)S(1)}, f32[3,192,1]{2,1,0:T(8,128)S(1)}, u32[]{:S(2)}, u32[]{:S(2)}) collective-permute-start(f32[3,192,1]{2,1,0:T(8,128)S(1)} %get-tuple-element.26), channel_id=1, source_target_pairs={{0,16},{16,32},{32,48},{48,64},{64,80},{80,96},{96,112},{112,128},... | collective-permute-start | bytes 6920 | tf_op jit(solution)/shard_map/ppermute | solution.py:25
  43.3 1.5 copy-start.7
  51.2 14.2 %all-to-all-start = ((f32[16,1,4680]{2,1,0:T(1,128)}), f32[16,1,4680]{2,1,0:T(1,128)S(1)}, u32[]{:S(2)}, u32[]{:S(2)}) async-start(f32[16,1,4680]{2,1,0:T(1,128)} %reshape.320), calls=%async_computation | async-start | bytes 606208 | tf_op jit(solution)/shard_map/all_to_all | solution.py:73
  69.7 12.7 %all-to-all-start.1 = ((f32[16,1,6606]{2,1,0:T(1,128)}), f32[16,1,6606]{2,1,0:T(1,128)S(1)}, u32[]{:S(2)}, u32[]{:S(2)}) async-start(f32[16,1,6606]{2,1,0:T(1,128)} %all_to_all.32), calls=%async_computation.1 | async-start | bytes 851968 | tf_op jit(solution)/shard_map/all_to_all | solution.py:81
  74.2 10.6 %copy-start.14 = (f32[192,130]{1,0:T(8,128)}, f32[192,130]{1,0:T(8,128)S(1)}, u32[]{:S(2)}) copy-start(f32[192,130]{1,0:T(8,128)S(1)} %pad_maximum_fusion.52) | copy-start | bytes 299524
  84.7 1.0 copy-start.17
  84.8 0.9 copy-start.18
  84.9 0.8 copy-start.13
  84.9 1.9 %copy-start.8 = (f32[1,192,450]{2,1,0:T(8,128)S(1)}, f32[1,192,450]{2,1,0:T(8,128)}, u32[]{:S(2)}) copy-start(f32[1,192,450]{2,1,0:T(8,128)} %copy-done.7) | copy-start | bytes 1036804
  84.9 1.9 %copy-start.10 = (f32[1,192,450]{2,1,0:T(8,128)S(1)}, f32[1,192,450]{2,1,0:T(8,128)}, u32[]{:S(2)}) copy-start(f32[1,192,450]{2,1,0:T(8,128)} %copy-done.9) | copy-start | bytes 1036804
  84.9 1.9 %copy-start.12 = (f32[1,192,450]{2,1,0:T(8,128)S(1)}, f32[1,192,450]{2,1,0:T(8,128)}, u32[]{:S(2)}) copy-start(f32[1,192,450]{2,1,0:T(8,128)} %copy-done.11) | copy-start | bytes 1036804
  84.9 1.9 %copy-start.25 = (pred[192]{0:T(512)(128)(4,1)S(1)}, pred[192]{0:T(512)(128)(4,1)}, u32[]{:S(2)}) copy-start(pred[192]{0:T(512)(128)(4,1)} %add_compare_fusion) | copy-start | bytes 580
  87.4 10.6 %copy-start.31 = (f32[130]{0:T(256)S(1)}, f32[130]{0:T(256)}, u32[]{:S(2)}) copy-start(f32[130]{0:T(256)} %pad_maximum_fusion.71) | copy-start | bytes 1564
  87.4 16.5 %copy-start.4 = (f32[65,450]{1,0:T(8,128)S(1)}, f32[65,450]{1,0:T(8,128)}, u32[]{:S(2)}) copy-start(f32[65,450]{1,0:T(8,128)} %copy-done.3) | copy-start | bytes 351004
  87.4 16.5 %copy-start.6 = (f32[65,450]{1,0:T(8,128)S(1)}, f32[65,450]{1,0:T(8,128)}, u32[]{:S(2)}) copy-start(f32[65,450]{1,0:T(8,128)} %copy-done.5) | copy-start | bytes 351004
  87.4 16.5 %copy-start.26 = (pred[192]{0:T(512)(128)(4,1)S(1)}, pred[192]{0:T(512)(128)(4,1)}, u32[]{:S(2)}) copy-start(pred[192]{0:T(512)(128)(4,1)} %add_compare_fusion) | copy-start | bytes 580
  87.4 16.5 %copy-start.29 = (f32[3]{0:T(128)S(1)}, f32[3]{0:T(128)}, u32[]{:S(2)}) copy-start(f32[3]{0:T(128)} %constant.136.clone) | copy-start | bytes 40
  87.5 16.9 %copy-start.22 = (f32[192]{0:T(256)S(1)}, f32[192]{0:T(256)}, u32[]{:S(2)}) copy-start(f32[192]{0:T(256)} %copy-done.21) | copy-start | bytes 2308
  87.5 16.9 %copy-start.24 = (f32[192]{0:T(256)S(1)}, f32[192]{0:T(256)}, u32[]{:S(2)}) copy-start(f32[192]{0:T(256)} %copy-done.23) | copy-start | bytes 2308
  87.5 8.4 %collective-permute-start.11 = (f32[3,1,450]{2,0,1:T(4,128)S(1)}, f32[3,1,450]{2,0,1:T(4,128)S(1)}, u32[]{:S(2)}, u32[]{:S(2)}) collective-permute-start(f32[3,1,450]{2,0,1:T(4,128)S(1)} %copy.174), channel_id=1, source_target_pairs={{1,0},{2,1},{3,2},{4,3},{5,4},{6,5},{7,6},{8,7},{9,8},{10,9},{11,1... | collective-permute-start | bytes 16208 | tf_op jit(solution)/shard_map/ppermute | solution.py:26
  95.9 8.0 %collective-permute-start.10 = (f32[3,1,450]{2,0,1:T(4,128)S(1)}, f32[3,1,450]{2,0,1:T(4,128)S(1)}, u32[]{:S(2)}, u32[]{:S(2)}) collective-permute-start(f32[3,1,450]{2,0,1:T(4,128)S(1)} %get-tuple-element.40), channel_id=1, source_target_pairs={{0,1},{1,2},{2,3},{3,4},{4,5},{5,6},{6,7},{7,8},{8,9},{9,10},{10,1... | collective-permute-start | bytes 16208 | tf_op jit(solution)/shard_map/ppermute | solution.py:25
  104.2 1.0 copy-start.20
  106.9 4.4 %collective-permute-start.16 = (f32[3,1,450]{2,0,1:T(4,128)S(1)}, f32[3,1,450]{2,0,1:T(4,128)S(1)}, u32[]{:S(2)}, u32[]{:S(2)}) collective-permute-start(f32[3,1,450]{2,0,1:T(4,128)S(1)} %copy.197), channel_id=1, source_target_pairs={{1,0},{2,1},{3,2},{4,3},{5,4},{6,5},{7,6},{8,7},{9,8},{10,9},{11,1... | collective-permute-start | bytes 16208 | tf_op jit(solution)/shard_map/ppermute | solution.py:26
  109.9 7.8 %collective-permute-start.14 = (f32[3,450]{1,0:T(4,128)S(1)}, f32[3,450]{1,0:T(4,128)S(1)}, u32[]{:S(2)}, u32[]{:S(2)}) collective-permute-start(f32[3,450]{1,0:T(4,128)S(1)} %bitcast.147), channel_id=1, source_target_pairs={{0,128},{16,144},{32,160},{48,176},{64,192},{80,208},{96,224},{112... | collective-permute-start | bytes 16208 | tf_op jit(solution)/shard_map/ppermute | solution.py:33
  111.3 8.0 %collective-permute-start.15 = (f32[3,1,450]{2,0,1:T(4,128)S(1)}, f32[3,1,450]{2,0,1:T(4,128)S(1)}, u32[]{:S(2)}, u32[]{:S(2)}) collective-permute-start(f32[3,1,450]{2,0,1:T(4,128)S(1)} %get-tuple-element.36), channel_id=1, source_target_pairs={{0,1},{1,2},{2,3},{3,4},{4,5},{5,6},{6,7},{7,8},{8,9},{9,10},{10,1... | collective-permute-start | bytes 16208 | tf_op jit(solution)/shard_map/ppermute | solution.py:25
  113.8 11.5 %collective-permute-start.12 = (f32[3,192,1]{2,1,0:T(8,128)S(1)}, f32[3,192,1]{2,1,0:T(8,128)S(1)}, u32[]{:S(2)}, u32[]{:S(2)}) collective-permute-start(f32[3,192,1]{2,1,0:T(8,128)S(1)} %get-tuple-element.19), channel_id=1, source_target_pairs={{16,0},{32,16},{48,32},{64,48},{80,64},{96,80},{112,96},{128,112},... | collective-permute-start | bytes 6920 | tf_op jit(solution)/shard_map/ppermute | solution.py:26
  117.1 8.1 %collective-permute-start.13 = (f32[3,192,1]{2,1,0:T(8,128)S(1)}, f32[3,192,1]{2,1,0:T(8,128)S(1)}, u32[]{:S(2)}, u32[]{:S(2)}) collective-permute-start(f32[3,192,1]{2,1,0:T(8,128)S(1)} %get-tuple-element.20), channel_id=1, source_target_pairs={{0,16},{16,32},{32,48},{48,64},{64,80},{80,96},{96,112},{112,128},... | collective-permute-start | bytes 6920 | tf_op jit(solution)/shard_map/ppermute | solution.py:25
  163.1 2.2 %copy-start.27 = (pred[192]{0:T(512)(128)(4,1)S(1)}, pred[192]{0:T(512)(128)(4,1)}, u32[]{:S(2)}) copy-start(pred[192]{0:T(512)(128)(4,1)} %add_compare_fusion) | copy-start | bytes 580
  164.1 1.3 copy-start.15
  (3 other events, 2.3 us)

commit v2 on v1

--- a/solution.py
+++ b/solution.py
@@ -191,14 +191,20 @@
     table = local_table(0, width)
     wide_table = local_table(-1, width + 2)
     state = jnp.stack([height, east_wind, north_wind], axis=0)
-    lon_halos = None
-    for step_index in range(STEPS):
+    edge_cols = jnp.concatenate([state[:, :, :1], state[:, :, -1:]], axis=2)
+    got_cols = with_halo(edge_cols, (("lon", 2),), 1, True)
+    mirror = from_behind(state[:, 0, :], "lon", lax.axis_size("lon") // 2)
+    lon_halos = (got_cols[:, :, 0:1], got_cols[:, :, 3:4], mirror)
+
+    def one_step(step_index, carry):
+        state, lon_halos = carry
         rates = tendency(state, cos_all, sinlat, lon_step, lat_step, lon_halos)
         middle = state + 0.5 * time_step * rates
         rates = tendency(middle, cos_all, sinlat, lon_step, lat_step)
         advanced = state + time_step * rates
-        last = step_index == STEPS - 1
-        state, lon_halos = filter_state(advanced, cutoffs, table, wide_table, not last)
+        return filter_state(advanced, cutoffs, table, wide_table, True)
+
+    state, lon_halos = lax.fori_loop(0, STEPS, one_step, (state, lon_halos))
     return (state[0], state[1], state[2])
 
 

time: 169 us -> 196 us (1.16)
  waiting for transfers between devices: 36.7 us -> 60.7 us
  blocking collectives: 22.7 us -> 0 us
  local copies, waits for them, and re-layouts: 23.9 us -> 33.5 us
  starting transfers between devices: 53.3 us -> 60.4 us
  other arithmetic: 22.5 us -> 29 us
    all_to_all x2 -> x0, blocking collectives: 22.7 us -> none  [the longest x1 12 us: low_pass(): lax.all_to_all(partial, 'lon', split_axis=1, concat_axis=0, tiled=True)]
    ppermute x7, waiting for transfers between devices: 13.2 us -> 26.6 us  [with_halo(): before = lax.ppermute(last, axis, up)]
    while x0 -> x54, local copies, waits for them, and re-layouts: none -> 10.6 us
    all_to_all x1 -> x2, waiting for transfers between devices: 6.9 us -> 15.9 us  [low_pass(): lax.all_to_all(jnp.concatenate(payload, axis=1), 'lon', split_axis=0, con...]
    ppermute x7, starting transfers between devices: 10.3 us -> 19 us  [with_halo(): before = lax.ppermute(last, axis, up)]
    unnamed x76 -> x5, local copies, waits for them, and re-layouts: 8.49 us -> 0.02 us
    ppermute x7, starting transfers between devices: 28.2 us -> 21.4 us  [with_halo(): after = lax.ppermute(first, axis, down)]
    all_to_all x1 -> x2, waiting for transfers between devices: 7.51 us -> 11.5 us  [low_pass(): lax.all_to_all(partial, 'lon', split_axis=1, concat_axis=0, tiled=True)]
  transfers between devices with their start and end apart: 19 -> 21, of which waited for: 10 -> 14; matrix products, arithmetic and copies ran while one was open for 5% -> 7% of each run, Pallas kernels for 0% -> 0%
where the time goes in v2:
time: 196 us; the launch traced here: 194 us
  waiting for transfers between devices  60.7 us (31%)
  starting transfers between devices  60.4 us (31%)
  local copies, waits for them, and re-layouts  33.5 us (17%)
  other arithmetic  29 us (15%)
  matrix products  8.25 us (4%)
    ppermute x7, waiting for transfers between devices, with_halo(): before = lax.ppermute(last, axis, up)  26.6 us
    ppermute x7, starting transfers between devices, with_halo(): after = lax.ppermute(first, axis, down)  21.4 us
    ppermute x7, starting transfers between devices, with_halo(): before = lax.ppermute(last, axis, up)  19 us
    all_to_all x2, waiting for transfers between devices, low_pass(): lax.all_to_all(jnp.concatenate(payload, axis=1), 'lon', split_axis=0, con...  15.9 us
    all_to_all x2, waiting for transfers between devices, low_pass(): lax.all_to_all(partial, 'lon', split_axis=1, concat_axis=0, tiled=True)  11.5 us
    while x54, local copies, waits for them, and re-layouts  10.6 us
    all_to_all x2, starting transfers between devices, low_pass(): lax.all_to_all(partial, 'lon', split_axis=1, concat_axis=0, tiled=True)  8.19 us
    all_to_all x2, starting transfers between devices, low_pass(): lax.all_to_all(jnp.concatenate(payload, axis=1), 'lon', split_axis=0, con...  7.56 us
  transfers between devices with their start and end apart: 21, of which 14 were waited for; matrix products, arithmetic and copies ran while one was open for 7% of the time, Pallas kernels for 0%

profile of v2, /device:TPU:17, one launch (start us, length us, event | category | flops | bytes accessed | tf_op | source)
XLA Modules:
  0.0 193.7 jit_solution(6695303868946862021)
XLA Ops:
  0.6 1.3 pad_maximum_fusion.31
  2.0 2.8 %collective-permute-start.9 = (f32[3,450]{1,0:T(4,128)S(1)}, f32[3,450]{1,0:T(4,128)S(1)}, u32[]{:S(2)}, u32[]{:S(2)}) collective-permute-start(f32[3,450]{1,0:T(4,128)S(1)} %bitcast.106), channel_id=1, source_target_pairs={{0,128},{16,144},{32,160},{48,176},{64,192},{80,208},{96,224},{112... | collective-permute-start | bytes 16208 | tf_op jit(solution)/shard_map/ppermute | solution.py:33
  5.0 1.0 collective-permute-start.8
  9.9 1.4 collective-permute-done.8
  11.3 2.5 %collective-permute-done.7 = f32[3,192,1]{2,1,0:T(8,128)S(1)} collective-permute-done((f32[3,192,1]{2,1,0:T(8,128)S(1)}, f32[3,192,1]{2,1,0:T(8,128)S(1)}, u32[]{:S(2)}, u32[]{:S(2)}) %collective-permute-start.7) | collective-permute-done | bytes 2336 | tf_op jit(solution)/shard_map/ppermute | solution.py:25
  13.8 178.8 %while.21 = (s32[]{:T(128)}, f32[3,192,450]{2,1,0:T(8,128)S(1)}, f32[3,192,1]{2,1,0:T(8,128)S(1)}, f32[3,192,1]{2,1,0:T(8,128)S(1)}, f32[3,450]{1,0:T(4,128)S(1)...) while((s32[]{:T(128)}, f32[3,192,450]{2,1,0:T(8,128)S(1)}, ...), condition=%wide.region_2.3_spmd.clone.clone, body=%wide.region_0.2_spmd.sunk.clone.clone.sunk | while | flops 831926592 | bytes 43611840 | solution.py:207
  14.1 7.5 %collective-permute-start = (f32[3,1,450]{2,1,0:T(1,128)S(1)}, f32[3,1,450]{2,1,0:T(1,128)S(1)}, u32[]{:S(2)}, u32[]{:S(2)}) collective-permute-start(f32[3,1,450]{2,1,0:T(1,128)S(1)} %slice.855), channel_id=1, source_target_pairs={{1,0},{2,1},{3,2},{4,3},{5,4},{6,5},{7,6},{8,7},{9,8},{10,9},{11,1... | collective-permute-start | bytes 16208 | tf_op jit(solution)/shard_map/while/body/eval_jaxpr/ppermute | solution.py:26
  22.9 1.9 collective-permute-start.1
  25.5 5.4 %collective-permute-done.1 = f32[3,1,450]{2,1,0:T(1,128)S(1)} collective-permute-done((f32[3,1,450]{2,1,0:T(1,128)S(1)}, f32[3,1,450]{2,1,0:T(1,128)S(1)}, u32[]{:S(2)}, u32[]{:S(2)}) %collective-permute-start.1) | collective-permute-done | bytes 5432 | tf_op jit(solution)/shard_map/while/body/eval_jaxpr/ppermute | solution.py:25
  33.7 3.1 %collective-permute-start.4 = (f32[3,1,450]{2,0,1:T(4,128)S(1)}, f32[3,1,450]{2,0,1:T(4,128)S(1)}, u32[]{:S(2)}, u32[]{:S(2)}) collective-permute-start(f32[3,1,450]{2,0,1:T(4,128)S(1)} %copy.119), channel_id=1, source_target_pairs={{1,0},{2,1},{3,2},{4,3},{5,4},{6,5},{7,6},{8,7},{9,8},{10,9},{11,1... | collective-permute-start | bytes 16208 | tf_op jit(solution)/shard_map/while/body/eval_jaxpr/ppermute | solution.py:26
  38.1 1.9 collective-permute-start.5
  40.2 6.0 %collective-permute-start.2 = (f32[3,192,1]{2,1,0:T(8,128)S(1)}, f32[3,192,1]{2,1,0:T(8,128)S(1)}, u32[]{:S(2)}, u32[]{:S(2)}) collective-permute-start(f32[3,192,1]{2,1,0:T(8,128)S(1)} %get-tuple-element.396), channel_id=1, source_target_pairs={{0,16},{16,32},{32,48},{48,64},{64,80},{80,96},{96,112},{112,128},... | collective-permute-start | bytes 6920 | tf_op jit(solution)/shard_map/while/body/eval_jaxpr/ppermute | solution.py:25
  46.4 6.6 %collective-permute-done.2 = f32[3,192,1]{2,1,0:T(8,128)S(1)} collective-permute-done((f32[3,192,1]{2,1,0:T(8,128)S(1)}, f32[3,192,1]{2,1,0:T(8,128)S(1)}, u32[]{:S(2)}, u32[]{:S(2)}) %collective-permute-start.2) | collective-permute-done | bytes 2336 | tf_op jit(solution)/shard_map/while/body/eval_jaxpr/ppermute | solution.py:25
  53.0 2.3 %collective-permute-done.3 = f32[3,192,1]{2,1,0:T(8,128)S(1)} collective-permute-done((f32[3,192,1]{2,1,0:T(8,128)S(1)}, f32[3,192,1]{2,1,0:T(8,128)S(1)}, u32[]{:S(2)}, u32[]{:S(2)}) %collective-permute-start.3) | collective-permute-done | bytes 2336 | tf_op jit(solution)/shard_map/while/body/eval_jaxpr/ppermute | solution.py:26
  57.9 1.0 slice_reduce_fusion.5
  58.9 2.1 %fusion.115 = f32[3,192,130]{1,2,0:T(8,128)} fusion(f32[3,192,450]{2,1,0:T(8,128)S(1)} %fusion.114, f32[130,450]{1,0:T(8,128)S(1)} %copy-done), kind=kOutput, calls=%fused_computation.96.clone.1 | convolution fusion | flops 404352000 | bytes 1570320 | tf_op jit(solution)/shard_map/while/body/eval_jaxpr/fnw,kw->fnk/dot_general | solution.py:59
  61.0 2.2 %copy.122 = f32[3,192,130]{2,0,1:T(4,128)} copy(f32[3,192,130]{1,2,0:T(8,128)} %fusion.115) | data formatting | bytes 599040 | tf_op jit(solution)/shard_map/while/body/eval_jaxpr/fnw,kw->fnk/dot_general | solution.py:59
  63.2 2.9 %reshape.306 = f32[16,1,4680]{2,1,0:T(1,128)} reshape(f32[192,3,130]{2,1,0:T(4,128)} %bitcast.89) | data formatting | bytes 599040 | tf_op jit(solution)/shard_map/while
  66.0 4.1 %all-to-all-start = ((f32[16,1,4680]{2,1,0:T(1,128)}), f32[16,1,4680]{2,1,0:T(1,128)}, u32[]{:S(2)}, u32[]{:S(2)}) async-start(f32[16,1,4680]{2,1,0:T(1,128)} %reshape.306), calls=%async_computation | async-start | bytes 606208 | tf_op jit(solution)/shard_map/while/body/eval_jaxpr/all_to_all | solution.py:73
  71.7 5.9 %all-to-all-done = f32[16,1,4680]{2,1,0:T(1,128)} async-done(((f32[16,1,4680]{2,1,0:T(1,128)}), f32[16,1,4680]{2,1,0:T(1,128)}, u32[]{:S(2)}, u32[]{:S(2)}) %all-to-all-start) | async-done | bytes 299552 | tf_op jit(solution)/shard_map/while/body/eval_jaxpr/all_to_all | solution.py:73
  78.2 2.3 %reduce.14 = f32[16,4680]{1,0:T(8,128)S(1)} reduce(f32[16,1,4680]{2,1,0:T(1,128)} %all-to-all-done, f32[]{:T(128)} %broadcast.451), dimensions={1}, to_apply=%all_to_all.39.reduce_sub_computation | reduce | bytes 599044 | tf_op jit(solution)/shard_map/while/body/eval_jaxpr/all_to_all | solution.py:73
  82.0 1.1 all_to_all.48
  83.0 3.8 %all-to-all-start.1 = ((f32[16,1,6606]{2,1,0:T(1,128)}), f32[16,1,6606]{2,1,0:T(1,128)S(1)}, u32[]{:S(2)}, u32[]{:S(2)}) async-start(f32[16,1,6606]{2,1,0:T(1,128)} %all_to_all.48), calls=%async_computation.1 | async-start | bytes 851968 | tf_op jit(solution)/shard_map/while/body/eval_jaxpr/all_to_all | solution.py:81
  87.8 7.9 %all-to-all-done.1 = f32[16,1,6606]{2,1,0:T(1,128)S(1)} async-done(((f32[16,1,6606]{2,1,0:T(1,128)}), f32[16,1,6606]{2,1,0:T(1,128)S(1)}, u32[]{:S(2)}, u32[]{:S(2)}) %all-to-all-start.1) | async-done | bytes 422816 | tf_op jit(solution)/shard_map/while/body/eval_jaxpr/all_to_all | solution.py:81
  98.4 1.2 reshape.309
  100.6 1.1 fusion.117
  104.6 6.7 %collective-permute-start = (f32[3,1,450]{2,1,0:T(1,128)S(1)}, f32[3,1,450]{2,1,0:T(1,128)S(1)}, u32[]{:S(2)}, u32[]{:S(2)}) collective-permute-start(f32[3,1,450]{2,1,0:T(1,128)S(1)} %slice.855), channel_id=1, source_target_pairs={{1,0},{2,1},{3,2},{4,3},{5,4},{6,5},{7,6},{8,7},{9,8},{10,9},{11,1... | collective-permute-start | bytes 16208 | tf_op jit(solution)/shard_map/while/body/eval_jaxpr/ppermute | solution.py:26
  112.5 1.9 collective-permute-start.1
  115.1 5.4 %collective-permute-done.1 = f32[3,1,450]{2,1,0:T(1,128)S(1)} collective-permute-done((f32[3,1,450]{2,1,0:T(1,128)S(1)}, f32[3,1,450]{2,1,0:T(1,128)S(1)}, u32[]{:S(2)}, u32[]{:S(2)}) %collective-permute-start.1) | collective-permute-done | bytes 5432 | tf_op jit(solution)/shard_map/while/body/eval_jaxpr/ppermute | solution.py:25
  123.3 3.1 %collective-permute-start.4 = (f32[3,1,450]{2,0,1:T(4,128)S(1)}, f32[3,1,450]{2,0,1:T(4,128)S(1)}, u32[]{:S(2)}, u32[]{:S(2)}) collective-permute-start(f32[3,1,450]{2,0,1:T(4,128)S(1)} %copy.119), channel_id=1, source_target_pairs={{1,0},{2,1},{3,2},{4,3},{5,4},{6,5},{7,6},{8,7},{9,8},{10,9},{11,1... | collective-permute-start | bytes 16208 | tf_op jit(solution)/shard_map/while/body/eval_jaxpr/ppermute | solution.py:26
  126.8 1.3 collective-permute-start.6
  128.2 2.2 %collective-permute-start.5 = (f32[3,1,450]{2,0,1:T(4,128)S(1)}, f32[3,1,450]{2,0,1:T(4,128)S(1)}, u32[]{:S(2)}, u32[]{:S(2)}) collective-permute-start(f32[3,1,450]{2,0,1:T(4,128)S(1)} %get-tuple-element.401), channel_id=1, source_target_pairs={{0,1},{1,2},{2,3},{3,4},{4,5},{5,6},{6,7},{7,8},{8,9},{9,10},{10,1... | collective-permute-start | bytes 16208 | tf_op jit(solution)/shard_map/while/body/eval_jaxpr/ppermute | solution.py:25
  130.5 4.0 %collective-permute-start.2 = (f32[3,192,1]{2,1,0:T(8,128)S(1)}, f32[3,192,1]{2,1,0:T(8,128)S(1)}, u32[]{:S(2)}, u32[]{:S(2)}) collective-permute-start(f32[3,192,1]{2,1,0:T(8,128)S(1)} %get-tuple-element.396), channel_id=1, source_target_pairs={{0,16},{16,32},{32,48},{48,64},{64,80},{80,96},{96,112},{112,128},... | collective-permute-start | bytes 6920 | tf_op jit(solution)/shard_map/while/body/eval_jaxpr/ppermute | solution.py:25
  134.5 1.6 collective-permute-done.5
  136.3 5.0 %collective-permute-done.2 = f32[3,192,1]{2,1,0:T(8,128)S(1)} collective-permute-done((f32[3,192,1]{2,1,0:T(8,128)S(1)}, f32[3,192,1]{2,1,0:T(8,128)S(1)}, u32[]{:S(2)}, u32[]{:S(2)}) %collective-permute-start.2) | collective-permute-done | bytes 2336 | tf_op jit(solution)/shard_map/while/body/eval_jaxpr/ppermute | solution.py:25
  141.4 2.5 %collective-permute-done.3 = f32[3,192,1]{2,1,0:T(8,128)S(1)} collective-permute-done((f32[3,192,1]{2,1,0:T(8,128)S(1)}, f32[3,192,1]{2,1,0:T(8,128)S(1)}, u32[]{:S(2)}, u32[]{:S(2)}) %collective-permute-start.3) | collective-permute-done | bytes 2336 | tf_op jit(solution)/shard_map/while/body/eval_jaxpr/ppermute | solution.py:26
  147.5 2.1 %fusion.115 = f32[3,192,130]{1,2,0:T(8,128)} fusion(f32[3,192,450]{2,1,0:T(8,128)S(1)} %fusion.114, f32[130,450]{1,0:T(8,128)S(1)} %copy-done), kind=kOutput, calls=%fused_computation.96.clone.1 | convolution fusion | flops 404352000 | bytes 1570320 | tf_op jit(solution)/shard_map/while/body/eval_jaxpr/fnw,kw->fnk/dot_general | solution.py:59
  149.5 2.2 %copy.122 = f32[3,192,130]{2,0,1:T(4,128)} copy(f32[3,192,130]{1,2,0:T(8,128)} %fusion.115) | data formatting | bytes 599040 | tf_op jit(solution)/shard_map/while/body/eval_jaxpr/fnw,kw->fnk/dot_general | solution.py:59
  151.7 2.9 %reshape.306 = f32[16,1,4680]{2,1,0:T(1,128)} reshape(f32[192,3,130]{2,1,0:T(4,128)} %bitcast.89) | data formatting | bytes 599040 | tf_op jit(solution)/shard_map/while
  154.6 4.1 %all-to-all-start = ((f32[16,1,4680]{2,1,0:T(1,128)}), f32[16,1,4680]{2,1,0:T(1,128)}, u32[]{:S(2)}, u32[]{:S(2)}) async-start(f32[16,1,4680]{2,1,0:T(1,128)} %reshape.306), calls=%async_computation | async-start | bytes 606208 | tf_op jit(solution)/shard_map/while/body/eval_jaxpr/all_to_all | solution.py:73
  160.3 5.5 %all-to-all-done = f32[16,1,4680]{2,1,0:T(1,128)} async-done(((f32[16,1,4680]{2,1,0:T(1,128)}), f32[16,1,4680]{2,1,0:T(1,128)}, u32[]{:S(2)}, u32[]{:S(2)}) %all-to-all-start) | async-done | bytes 299552 | tf_op jit(solution)/shard_map/while/body/eval_jaxpr/all_to_all | solution.py:73
  166.3 2.3 %reduce.14 = f32[16,4680]{1,0:T(8,128)S(1)} reduce(f32[16,1,4680]{2,1,0:T(1,128)} %all-to-all-done, f32[]{:T(128)} %broadcast.451), dimensions={1}, to_apply=%all_to_all.39.reduce_sub_computation | reduce | bytes 599044 | tf_op jit(solution)/shard_map/while/body/eval_jaxpr/all_to_all | solution.py:73
  170.1 1.1 all_to_all.48
  171.2 3.8 %all-to-all-start.1 = ((f32[16,1,6606]{2,1,0:T(1,128)}), f32[16,1,6606]{2,1,0:T(1,128)S(1)}, u32[]{:S(2)}, u32[]{:S(2)}) async-start(f32[16,1,6606]{2,1,0:T(1,128)} %all_to_all.48), calls=%async_computation.1 | async-start | bytes 851968 | tf_op jit(solution)/shard_map/while/body/eval_jaxpr/all_to_all | solution.py:81
  175.9 7.9 %all-to-all-done.1 = f32[16,1,6606]{2,1,0:T(1,128)S(1)} async-done(((f32[16,1,6606]{2,1,0:T(1,128)}), f32[16,1,6606]{2,1,0:T(1,128)S(1)}, u32[]{:S(2)}, u32[]{:S(2)}) %all-to-all-start.1) | async-done | bytes 422816 | tf_op jit(solution)/shard_map/while/body/eval_jaxpr/all_to_all | solution.py:81
  186.6 1.2 reshape.309
  188.8 1.1 fusion.117
  192.7 1.0 slice_bitcast_fusion
  (191 shorter events, 43.6 us)
Async XLA Ops:
  2.0 11.9 %collective-permute-start.9 = (f32[3,450]{1,0:T(4,128)S(1)}, f32[3,450]{1,0:T(4,128)S(1)}, u32[]{:S(2)}, u32[]{:S(2)}) collective-permute-start(f32[3,450]{1,0:T(4,128)S(1)} %bitcast.106), channel_id=1, source_target_pairs={{0,128},{16,144},{32,160},{48,176},{64,192},{80,208},{96,224},{112... | collective-permute-start | bytes 16208 | tf_op jit(solution)/shard_map/ppermute | solution.py:33
  5.0 8.9 %copy-start.7 = (f32[3]{0:T(128)S(1)}, f32[3]{0:T(128)}, u32[]{:S(2)}) copy-start(f32[3]{0:T(128)} %constant.247.clone..sunk.5) | copy-start | bytes 40
  5.0 8.9 %copy-start.9 = (s32[512]{0:T(512)S(1)}, s32[512]{0:T(512)}, u32[]{:S(2)}) copy-start(s32[512]{0:T(512)} %param.11) | copy-start | bytes 6148
  5.0 6.3 %collective-permute-start.8 = (f32[3,192,1]{2,1,0:T(8,128)S(1)}, f32[3,192,1]{2,1,0:T(8,128)S(1)}, u32[]{:S(2)}, u32[]{:S(2)}) collective-permute-start(f32[3,192,1]{2,1,0:T(8,128)S(1)} %get-tuple-element.299), channel_id=1, source_target_pairs={{16,0},{32,16},{48,32},{64,48},{80,64},{96,80},{112,96},{128,112},... | collective-permute-start | bytes 6920 | tf_op jit(solution)/shard_map/ppermute | solution.py:26
  6.0 7.8 %collective-permute-start.7 = (f32[3,192,1]{2,1,0:T(8,128)S(1)}, f32[3,192,1]{2,1,0:T(8,128)S(1)}, u32[]{:S(2)}, u32[]{:S(2)}) collective-permute-start(f32[3,192,1]{2,1,0:T(8,128)S(1)} %get-tuple-element.300), channel_id=1, source_target_pairs={{0,16},{16,32},{32,48},{48,64},{64,80},{80,96},{96,112},{112,128},... | collective-permute-start | bytes 6920 | tf_op jit(solution)/shard_map/ppermute | solution.py:25
  14.0 17.8 %copy-start.4 = (f32[194]{0:T(256)}, f32[194]{0:T(256)S(1)}, u32[]{:S(2)}) copy-start(f32[194]{0:T(256)S(1)} %get-tuple-element.463) | copy-start | bytes 2332 | tf_op jit(solution)/shard_map/while
  14.1 8.9 %collective-permute-start = (f32[3,1,450]{2,1,0:T(1,128)S(1)}, f32[3,1,450]{2,1,0:T(1,128)S(1)}, u32[]{:S(2)}, u32[]{:S(2)}) collective-permute-start(f32[3,1,450]{2,1,0:T(1,128)S(1)} %slice.855), channel_id=1, source_target_pairs={{1,0},{2,1},{3,2},{4,3},{5,4},{6,5},{7,6},{8,7},{9,8},{10,9},{11,1... | collective-permute-start | bytes 16208 | tf_op jit(solution)/shard_map/while/body/eval_jaxpr/ppermute | solution.py:26
  22.9 8.0 %collective-permute-start.1 = (f32[3,1,450]{2,1,0:T(1,128)S(1)}, f32[3,1,450]{2,1,0:T(1,128)S(1)}, u32[]{:S(2)}, u32[]{:S(2)}) collective-permute-start(f32[3,1,450]{2,1,0:T(1,128)S(1)} %get-tuple-element.391), channel_id=1, source_target_pairs={{0,1},{1,2},{2,3},{3,4},{4,5},{5,6},{6,7},{7,8},{8,9},{9,10},{10,1... | collective-permute-start | bytes 16208 | tf_op jit(solution)/shard_map/while/body/eval_jaxpr/ppermute | solution.py:25
  33.7 4.4 %collective-permute-start.4 = (f32[3,1,450]{2,0,1:T(4,128)S(1)}, f32[3,1,450]{2,0,1:T(4,128)S(1)}, u32[]{:S(2)}, u32[]{:S(2)}) collective-permute-start(f32[3,1,450]{2,0,1:T(4,128)S(1)} %copy.119), channel_id=1, source_target_pairs={{1,0},{2,1},{3,2},{4,3},{5,4},{6,5},{7,6},{8,7},{9,8},{10,9},{11,1... | collective-permute-start | bytes 16208 | tf_op jit(solution)/shard_map/while/body/eval_jaxpr/ppermute | solution.py:26
  37.2 9.0 %collective-permute-start.6 = (f32[3,450]{1,0:T(4,128)S(1)}, f32[3,450]{1,0:T(4,128)S(1)}, u32[]{:S(2)}, u32[]{:S(2)}) collective-permute-start(f32[3,450]{1,0:T(4,128)S(1)} %bitcast.104), channel_id=1, source_target_pairs={{0,128},{16,144},{32,160},{48,176},{64,192},{80,208},{96,224},{112... | collective-permute-start | bytes 16208 | tf_op jit(solution)/shard_map/while/body/eval_jaxpr/ppermute | solution.py:33
  38.1 8.1 %collective-permute-start.5 = (f32[3,1,450]{2,0,1:T(4,128)S(1)}, f32[3,1,450]{2,0,1:T(4,128)S(1)}, u32[]{:S(2)}, u32[]{:S(2)}) collective-permute-start(f32[3,1,450]{2,0,1:T(4,128)S(1)} %get-tuple-element.401), channel_id=1, source_target_pairs={{0,1},{1,2},{2,3},{3,4},{4,5},{5,6},{6,7},{7,8},{8,9},{9,10},{10,1... | collective-permute-start | bytes 16208 | tf_op jit(solution)/shard_map/while/body/eval_jaxpr/ppermute | solution.py:25
  40.2 12.9 %collective-permute-start.2 = (f32[3,192,1]{2,1,0:T(8,128)S(1)}, f32[3,192,1]{2,1,0:T(8,128)S(1)}, u32[]{:S(2)}, u32[]{:S(2)}) collective-permute-start(f32[3,192,1]{2,1,0:T(8,128)S(1)} %get-tuple-element.396), channel_id=1, source_target_pairs={{0,16},{16,32},{32,48},{48,64},{64,80},{80,96},{96,112},{112,128},... | collective-permute-start | bytes 6920 | tf_op jit(solution)/shard_map/while/body/eval_jaxpr/ppermute | solution.py:25
  46.2 9.1 %collective-permute-start.3 = (f32[3,192,1]{2,1,0:T(8,128)S(1)}, f32[3,192,1]{2,1,0:T(8,128)S(1)}, u32[]{:S(2)}, u32[]{:S(2)}) collective-permute-start(f32[3,192,1]{2,1,0:T(8,128)S(1)} %get-tuple-element.397), channel_id=1, source_target_pairs={{16,0},{32,16},{48,32},{64,48},{80,64},{96,80},{112,96},{128,112},... | collective-permute-start | bytes 6920 | tf_op jit(solution)/shard_map/while/body/eval_jaxpr/ppermute | solution.py:26
  57.6 1.3 copy-start
  66.0 11.6 %all-to-all-start = ((f32[16,1,4680]{2,1,0:T(1,128)}), f32[16,1,4680]{2,1,0:T(1,128)}, u32[]{:S(2)}, u32[]{:S(2)}) async-start(f32[16,1,4680]{2,1,0:T(1,128)} %reshape.306), calls=%async_computation | async-start | bytes 606208 | tf_op jit(solution)/shard_map/while/body/eval_jaxpr/all_to_all | solution.py:73
  81.8 5.0 %copy-start.6 = (s32[192]{0:T(256)S(1)}, s32[192]{0:T(256)}, u32[]{:S(2)}) copy-start(s32[192]{0:T(256)} %pad_dynamic-slice_fusion.2) | copy-start | bytes 2308 | tf_op jit(solution)/shard_map/while
  81.8 5.0 %copy-start.12 = (f32[65]{0:T(128)S(1)}, f32[65]{0:T(128)}, u32[]{:S(2)}) copy-start(f32[65]{0:T(128)} %get-tuple-element.406) | copy-start | bytes 784 | tf_op jit(solution)/shard_map/while
  83.0 12.7 %all-to-all-start.1 = ((f32[16,1,6606]{2,1,0:T(1,128)}), f32[16,1,6606]{2,1,0:T(1,128)S(1)}, u32[]{:S(2)}, u32[]{:S(2)}) async-start(f32[16,1,6606]{2,1,0:T(1,128)} %all_to_all.48), calls=%async_computation.1 | async-start | bytes 851968 | tf_op jit(solution)/shard_map/while/body/eval_jaxpr/all_to_all | solution.py:81
  97.5 2.2 %copy-start.2 = (f32[192,130]{1,0:T(8,128)S(1)}, f32[192,130]{1,0:T(8,128)}, u32[]{:S(2)}) copy-start(f32[192,130]{1,0:T(8,128)} %pad_maximum_fusion.40) | copy-start | bytes 299524 | tf_op jit(solution)/shard_map/while
  98.4 1.3 copy-start.11
  99.7 1.0 copy-start.3
  102.6 1.0 copy-start.1
  102.6 1.9 copy-start.5
  102.6 1.9 copy-start.8
  102.6 1.9 copy-start.10
  104.5 16.9 %copy-start.4 = (f32[194]{0:T(256)}, f32[194]{0:T(256)S(1)}, u32[]{:S(2)}) copy-start(f32[194]{0:T(256)S(1)} %get-tuple-element.463) | copy-start | bytes 2332 | tf_op jit(solution)/shard_map/while
  104.6 8.0 %collective-permute-start = (f32[3,1,450]{2,1,0:T(1,128)S(1)}, f32[3,1,450]{2,1,0:T(1,128)S(1)}, u32[]{:S(2)}, u32[]{:S(2)}) collective-permute-start(f32[3,1,450]{2,1,0:T(1,128)S(1)} %slice.855), channel_id=1, source_target_pairs={{1,0},{2,1},{3,2},{4,3},{5,4},{6,5},{7,6},{8,7},{9,8},{10,9},{11,1... | collective-permute-start | bytes 16208 | tf_op jit(solution)/shard_map/while/body/eval_jaxpr/ppermute | solution.py:26
  112.5 8.0 %collective-permute-start.1 = (f32[3,1,450]{2,1,0:T(1,128)S(1)}, f32[3,1,450]{2,1,0:T(1,128)S(1)}, u32[]{:S(2)}, u32[]{:S(2)}) collective-permute-start(f32[3,1,450]{2,1,0:T(1,128)S(1)} %get-tuple-element.391), channel_id=1, source_target_pairs={{0,1},{1,2},{2,3},{3,4},{4,5},{5,6},{6,7},{7,8},{8,9},{9,10},{10,1... | collective-permute-start | bytes 16208 | tf_op jit(solution)/shard_map/while/body/eval_jaxpr/ppermute | solution.py:25
  123.3 4.9 %collective-permute-start.4 = (f32[3,1,450]{2,0,1:T(4,128)S(1)}, f32[3,1,450]{2,0,1:T(4,128)S(1)}, u32[]{:S(2)}, u32[]{:S(2)}) collective-permute-start(f32[3,1,450]{2,0,1:T(4,128)S(1)} %copy.119), channel_id=1, source_target_pairs={{1,0},{2,1},{3,2},{4,3},{5,4},{6,5},{7,6},{8,7},{9,8},{10,9},{11,1... | collective-permute-start | bytes 16208 | tf_op jit(solution)/shard_map/while/body/eval_jaxpr/ppermute | solution.py:26
  126.8 7.7 %collective-permute-start.6 = (f32[3,450]{1,0:T(4,128)S(1)}, f32[3,450]{1,0:T(4,128)S(1)}, u32[]{:S(2)}, u32[]{:S(2)}) collective-permute-start(f32[3,450]{1,0:T(4,128)S(1)} %bitcast.104), channel_id=1, source_target_pairs={{0,128},{16,144},{32,160},{48,176},{64,192},{80,208},{96,224},{112... | collective-permute-start | bytes 16208 | tf_op jit(solution)/shard_map/while/body/eval_jaxpr/ppermute | solution.py:33
  128.2 8.0 %collective-permute-start.5 = (f32[3,1,450]{2,0,1:T(4,128)S(1)}, f32[3,1,450]{2,0,1:T(4,128)S(1)}, u32[]{:S(2)}, u32[]{:S(2)}) collective-permute-start(f32[3,1,450]{2,0,1:T(4,128)S(1)} %get-tuple-element.401), channel_id=1, source_target_pairs={{0,1},{1,2},{2,3},{3,4},{4,5},{5,6},{6,7},{7,8},{8,9},{9,10},{10,1... | collective-permute-start | bytes 16208 | tf_op jit(solution)/shard_map/while/body/eval_jaxpr/ppermute | solution.py:25
  130.5 10.8 %collective-permute-start.2 = (f32[3,192,1]{2,1,0:T(8,128)S(1)}, f32[3,192,1]{2,1,0:T(8,128)S(1)}, u32[]{:S(2)}, u32[]{:S(2)}) collective-permute-start(f32[3,192,1]{2,1,0:T(8,128)S(1)} %get-tuple-element.396), channel_id=1, source_target_pairs={{0,16},{16,32},{32,48},{48,64},{64,80},{80,96},{96,112},{112,128},... | collective-permute-start | bytes 6920 | tf_op jit(solution)/shard_map/while/body/eval_jaxpr/ppermute | solution.py:25
  134.5 9.3 %collective-permute-start.3 = (f32[3,192,1]{2,1,0:T(8,128)S(1)}, f32[3,192,1]{2,1,0:T(8,128)S(1)}, u32[]{:S(2)}, u32[]{:S(2)}) collective-permute-start(f32[3,192,1]{2,1,0:T(8,128)S(1)} %get-tuple-element.397), channel_id=1, source_target_pairs={{16,0},{32,16},{48,32},{64,48},{80,64},{96,80},{112,96},{128,112},... | collective-permute-start | bytes 6920 | tf_op jit(solution)/shard_map/while/body/eval_jaxpr/ppermute | solution.py:26
  146.2 1.3 copy-start
  154.6 11.2 %all-to-all-start = ((f32[16,1,4680]{2,1,0:T(1,128)}), f32[16,1,4680]{2,1,0:T(1,128)}, u32[]{:S(2)}, u32[]{:S(2)}) async-start(f32[16,1,4680]{2,1,0:T(1,128)} %reshape.306), calls=%async_computation | async-start | bytes 606208 | tf_op jit(solution)/shard_map/while/body/eval_jaxpr/all_to_all | solution.py:73
  170.0 5.0 %copy-start.6 = (s32[192]{0:T(256)S(1)}, s32[192]{0:T(256)}, u32[]{:S(2)}) copy-start(s32[192]{0:T(256)} %pad_dynamic-slice_fusion.2) | copy-start | bytes 2308 | tf_op jit(solution)/shard_map/while
  170.0 5.0 %copy-start.12 = (f32[65]{0:T(128)S(1)}, f32[65]{0:T(128)}, u32[]{:S(2)}) copy-start(f32[65]{0:T(128)} %get-tuple-element.406) | copy-start | bytes 784 | tf_op jit(solution)/shard_map/while
  171.2 12.7 %all-to-all-start.1 = ((f32[16,1,6606]{2,1,0:T(1,128)}), f32[16,1,6606]{2,1,0:T(1,128)S(1)}, u32[]{:S(2)}, u32[]{:S(2)}) async-start(f32[16,1,6606]{2,1,0:T(1,128)} %all_to_all.48), calls=%async_computation.1 | async-start | bytes 851968 | tf_op jit(solution)/shard_map/while/body/eval_jaxpr/all_to_all | solution.py:81
  185.6 2.2 %copy-start.2 = (f32[192,130]{1,0:T(8,128)S(1)}, f32[192,130]{1,0:T(8,128)}, u32[]{:S(2)}) copy-start(f32[192,130]{1,0:T(8,128)} %pad_maximum_fusion.40) | copy-start | bytes 299524 | tf_op jit(solution)/shard_map/while
  186.6 1.3 copy-start.11
  187.8 1.0 copy-start.3
  190.7 1.0 copy-start.1
  190.7 1.9 copy-start.5
  190.7 1.9 copy-start.8
  190.7 1.9 copy-start.10

commit v3 on v1

--- a/solution.py
+++ b/solution.py
@@ -86,7 +86,7 @@
     scaled = coeffs * weights[None]
     if not with_halos:
         smooth = expand(scaled, table)
-        return jnp.where(active[None, :, None], smooth, fields), None
+        return jnp.where(active[None, :, None], smooth, fields), None, None
     wide = expand(scaled, wide_table)
     smooth = wide[:, :, 1:-1]
     filtered = jnp.where(active[None, :, None], smooth, fields)
@@ -97,9 +97,9 @@
     far_raw = rows_far[(lon_index + devices // 2) % devices]
     west = jnp.where(active[None, :], wide[:, :, 0], west_raw)[:, :, None]
     east = jnp.where(active[None, :], wide[:, :, -1], east_raw)[:, :, None]
-    far_smooth = expand(scaled[:, :1, :] * half_turn_signs()[None, None, :], table)[:, 0, :]
-    far = jnp.where(active[0], far_smooth, far_raw)
-    return filtered, (west, east, far)
+    far_wide = expand(scaled[:, :2, :] * half_turn_signs()[None, None, :], wide_table)
+    far = jnp.where(active[0], far_wide[:, 0, 1:-1], far_raw)
+    return filtered, (west, east, far), (far_wide, wide[:, 0, :])
 
 
 def filter_state(state, cutoffs, table, wide_table, with_halos):
@@ -113,7 +113,51 @@
     return low_pass(state, cut_rows, global_rows < filtered_rows, table, wide_table, with_halos)
 
 
-def tendency(state, cos_all, sinlat, lon_step, lat_step, lon_halos=None):
+def rates(ext, cos_all, sinlat, lon_step, lat_step):
+    east_side = ext[:, 1:-1, 2:]
+    west_side = ext[:, 1:-1, :-2]
+    north_side = ext[:, :-2, 1:-1]
+    south_side = ext[:, 2:, 1:-1]
+    cos_north = cos_all[:-2][:, None]
+    cos_south = cos_all[2:][:, None]
+    coslat = cos_all[1:-1][:, None]
+    sinlat = sinlat[:, None]
+
+    def zonal_pair(east_value, west_value):
+        return (east_value - west_value) * (0.5 / lon_step)
+
+    def north_pair(north_value, south_value):
+        return (north_value - south_value) * (0.5 / lat_step)
+
+    centre = ext[:, 1:-1, 1:-1]
+    height, east, north = (centre[0], centre[1], centre[2])
+    inv_cos = 1.0 / coslat
+    turning = 2.0 * OMEGA_RATE * sinlat + east * sinlat * inv_cos
+    flux_north = north_side[0] * north_side[2] * cos_north
+    flux_south = south_side[0] * south_side[2] * cos_south
+    rate_height = (
+        -(
+            zonal_pair(east_side[0] * east_side[1], west_side[0] * west_side[1])
+            + north_pair(flux_north, flux_south)
+        )
+        * inv_cos
+    )
+    rate_east = (
+        -east * zonal_pair(east_side[1], west_side[1]) * inv_cos
+        - north * north_pair(north_side[1], south_side[1])
+        + turning * north
+        - zonal_pair(east_side[0], west_side[0]) * inv_cos
+    )
+    rate_north = (
+        -east * zonal_pair(east_side[2], west_side[2]) * inv_cos
+        - north * north_pair(north_side[2], south_side[2])
+        - turning * east
+        - north_pair(north_side[0], south_side[0])
+    )
+    return jnp.stack([rate_height, rate_east, rate_north], axis=0)
+
+
+def tendency(state, cos_all, sinlat, lon_step, lat_step, lon_halos=None, far=None):
     lat_index = lax.axis_index("lat")
     lat_count = lax.axis_size("lat")
     flips = jnp.array([1.0, -1.0, -1.0], jnp.float32)
@@ -122,7 +166,10 @@
         got_cols = with_halo(edge_cols, (("lon", 2),), 1, True)
         west_col = got_cols[:, :, 0:1]
         east_col = got_cols[:, :, 3:4]
-        mirror = from_behind(state[:, 0, :], "lon", lax.axis_size("lon") // 2)
+        if far is None:
+            mirror = from_behind(state[:, 0, :], "lon", lax.axis_size("lon") // 2)
+        else:
+            mirror = far
     else:
         west_col, east_col, mirror = lon_halos
     mirror = mirror * flips[:, None]
@@ -192,13 +239,21 @@
     wide_table = local_table(-1, width + 2)
     state = jnp.stack([height, east_wind, north_wind], axis=0)
     lon_halos = None
+    pole = None
+    flips = jnp.array([1.0, -1.0, -1.0], jnp.float32)[:, None]
     for step_index in range(STEPS):
-        rates = tendency(state, cos_all, sinlat, lon_step, lat_step, lon_halos)
-        middle = state + 0.5 * time_step * rates
-        rates = tendency(middle, cos_all, sinlat, lon_step, lat_step)
-        advanced = state + time_step * rates
+        rates_now = tendency(state, cos_all, sinlat, lon_step, lat_step, lon_halos)
+        middle = state + 0.5 * time_step * rates_now
+        far = None
+        if pole is not None:
+            far_wide, near_row = pole
+            far_box = jnp.stack([near_row * flips, far_wide[:, 0, :], far_wide[:, 1, :]], axis=1)
+            far_rate = rates(far_box, cos_all[0:3], sin_all[1:2], lon_step, lat_step)[:, 0, :]
+            far = far_wide[:, 0, 1:-1] + 0.5 * time_step * far_rate
+        rates_now = tendency(middle, cos_all, sinlat, lon_step, lat_step, None, far)
+        advanced = state + time_step * rates_now
         last = step_index == STEPS - 1
-        state, lon_halos = filter_state(advanced, cutoffs, table, wide_table, not last)
+        state, lon_halos, pole = filter_state(advanced, cutoffs, table, wide_table, not last)
     return (state[0], state[1], state[2])
 
 

time: 169 us -> 164 us (0.970)
  waiting for transfers between devices: 36.7 us -> 31.1 us
  starting transfers between devices: 53.3 us -> 49.1 us
  other arithmetic: 22.5 us -> 24.3 us
  blocking collectives: 22.7 us -> 24.5 us
    ppermute x7, starting transfers between devices: 28.2 us -> 21.8 us  [with_halo(): after = lax.ppermute(first, axis, down)]
    ppermute x7, starting transfers between devices: 10.3 us -> 13.6 us  [with_halo(): before = lax.ppermute(last, axis, up)]
    ppermute x7, waiting for transfers between devices: 9.1 us -> 7.06 us  [with_halo(): after = lax.ppermute(first, axis, down)]
    ppermute x7, waiting for transfers between devices: 13.2 us -> 11.4 us  [with_halo(): before = lax.ppermute(last, axis, up)]
    all_to_all x1, blocking collectives: 12 us -> 13.8 us  [low_pass(): lax.all_to_all(partial, 'lon', split_axis=1, concat_axis=0, tiled=True)]
    all_to_all x1, waiting for transfers between devices: 6.9 us -> 5.21 us  [low_pass(): lax.all_to_all(jnp.concatenate(payload, axis=1), 'lon', split_axis=0, con...]
    ppermute x3 -> x2, starting transfers between devices: 4.52 us -> 2.96 us  [from_behind(): lax.ppermute(value, axis, [(i, (i + by) % devices) for i in range(devices)])]
    unnamed x76 -> x99, local copies, waits for them, and re-layouts: 8.49 us -> 7.14 us
  transfers between devices with their start and end apart: 19 -> 18, of which waited for: 10 -> 10; matrix products, arithmetic and copies ran while one was open for 5% -> 7% of each run, Pallas kernels for 0% -> 0%
where the time goes in v3:
time: 164 us; the launch traced here: 163 us
  starting transfers between devices  49.1 us (30%)
  waiting for transfers between devices  31.1 us (19%)
  blocking collectives  24.5 us (15%)
  other arithmetic  24.3 us (15%)
  local copies, waits for them, and re-layouts  22.8 us (14%)
  matrix products  8.04 us (5%)
  between operations  2.95 us (2%)
    ppermute x7, starting transfers between devices, with_halo(): after = lax.ppermute(first, axis, down)  21.8 us
    all_to_all x1, blocking collectives, low_pass(): lax.all_to_all(partial, 'lon', split_axis=1, concat_axis=0, tiled=True)  13.8 us
    ppermute x7, starting transfers between devices, with_halo(): before = lax.ppermute(last, axis, up)  13.6 us
    ppermute x7, waiting for transfers between devices, with_halo(): before = lax.ppermute(last, axis, up)  11.4 us
    all_to_all x1, blocking collectives, low_pass(): lax.all_to_all(jnp.concatenate(payload, axis=1), 'lon', split_axis=0, con...  10.7 us
    all_to_all x1, waiting for transfers between devices, low_pass(): lax.all_to_all(partial, 'lon', split_axis=1, concat_axis=0, tiled=True)  7.45 us
    unnamed x99, local copies, waits for them, and re-layouts  7.14 us
    ppermute x7, waiting for transfers between devices, with_halo(): after = lax.ppermute(first, axis, down)  7.06 us
  transfers between devices with their start and end apart: 18, of which 10 were waited for; matrix products, arithmetic and copies ran while one was open for 7% of the time, Pallas kernels for 0%

profile of v3, /device:TPU:17, one launch (start us, length us, event | category | flops | bytes accessed | tf_op | source)
XLA Modules:
  0.0 162.8 jit_solution(11849505077857025039)
XLA Ops:
  0.6 1.3 pad_maximum_fusion.4
  2.0 7.4 %collective-permute-start.4 = (f32[3,1,450]{2,0,1:T(4,128)S(1)}, f32[3,1,450]{2,0,1:T(4,128)S(1)}, u32[]{:S(2)}, u32[]{:S(2)}) collective-permute-start(f32[3,1,450]{2,0,1:T(4,128)S(1)} %copy.237), channel_id=1, source_target_pairs={{1,0},{2,1},{3,2},{4,3},{5,4},{6,5},{7,6},{8,7},{9,8},{10,9},{11,1... | collective-permute-start | bytes 16208 | tf_op jit(solution)/shard_map/ppermute | solution.py:26
  9.4 2.8 %collective-permute-start.2 = (f32[3,450]{1,0:T(4,128)S(1)}, f32[3,450]{1,0:T(4,128)S(1)}, u32[]{:S(2)}, u32[]{:S(2)}) collective-permute-start(f32[3,450]{1,0:T(4,128)S(1)} %bitcast.208), channel_id=1, source_target_pairs={{0,128},{16,144},{32,160},{48,176},{64,192},{80,208},{96,224},{112... | collective-permute-start | bytes 16208 | tf_op jit(solution)/shard_map/ppermute | solution.py:33
  12.4 1.3 collective-permute-start
  13.7 1.9 %collective-permute-start.1 = (f32[3,192,1]{2,1,0:T(8,128)S(1)}, f32[3,192,1]{2,1,0:T(8,128)S(1)}, u32[]{:S(2)}, u32[]{:S(2)}) collective-permute-start(f32[3,192,1]{2,1,0:T(8,128)S(1)} %get-tuple-element.32), channel_id=1, source_target_pairs={{0,16},{16,32},{32,48},{48,64},{64,80},{80,96},{96,112},{112,128},... | collective-permute-start | bytes 6920 | tf_op jit(solution)/shard_map/ppermute | solution.py:25
  17.5 1.9 %collective-permute-start.3 = (f32[3,1,450]{2,0,1:T(4,128)S(1)}, f32[3,1,450]{2,0,1:T(4,128)S(1)}, u32[]{:S(2)}, u32[]{:S(2)}) collective-permute-start(f32[3,1,450]{2,0,1:T(4,128)S(1)} %get-tuple-element.45), channel_id=1, source_target_pairs={{0,1},{1,2},{2,3},{3,4},{4,5},{5,6},{6,7},{7,8},{8,9},{9,10},{10,1... | collective-permute-start | bytes 16208 | tf_op jit(solution)/shard_map/ppermute | solution.py:25
  19.4 3.9 %collective-permute-done = f32[3,192,1]{2,1,0:T(8,128)S(1)} collective-permute-done((f32[3,192,1]{2,1,0:T(8,128)S(1)}, f32[3,192,1]{2,1,0:T(8,128)S(1)}, u32[]{:S(2)}, u32[]{:S(2)}) %collective-permute-start) | collective-permute-done | bytes 2336 | tf_op jit(solution)/shard_map/ppermute | solution.py:26
  23.8 1.9 %collective-permute-done.3 = f32[3,1,450]{2,0,1:T(4,128)S(1)} collective-permute-done((f32[3,1,450]{2,0,1:T(4,128)S(1)}, f32[3,1,450]{2,0,1:T(4,128)S(1)}, u32[]{:S(2)}, u32[]{:S(2)}) %collective-permute-start.3) | collective-permute-done | bytes 5432 | tf_op jit(solution)/shard_map/ppermute | solution.py:25
  27.7 1.9 %collective-permute-start.9 = (f32[3,1,450]{2,0,1:T(4,128)S(1)}, f32[3,1,450]{2,0,1:T(4,128)S(1)}, u32[]{:S(2)}, u32[]{:S(2)}) collective-permute-start(f32[3,1,450]{2,0,1:T(4,128)S(1)} %copy.238), channel_id=1, source_target_pairs={{1,0},{2,1},{3,2},{4,3},{5,4},{6,5},{7,6},{8,7},{9,8},{10,9},{11,1... | collective-permute-start | bytes 16208 | tf_op jit(solution)/shard_map/ppermute | solution.py:26
  29.9 2.4 %collective-permute-start.5 = (f32[3,192,1]{2,1,0:T(8,128)S(1)}, f32[3,192,1]{2,1,0:T(8,128)S(1)}, u32[]{:S(2)}, u32[]{:S(2)}) collective-permute-start(f32[3,192,1]{2,1,0:T(8,128)S(1)} %get-tuple-element.25), channel_id=1, source_target_pairs={{16,0},{32,16},{48,32},{64,48},{80,64},{96,80},{112,96},{128,112},... | collective-permute-start | bytes 6920 | tf_op jit(solution)/shard_map/ppermute | solution.py:26
  32.4 3.7 %collective-permute-start.8 = (f32[3,1,450]{2,0,1:T(4,128)S(1)}, f32[3,1,450]{2,0,1:T(4,128)S(1)}, u32[]{:S(2)}, u32[]{:S(2)}) collective-permute-start(f32[3,1,450]{2,0,1:T(4,128)S(1)} %get-tuple-element.40), channel_id=1, source_target_pairs={{0,1},{1,2},{2,3},{3,4},{4,5},{5,6},{6,7},{7,8},{8,9},{9,10},{10,1... | collective-permute-start | bytes 16208 | tf_op jit(solution)/shard_map/ppermute | solution.py:25
  36.2 4.2 %collective-permute-done.8 = f32[3,1,450]{2,0,1:T(4,128)S(1)} collective-permute-done((f32[3,1,450]{2,0,1:T(4,128)S(1)}, f32[3,1,450]{2,0,1:T(4,128)S(1)}, u32[]{:S(2)}, u32[]{:S(2)}) %collective-permute-start.8) | collective-permute-done | bytes 5432 | tf_op jit(solution)/shard_map/ppermute | solution.py:25
  41.1 0.9 fusion.78
  44.8 2.1 %fusion.84 = f32[3,192,130]{1,2,0:T(8,128)} fusion(f32[3,192,450]{2,1,0:T(8,128)S(1)} %fusion.3, f32[65,450]{1,0:T(8,128)S(1)} %get-tuple-element.54, f32[65,450]{1,0:T(8,128)S(1)} %get-tuple-element.53), kind=kOutput, calls=%fused_computation.188 | convolution fusion | flops 404410496 | bytes 1570320 | tf_op jit(solution)/shard_map/fnw,kw->fnk/dot_general | solution.py:59
  46.9 1.4 copy.156
  48.3 1.7 %reshape.465 = f32[16,1,4680]{2,1,0:T(1,128)} reshape(f32[192,3,130]{2,1,0:T(4,128)S(1)} %bitcast.198) | data formatting | bytes 599040
  50.0 6.9 %all-to-all-start = ((f32[16,1,4680]{2,1,0:T(1,128)}), f32[16,1,4680]{2,1,0:T(1,128)S(1)}, u32[]{:S(2)}, u32[]{:S(2)}) async-start(f32[16,1,4680]{2,1,0:T(1,128)} %reshape.465), calls=%async_computation | async-start | bytes 606208 | tf_op jit(solution)/shard_map/all_to_all | solution.py:73
  57.3 7.4 %all-to-all-done = f32[16,1,4680]{2,1,0:T(1,128)S(1)} async-done(((f32[16,1,4680]{2,1,0:T(1,128)}), f32[16,1,4680]{2,1,0:T(1,128)S(1)}, u32[]{:S(2)}, u32[]{:S(2)}) %all-to-all-start) | async-done | bytes 299552 | tf_op jit(solution)/shard_map/all_to_all | solution.py:73
  65.3 1.3 reduce.11
  66.5 0.9 reshape.466
  67.9 1.1 all_to_all.32
  69.0 3.8 %all-to-all-start.1 = ((f32[16,1,6606]{2,1,0:T(1,128)}), f32[16,1,6606]{2,1,0:T(1,128)S(1)}, u32[]{:S(2)}, u32[]{:S(2)}) async-start(f32[16,1,6606]{2,1,0:T(1,128)} %all_to_all.32), calls=%async_computation.1 | async-start | bytes 851968 | tf_op jit(solution)/shard_map/all_to_all | solution.py:81
  75.1 1.3 fusion.92
  76.5 5.2 %all-to-all-done.1 = f32[16,1,6606]{2,1,0:T(1,128)S(1)} async-done(((f32[16,1,6606]{2,1,0:T(1,128)}), f32[16,1,6606]{2,1,0:T(1,128)S(1)}, u32[]{:S(2)}, u32[]{:S(2)}) %all-to-all-start.1) | async-done | bytes 422816 | tf_op jit(solution)/shard_map/all_to_all | solution.py:81
  85.0 1.1 fusion.82
  87.7 1.9 %collective-permute-start.11 = (f32[3,1,450]{2,0,1:T(4,128)S(1)}, f32[3,1,450]{2,0,1:T(4,128)S(1)}, u32[]{:S(2)}, u32[]{:S(2)}) collective-permute-start(f32[3,1,450]{2,0,1:T(4,128)S(1)} %copy.206), channel_id=1, source_target_pairs={{1,0},{2,1},{3,2},{4,3},{5,4},{6,5},{7,6},{8,7},{9,8},{10,9},{11,1... | collective-permute-start | bytes 16208 | tf_op jit(solution)/shard_map/ppermute | solution.py:26
  92.1 3.4 %collective-permute-start.10 = (f32[3,1,450]{2,0,1:T(4,128)S(1)}, f32[3,1,450]{2,0,1:T(4,128)S(1)}, u32[]{:S(2)}, u32[]{:S(2)}) collective-permute-start(f32[3,1,450]{2,0,1:T(4,128)S(1)} %get-tuple-element.38), channel_id=1, source_target_pairs={{0,1},{1,2},{2,3},{3,4},{4,5},{5,6},{6,7},{7,8},{8,9},{9,10},{10,1... | collective-permute-start | bytes 16208 | tf_op jit(solution)/shard_map/ppermute | solution.py:25
  96.1 1.0 slice.634
  97.3 2.8 %collective-permute-done.10 = f32[3,1,450]{2,0,1:T(4,128)S(1)} collective-permute-done((f32[3,1,450]{2,0,1:T(4,128)S(1)}, f32[3,1,450]{2,0,1:T(4,128)S(1)}, u32[]{:S(2)}, u32[]{:S(2)}) %collective-permute-start.10) | collective-permute-done | bytes 5432 | tf_op jit(solution)/shard_map/ppermute | solution.py:25
  103.0 2.7 %collective-permute-start.15 = (f32[3,1,450]{2,1,0:T(1,128)S(1)}, f32[3,1,450]{2,1,0:T(1,128)S(1)}, u32[]{:S(2)}, u32[]{:S(2)}) collective-permute-start(f32[3,1,450]{2,1,0:T(1,128)S(1)} %slice.667), channel_id=1, source_target_pairs={{1,0},{2,1},{3,2},{4,3},{5,4},{6,5},{7,6},{8,7},{9,8},{10,9},{11,1... | collective-permute-start | bytes 16208 | tf_op jit(solution)/shard_map/ppermute | solution.py:26
  105.7 1.4 fusion.112
  107.4 2.3 %collective-permute-start.14 = (f32[3,1,450]{2,1,0:T(1,128)S(1)}, f32[3,1,450]{2,1,0:T(1,128)S(1)}, u32[]{:S(2)}, u32[]{:S(2)}) collective-permute-start(f32[3,1,450]{2,1,0:T(1,128)S(1)} %get-tuple-element.18), channel_id=1, source_target_pairs={{0,1},{1,2},{2,3},{3,4},{4,5},{5,6},{6,7},{7,8},{8,9},{9,10},{10,1... | collective-permute-start | bytes 16208 | tf_op jit(solution)/shard_map/ppermute | solution.py:25
  109.9 4.2 %collective-permute-start.12 = (f32[3,192,1]{2,1,0:T(8,128)S(1)}, f32[3,192,1]{2,1,0:T(8,128)S(1)}, u32[]{:S(2)}, u32[]{:S(2)}) collective-permute-start(f32[3,192,1]{2,1,0:T(8,128)S(1)} %get-tuple-element.19), channel_id=1, source_target_pairs={{16,0},{32,16},{48,32},{64,48},{80,64},{96,80},{112,96},{128,112},... | collective-permute-start | bytes 6920 | tf_op jit(solution)/shard_map/ppermute | solution.py:26
  114.3 1.0 collective-permute-done.14
  115.4 3.0 %collective-permute-done.12 = f32[3,192,1]{2,1,0:T(8,128)S(1)} collective-permute-done((f32[3,192,1]{2,1,0:T(8,128)S(1)}, f32[3,192,1]{2,1,0:T(8,128)S(1)}, u32[]{:S(2)}, u32[]{:S(2)}) %collective-permute-start.12) | collective-permute-done | bytes 2336 | tf_op jit(solution)/shard_map/ppermute | solution.py:26
  118.4 1.5 collective-permute-done.13
  120.4 0.9 fusion.76
  123.2 2.2 %fusion.83 = f32[3,192,130]{1,2,0:T(8,128)} fusion(f32[65,450]{1,0:T(8,128)S(1)} %copy-done.12, f32[65,450]{1,0:T(8,128)S(1)} %copy-done.10, f32[3,192,450]{2,1,0:T(8,128)S(1)} %slice_select_fusion, f32[1,192,450]{2,1,0:T(8,128)S(1)} %fusion.25, f32[1,192,450]{2,1,0:T(8,128)S(1)} %fusion.32, f32[1,192,450]{2,1,0:T(8,128)S(1)} %fusion.76), kind=kOutput, calls=%fused_computation.187 | convolution fusion | flops 405447296 | bytes 2607120 | tf_op jit(solution)/shard_map/fnw,kw->fnk/dot_general | solution.py:59
  125.4 1.4 copy.190
  126.8 1.0 reshape.467
  127.8 13.8 %all_to_all.42 = f32[16,1,4680]{2,1,0:T(1,128)S(1)} all-to-all(f32[16,1,4680]{2,1,0:T(1,128)S(1)} %reshape.467), channel_id=1, replica_groups=mesh['lon'=16,'lat'=16] {'lon'}, dimensions={0} | all-to-all | bytes 599040 | tf_op jit(solution)/shard_map/all_to_all | solution.py:73
  141.5 1.3 reduce.12
  142.8 0.9 reshape.468
  144.2 10.7 %all_to_all.43 = f32[16,1,4680]{2,1,0:T(1,128)S(1)} all-to-all(f32[16,1,4680]{2,1,0:T(1,128)S(1)} %broadcast_in_dim.159), channel_id=1, replica_groups=mesh['lon'=16,'lat'=16] {'lon'}, dimensions={0} | all-to-all | bytes 599040 | tf_op jit(solution)/shard_map/all_to_all | solution.py:81
  156.3 1.0 copy.192
  157.3 2.0 %reshape.458 = f32[3,192,130]{2,1,0:T(8,128)} reshape(f32[3,16,12,130]{3,2,1,0:T(8,128)} %copy.192) | data formatting | bytes 599040 | tf_op jit(solution)/shard_map/reshape | solution.py:84
  159.3 2.4 %convolution_select_fusion = f32[3,192,450]{2,1,0:T(8,128)S(1)} fusion(f32[3,192,130]{2,1,0:T(8,128)} %reshape.458, pred[192]{0:T(512)(128)(4,1)S(1)} %copy-done.43, f32[192,130]{1,0:T(8,128)} %copy-done.13, f32[65,450]{1,0:T(8,128)} %copy-done.11, f32[65,450]{1,0:T(8,128)} %copy-done.9, f32[3,192,450]{2,1,0:T(8,128)S(1)} %slice_select_fusion, ...), kind=kOutput, calls=%fused_computation.16 | convolution fusion | flops 405781376 | bytes 3743952 | tf_op jit(solution)/shard_map/fnk,kw->fnw/dot_general | solution.py:63
  161.7 1.0 slice_bitcast_fusion
  (198 shorter events, 26.4 us)
Async XLA Ops:
  2.0 15.3 %copy-start.44 = (s32[512]{0:T(512)S(1)}, s32[512]{0:T(512)}, u32[]{:S(2)}) copy-start(s32[512]{0:T(512)} %param.12) | copy-start | bytes 6148
  2.0 21.3 %copy-start = (f32[192,450]{1,0:T(8,128)S(1)}, f32[192,450]{1,0:T(8,128)}, u32[]{:S(2)}) copy-start(f32[192,450]{1,0:T(8,128)} %param.11) | copy-start | bytes 1036804
  2.0 21.3 %copy-start.1 = (f32[192,450]{1,0:T(8,128)S(1)}, f32[192,450]{1,0:T(8,128)}, u32[]{:S(2)}) copy-start(f32[192,450]{1,0:T(8,128)} %param.10) | copy-start | bytes 1036804
  2.0 21.3 %copy-start.2 = (f32[192,450]{1,0:T(8,128)S(1)}, f32[192,450]{1,0:T(8,128)}, u32[]{:S(2)}) copy-start(f32[192,450]{1,0:T(8,128)} %param.9) | copy-start | bytes 1036804
  2.0 15.4 %collective-permute-start.4 = (f32[3,1,450]{2,0,1:T(4,128)S(1)}, f32[3,1,450]{2,0,1:T(4,128)S(1)}, u32[]{:S(2)}, u32[]{:S(2)}) collective-permute-start(f32[3,1,450]{2,0,1:T(4,128)S(1)} %copy.237), channel_id=1, source_target_pairs={{1,0},{2,1},{3,2},{4,3},{5,4},{6,5},{7,6},{8,7},{9,8},{10,9},{11,1... | collective-permute-start | bytes 16208 | tf_op jit(solution)/shard_map/ppermute | solution.py:26
  9.4 14.4 %collective-permute-start.2 = (f32[3,450]{1,0:T(4,128)S(1)}, f32[3,450]{1,0:T(4,128)S(1)}, u32[]{:S(2)}, u32[]{:S(2)}) collective-permute-start(f32[3,450]{1,0:T(4,128)S(1)} %bitcast.208), channel_id=1, source_target_pairs={{0,128},{16,144},{32,160},{48,176},{64,192},{80,208},{96,224},{112... | collective-permute-start | bytes 16208 | tf_op jit(solution)/shard_map/ppermute | solution.py:33
  12.4 10.9 %collective-permute-start = (f32[3,192,1]{2,1,0:T(8,128)S(1)}, f32[3,192,1]{2,1,0:T(8,128)S(1)}, u32[]{:S(2)}, u32[]{:S(2)}) collective-permute-start(f32[3,192,1]{2,1,0:T(8,128)S(1)} %get-tuple-element.31), channel_id=1, source_target_pairs={{16,0},{32,16},{48,32},{64,48},{80,64},{96,80},{112,96},{128,112},... | collective-permute-start | bytes 6920 | tf_op jit(solution)/shard_map/ppermute | solution.py:26
  13.7 9.5 %collective-permute-start.1 = (f32[3,192,1]{2,1,0:T(8,128)S(1)}, f32[3,192,1]{2,1,0:T(8,128)S(1)}, u32[]{:S(2)}, u32[]{:S(2)}) collective-permute-start(f32[3,192,1]{2,1,0:T(8,128)S(1)} %get-tuple-element.32), channel_id=1, source_target_pairs={{0,16},{16,32},{32,48},{48,64},{64,80},{80,96},{96,112},{112,128},... | collective-permute-start | bytes 6920 | tf_op jit(solution)/shard_map/ppermute | solution.py:25
  15.7 25.3 %copy-start.32 = (f32[192]{0:T(256)}, f32[192]{0:T(256)S(1)}, u32[]{:S(2)}) copy-start(f32[192]{0:T(256)S(1)} %get-tuple-element.60) | copy-start | bytes 2308
  15.7 25.3 %copy-start.35 = (f32[192]{0:T(256)}, f32[192]{0:T(256)S(1)}, u32[]{:S(2)}) copy-start(f32[192]{0:T(256)S(1)} %get-tuple-element.61) | copy-start | bytes 2308
  15.8 26.3 %copy-start.30 = (f32[192]{0:T(256)}, f32[192]{0:T(256)S(1)}, u32[]{:S(2)}) copy-start(f32[192]{0:T(256)S(1)} %get-tuple-element.10) | copy-start | bytes 2308
  15.8 27.1 %copy-start.17 = (f32[192]{0:T(256)}, f32[192]{0:T(256)S(1)}, u32[]{:S(2)}) copy-start(f32[192]{0:T(256)S(1)} %get-tuple-element.11) | copy-start | bytes 2308
  16.5 26.4 %copy-start.20 = (f32[192]{0:T(256)}, f32[192]{0:T(256)S(1)}, u32[]{:S(2)}) copy-start(f32[192]{0:T(256)S(1)} %get-tuple-element.58) | copy-start | bytes 2308
  16.5 26.4 %copy-start.22 = (f32[192]{0:T(256)}, f32[192]{0:T(256)S(1)}, u32[]{:S(2)}) copy-start(f32[192]{0:T(256)S(1)} %get-tuple-element.59) | copy-start | bytes 2308
  17.1 27.7 %copy-start.9 = (f32[65,450]{1,0:T(8,128)}, f32[65,450]{1,0:T(8,128)S(1)}, u32[]{:S(2)}) copy-start(f32[65,450]{1,0:T(8,128)S(1)} %get-tuple-element.53) | copy-start | bytes 351004
  17.1 27.7 %copy-start.11 = (f32[65,450]{1,0:T(8,128)}, f32[65,450]{1,0:T(8,128)S(1)}, u32[]{:S(2)}) copy-start(f32[65,450]{1,0:T(8,128)S(1)} %get-tuple-element.54) | copy-start | bytes 351004
  17.5 8.2 %copy-start.38 = (f32[3]{0:T(128)S(1)}, f32[3]{0:T(128)}, u32[]{:S(2)}) copy-start(f32[3]{0:T(128)} %constant.144.clone) | copy-start | bytes 40
  17.5 8.2 %collective-permute-start.3 = (f32[3,1,450]{2,0,1:T(4,128)S(1)}, f32[3,1,450]{2,0,1:T(4,128)S(1)}, u32[]{:S(2)}, u32[]{:S(2)}) collective-permute-start(f32[3,1,450]{2,0,1:T(4,128)S(1)} %get-tuple-element.45), channel_id=1, source_target_pairs={{0,1},{1,2},{2,3},{3,4},{4,5},{5,6},{6,7},{7,8},{8,9},{9,10},{10,1... | collective-permute-start | bytes 16208 | tf_op jit(solution)/shard_map/ppermute | solution.py:25
  25.8 10.4 %copy-start.28 = (f32[3,1,1]{2,0,1:T(4,128)}, f32[3,1,1]{2,0,1:T(4,128)S(1)}, u32[]{:S(2)}) copy-start(f32[3,1,1]{2,0,1:T(4,128)S(1)} %broadcast.385.clone) | copy-start | bytes 40
  27.7 4.7 %collective-permute-start.9 = (f32[3,1,450]{2,0,1:T(4,128)S(1)}, f32[3,1,450]{2,0,1:T(4,128)S(1)}, u32[]{:S(2)}, u32[]{:S(2)}) collective-permute-start(f32[3,1,450]{2,0,1:T(4,128)S(1)} %copy.238), channel_id=1, source_target_pairs={{1,0},{2,1},{3,2},{4,3},{5,4},{6,5},{7,6},{8,7},{9,8},{10,9},{11,1... | collective-permute-start | bytes 16208 | tf_op jit(solution)/shard_map/ppermute | solution.py:26
  29.8 6.4 %collective-permute-start.7 = (f32[3,450]{1,0:T(4,128)S(1)}, f32[3,450]{1,0:T(4,128)S(1)}, u32[]{:S(2)}, u32[]{:S(2)}) collective-permute-start(f32[3,450]{1,0:T(4,128)S(1)} %bitcast.209), channel_id=1, source_target_pairs={{0,128},{16,144},{32,160},{48,176},{64,192},{80,208},{96,224},{112... | collective-permute-start | bytes 16208 | tf_op jit(solution)/shard_map/ppermute | solution.py:33
  29.9 10.6 %collective-permute-start.5 = (f32[3,192,1]{2,1,0:T(8,128)S(1)}, f32[3,192,1]{2,1,0:T(8,128)S(1)}, u32[]{:S(2)}, u32[]{:S(2)}) collective-permute-start(f32[3,192,1]{2,1,0:T(8,128)S(1)} %get-tuple-element.25), channel_id=1, source_target_pairs={{16,0},{32,16},{48,32},{64,48},{80,64},{96,80},{112,96},{128,112},... | collective-permute-start | bytes 6920 | tf_op jit(solution)/shard_map/ppermute | solution.py:26
  32.3 8.3 %collective-permute-start.6 = (f32[3,192,1]{2,1,0:T(8,128)S(1)}, f32[3,192,1]{2,1,0:T(8,128)S(1)}, u32[]{:S(2)}, u32[]{:S(2)}) collective-permute-start(f32[3,192,1]{2,1,0:T(8,128)S(1)} %get-tuple-element.26), channel_id=1, source_target_pairs={{0,16},{16,32},{32,48},{48,64},{64,80},{80,96},{96,112},{112,128},... | collective-permute-start | bytes 6920 | tf_op jit(solution)/shard_map/ppermute | solution.py:25
  32.4 8.0 %collective-permute-start.8 = (f32[3,1,450]{2,0,1:T(4,128)S(1)}, f32[3,1,450]{2,0,1:T(4,128)S(1)}, u32[]{:S(2)}, u32[]{:S(2)}) collective-permute-start(f32[3,1,450]{2,0,1:T(4,128)S(1)} %get-tuple-element.40), channel_id=1, source_target_pairs={{0,1},{1,2},{2,3},{3,4},{4,5},{5,6},{6,7},{7,8},{8,9},{9,10},{10,1... | collective-permute-start | bytes 16208 | tf_op jit(solution)/shard_map/ppermute | solution.py:25
  50.0 14.7 %all-to-all-start = ((f32[16,1,4680]{2,1,0:T(1,128)}), f32[16,1,4680]{2,1,0:T(1,128)S(1)}, u32[]{:S(2)}, u32[]{:S(2)}) async-start(f32[16,1,4680]{2,1,0:T(1,128)} %reshape.465), calls=%async_computation | async-start | bytes 606208 | tf_op jit(solution)/shard_map/all_to_all | solution.py:73
  69.0 12.7 %all-to-all-start.1 = ((f32[16,1,6606]{2,1,0:T(1,128)}), f32[16,1,6606]{2,1,0:T(1,128)S(1)}, u32[]{:S(2)}, u32[]{:S(2)}) async-start(f32[16,1,6606]{2,1,0:T(1,128)} %all_to_all.32), calls=%async_computation.1 | async-start | bytes 851968 | tf_op jit(solution)/shard_map/all_to_all | solution.py:81
  75.1 8.9 %copy-start.13 = (f32[192,130]{1,0:T(8,128)}, f32[192,130]{1,0:T(8,128)S(1)}, u32[]{:S(2)}) copy-start(f32[192,130]{1,0:T(8,128)S(1)} %pad_maximum_fusion.45) | copy-start | bytes 299524
  87.6 3.8 %copy-start.26 = (f32[3,1,452]{2,1,0:T(1,128)S(1)}, f32[3,1,452]{2,1,0:T(1,128)}, u32[]{:S(2)}) copy-start(f32[3,1,452]{2,1,0:T(1,128)} %slice_multiply_fusion) | copy-start | bytes 16276
  87.6 12.5 %copy-start.39 = (f32[3]{0:T(128)S(1)}, f32[3]{0:T(128)}, u32[]{:S(2)}) copy-start(f32[3]{0:T(128)} %constant.144.clone) | copy-start | bytes 40
  87.6 12.5 %copy-start.42 = (pred[192]{0:T(512)(128)(4,1)S(1)}, pred[192]{0:T(512)(128)(4,1)}, u32[]{:S(2)}) copy-start(pred[192]{0:T(512)(128)(4,1)} %add_compare_fusion) | copy-start | bytes 580
  87.6 12.6 %copy-start.29 = (f32[3,1,1]{2,0,1:T(4,128)S(1)}, f32[3,1,1]{2,0,1:T(4,128)}, u32[]{:S(2)}) copy-start(f32[3,1,1]{2,0,1:T(4,128)} %copy-done.28) | copy-start | bytes 40
  87.6 12.7 %copy-start.18 = (f32[192]{0:T(256)S(1)}, f32[192]{0:T(256)}, u32[]{:S(2)}) copy-start(f32[192]{0:T(256)} %copy-done.17) | copy-start | bytes 2308
  87.6 12.7 %copy-start.33 = (f32[192]{0:T(256)S(1)}, f32[192]{0:T(256)}, u32[]{:S(2)}) copy-start(f32[192]{0:T(256)} %copy-done.32) | copy-start | bytes 2308
  87.7 12.7 %copy-start.36 = (f32[192]{0:T(256)S(1)}, f32[192]{0:T(256)}, u32[]{:S(2)}) copy-start(f32[192]{0:T(256)} %copy-done.35) | copy-start | bytes 2308
  87.7 4.4 %collective-permute-start.11 = (f32[3,1,450]{2,0,1:T(4,128)S(1)}, f32[3,1,450]{2,0,1:T(4,128)S(1)}, u32[]{:S(2)}, u32[]{:S(2)}) collective-permute-start(f32[3,1,450]{2,0,1:T(4,128)S(1)} %copy.206), channel_id=1, source_target_pairs={{1,0},{2,1},{3,2},{4,3},{5,4},{6,5},{7,6},{8,7},{9,8},{10,9},{11,1... | collective-permute-start | bytes 16208 | tf_op jit(solution)/shard_map/ppermute | solution.py:26
  92.1 8.0 %collective-permute-start.10 = (f32[3,1,450]{2,0,1:T(4,128)S(1)}, f32[3,1,450]{2,0,1:T(4,128)S(1)}, u32[]{:S(2)}, u32[]{:S(2)}) collective-permute-start(f32[3,1,450]{2,0,1:T(4,128)S(1)} %get-tuple-element.38), channel_id=1, source_target_pairs={{0,1},{1,2},{2,3},{3,4},{4,5},{5,6},{6,7},{7,8},{8,9},{9,10},{10,1... | collective-permute-start | bytes 16208 | tf_op jit(solution)/shard_map/ppermute | solution.py:25
  97.3 3.9 %copy-start.21 = (f32[192]{0:T(256)S(1)}, f32[192]{0:T(256)}, u32[]{:S(2)}) copy-start(f32[192]{0:T(256)} %copy-done.20) | copy-start | bytes 2308
  97.3 3.9 %copy-start.23 = (f32[192]{0:T(256)S(1)}, f32[192]{0:T(256)}, u32[]{:S(2)}) copy-start(f32[192]{0:T(256)} %copy-done.22) | copy-start | bytes 2308
  97.3 3.9 %copy-start.31 = (f32[192]{0:T(256)S(1)}, f32[192]{0:T(256)}, u32[]{:S(2)}) copy-start(f32[192]{0:T(256)} %copy-done.30) | copy-start | bytes 2308
  102.9 12.4 %copy-start.40 = (f32[3]{0:T(128)S(1)}, f32[3]{0:T(128)}, u32[]{:S(2)}) copy-start(f32[3]{0:T(128)} %constant.144.clone) | copy-start | bytes 40
  103.0 16.9 %copy-start.25 = (f32[3,1,1]{2,1,0:T(1,128)S(1)}, f32[3,1,1]{2,1,0:T(1,128)}, u32[]{:S(2)}) copy-start(f32[3,1,1]{2,1,0:T(1,128)} %copy-done.24) | copy-start | bytes 40
  103.0 4.4 %collective-permute-start.15 = (f32[3,1,450]{2,1,0:T(1,128)S(1)}, f32[3,1,450]{2,1,0:T(1,128)S(1)}, u32[]{:S(2)}, u32[]{:S(2)}) collective-permute-start(f32[3,1,450]{2,1,0:T(1,128)S(1)} %slice.667), channel_id=1, source_target_pairs={{1,0},{2,1},{3,2},{4,3},{5,4},{6,5},{7,6},{8,7},{9,8},{10,9},{11,1... | collective-permute-start | bytes 16208 | tf_op jit(solution)/shard_map/ppermute | solution.py:26
  107.4 8.0 %collective-permute-start.14 = (f32[3,1,450]{2,1,0:T(1,128)S(1)}, f32[3,1,450]{2,1,0:T(1,128)S(1)}, u32[]{:S(2)}, u32[]{:S(2)}) collective-permute-start(f32[3,1,450]{2,1,0:T(1,128)S(1)} %get-tuple-element.18), channel_id=1, source_target_pairs={{0,1},{1,2},{2,3},{3,4},{4,5},{5,6},{6,7},{7,8},{8,9},{9,10},{10,1... | collective-permute-start | bytes 16208 | tf_op jit(solution)/shard_map/ppermute | solution.py:25
  109.9 8.5 %collective-permute-start.12 = (f32[3,192,1]{2,1,0:T(8,128)S(1)}, f32[3,192,1]{2,1,0:T(8,128)S(1)}, u32[]{:S(2)}, u32[]{:S(2)}) collective-permute-start(f32[3,192,1]{2,1,0:T(8,128)S(1)} %get-tuple-element.19), channel_id=1, source_target_pairs={{16,0},{32,16},{48,32},{64,48},{80,64},{96,80},{112,96},{128,112},... | collective-permute-start | bytes 6920 | tf_op jit(solution)/shard_map/ppermute | solution.py:26
  114.0 5.9 %collective-permute-start.13 = (f32[3,192,1]{2,1,0:T(8,128)S(1)}, f32[3,192,1]{2,1,0:T(8,128)S(1)}, u32[]{:S(2)}, u32[]{:S(2)}) collective-permute-start(f32[3,192,1]{2,1,0:T(8,128)S(1)} %get-tuple-element.20), channel_id=1, source_target_pairs={{0,16},{16,32},{32,48},{48,64},{64,80},{80,96},{96,112},{112,128},... | collective-permute-start | bytes 6920 | tf_op jit(solution)/shard_map/ppermute | solution.py:25
  115.4 5.0 %copy-start.19 = (f32[192]{0:T(256)S(1)}, f32[192]{0:T(256)}, u32[]{:S(2)}) copy-start(f32[192]{0:T(256)} %copy-done.17) | copy-start | bytes 2308
  115.4 5.0 %copy-start.34 = (f32[192]{0:T(256)S(1)}, f32[192]{0:T(256)}, u32[]{:S(2)}) copy-start(f32[192]{0:T(256)} %copy-done.32) | copy-start | bytes 2308
  115.4 5.0 %copy-start.37 = (f32[192]{0:T(256)S(1)}, f32[192]{0:T(256)}, u32[]{:S(2)}) copy-start(f32[192]{0:T(256)} %copy-done.35) | copy-start | bytes 2308
  (15 other events, 22.4 us)

commit v4 on v3

--- a/solution.py
+++ b/solution.py
@@ -77,7 +77,7 @@
         targets = jnp.arange(devices, dtype=jnp.int32)[:, None]
         to_east = targets == (lon_index + 1) % devices
         edge = jnp.where(to_east, fields[:, :, -1].reshape(1, -1), fields[:, :, 0].reshape(1, -1))
-        payload += [edge, jnp.broadcast_to(fields[:, 0, :].reshape(1, -1), (devices, count * width))]
+        payload += [edge]
     spread = lax.all_to_all(jnp.concatenate(payload, axis=1), "lon", split_axis=0, concat_axis=0, tiled=True)
     block = count * share * modes
     coeffs = spread[:, :block].reshape(devices, count, share, modes)
@@ -90,15 +90,13 @@
     wide = expand(scaled, wide_table)
     smooth = wide[:, :, 1:-1]
     filtered = jnp.where(active[None, :, None], smooth, fields)
-    edges = spread[:, block:block + count * rows].reshape(devices, count, rows)
-    rows_far = spread[:, block + count * rows:].reshape(devices, count, width)
+    edges = spread[:, block:].reshape(devices, count, rows)
     west_raw = edges[(lon_index - 1) % devices]
     east_raw = edges[(lon_index + 1) % devices]
-    far_raw = rows_far[(lon_index + devices // 2) % devices]
     west = jnp.where(active[None, :], wide[:, :, 0], west_raw)[:, :, None]
     east = jnp.where(active[None, :], wide[:, :, -1], east_raw)[:, :, None]
     far_wide = expand(scaled[:, :2, :] * half_turn_signs()[None, None, :], wide_table)
-    far = jnp.where(active[0], far_wide[:, 0, 1:-1], far_raw)
+    far = far_wide[:, 0, 1:-1]
     return filtered, (west, east, far), (far_wide, wide[:, 0, :])
 
 

time: 164 us -> 166 us (1.012)
  waiting for transfers between devices: 31.1 us -> 35.8 us
  other arithmetic: 24.3 us -> 26.3 us
  blocking collectives: 24.5 us -> 22.5 us
    ppermute x7, waiting for transfers between devices: 11.4 us -> 13.7 us  [with_halo(): before = lax.ppermute(last, axis, up)]
    all_to_all x1, blocking collectives: 13.8 us -> 11.8 us  [low_pass(): lax.all_to_all(partial, 'lon', split_axis=1, concat_axis=0, tiled=True)]
    unnamed x99 -> x89, local copies, waits for them, and re-layouts: 7.14 us -> 8.09 us
  transfers between devices with their start and end apart: 18 -> 18, of which waited for: 10 -> 9; matrix products, arithmetic and copies ran while one was open for 7% -> 7% of each run, Pallas kernels for 0% -> 0%
where the time goes in v4:
time: 166 us; the launch traced here: 165 us
  starting transfers between devices  47.9 us (29%)
  waiting for transfers between devices  35.8 us (22%)
  other arithmetic  26.3 us (16%)
  local copies, waits for them, and re-layouts  22.6 us (14%)
  blocking collectives  22.5 us (14%)
  matrix products  6.8 us (4%)
  between operations  3.02 us (2%)
    ppermute x7, starting transfers between devices, with_halo(): after = lax.ppermute(first, axis, down)  20.3 us
    ppermute x7, waiting for transfers between devices, with_halo(): before = lax.ppermute(last, axis, up)  13.7 us
    ppermute x7, starting transfers between devices, with_halo(): before = lax.ppermute(last, axis, up)  13.6 us
    all_to_all x1, blocking collectives, low_pass(): lax.all_to_all(partial, 'lon', split_axis=1, concat_axis=0, tiled=True)  11.8 us
    all_to_all x1, blocking collectives, low_pass(): lax.all_to_all(jnp.concatenate(payload, axis=1), 'lon', split_axis=0, con...  10.7 us
    ppermute x7, waiting for transfers between devices, with_halo(): after = lax.ppermute(first, axis, down)  8.64 us
    unnamed x89, local copies, waits for them, and re-layouts  8.09 us
    all_to_all x1, waiting for transfers between devices, low_pass(): lax.all_to_all(partial, 'lon', split_axis=1, concat_axis=0, tiled=True)  7.13 us
  transfers between devices with their start and end apart: 18, of which 9 were waited for; matrix products, arithmetic and copies ran while one was open for 7% of the time, Pallas kernels for 0%

profile of v4, /device:TPU:17, one launch (start us, length us, event | category | flops | bytes accessed | tf_op | source)
XLA Modules:
  0.0 164.9 jit_solution(14400996199445825882)
XLA Ops:
  0.6 1.3 pad_maximum_fusion.4
  2.0 7.4 %collective-permute-start.4 = (f32[3,1,450]{2,0,1:T(4,128)S(1)}, f32[3,1,450]{2,0,1:T(4,128)S(1)}, u32[]{:S(2)}, u32[]{:S(2)}) collective-permute-start(f32[3,1,450]{2,0,1:T(4,128)S(1)} %copy.237), channel_id=1, source_target_pairs={{1,0},{2,1},{3,2},{4,3},{5,4},{6,5},{7,6},{8,7},{9,8},{10,9},{11,1... | collective-permute-start | bytes 16208 | tf_op jit(solution)/shard_map/ppermute | solution.py:26
  9.4 2.8 %collective-permute-start.2 = (f32[3,450]{1,0:T(4,128)S(1)}, f32[3,450]{1,0:T(4,128)S(1)}, u32[]{:S(2)}, u32[]{:S(2)}) collective-permute-start(f32[3,450]{1,0:T(4,128)S(1)} %bitcast.198), channel_id=1, source_target_pairs={{0,128},{16,144},{32,160},{48,176},{64,192},{80,208},{96,224},{112... | collective-permute-start | bytes 16208 | tf_op jit(solution)/shard_map/ppermute | solution.py:33
  12.4 1.3 collective-permute-start
  13.7 1.9 %collective-permute-start.1 = (f32[3,192,1]{2,1,0:T(8,128)S(1)}, f32[3,192,1]{2,1,0:T(8,128)S(1)}, u32[]{:S(2)}, u32[]{:S(2)}) collective-permute-start(f32[3,192,1]{2,1,0:T(8,128)S(1)} %get-tuple-element.32), channel_id=1, source_target_pairs={{0,16},{16,32},{32,48},{48,64},{64,80},{80,96},{96,112},{112,128},... | collective-permute-start | bytes 6920 | tf_op jit(solution)/shard_map/ppermute | solution.py:25
  19.5 1.9 %collective-permute-start.3 = (f32[3,1,450]{2,0,1:T(4,128)S(1)}, f32[3,1,450]{2,0,1:T(4,128)S(1)}, u32[]{:S(2)}, u32[]{:S(2)}) collective-permute-start(f32[3,1,450]{2,0,1:T(4,128)S(1)} %get-tuple-element.45), channel_id=1, source_target_pairs={{0,1},{1,2},{2,3},{3,4},{4,5},{5,6},{6,7},{7,8},{8,9},{9,10},{10,1... | collective-permute-start | bytes 16208 | tf_op jit(solution)/shard_map/ppermute | solution.py:25
  21.5 1.8 %collective-permute-done = f32[3,192,1]{2,1,0:T(8,128)S(1)} collective-permute-done((f32[3,192,1]{2,1,0:T(8,128)S(1)}, f32[3,192,1]{2,1,0:T(8,128)S(1)}, u32[]{:S(2)}, u32[]{:S(2)}) %collective-permute-start) | collective-permute-done | bytes 2336 | tf_op jit(solution)/shard_map/ppermute | solution.py:26
  23.8 3.9 %collective-permute-done.3 = f32[3,1,450]{2,0,1:T(4,128)S(1)} collective-permute-done((f32[3,1,450]{2,0,1:T(4,128)S(1)}, f32[3,1,450]{2,0,1:T(4,128)S(1)}, u32[]{:S(2)}, u32[]{:S(2)}) %collective-permute-start.3) | collective-permute-done | bytes 5432 | tf_op jit(solution)/shard_map/ppermute | solution.py:25
  29.7 1.9 %collective-permute-start.9 = (f32[3,1,450]{2,0,1:T(4,128)S(1)}, f32[3,1,450]{2,0,1:T(4,128)S(1)}, u32[]{:S(2)}, u32[]{:S(2)}) collective-permute-start(f32[3,1,450]{2,0,1:T(4,128)S(1)} %copy.238), channel_id=1, source_target_pairs={{1,0},{2,1},{3,2},{4,3},{5,4},{6,5},{7,6},{8,7},{9,8},{10,9},{11,1... | collective-permute-start | bytes 16208 | tf_op jit(solution)/shard_map/ppermute | solution.py:26
  32.1 2.3 %collective-permute-start.5 = (f32[3,192,1]{2,1,0:T(8,128)S(1)}, f32[3,192,1]{2,1,0:T(8,128)S(1)}, u32[]{:S(2)}, u32[]{:S(2)}) collective-permute-start(f32[3,192,1]{2,1,0:T(8,128)S(1)} %get-tuple-element.25), channel_id=1, source_target_pairs={{16,0},{32,16},{48,32},{64,48},{80,64},{96,80},{112,96},{128,112},... | collective-permute-start | bytes 6920 | tf_op jit(solution)/shard_map/ppermute | solution.py:26
  34.4 3.8 %collective-permute-start.8 = (f32[3,1,450]{2,0,1:T(4,128)S(1)}, f32[3,1,450]{2,0,1:T(4,128)S(1)}, u32[]{:S(2)}, u32[]{:S(2)}) collective-permute-start(f32[3,1,450]{2,0,1:T(4,128)S(1)} %get-tuple-element.40), channel_id=1, source_target_pairs={{0,1},{1,2},{2,3},{3,4},{4,5},{5,6},{6,7},{7,8},{8,9},{9,10},{10,1... | collective-permute-start | bytes 16208 | tf_op jit(solution)/shard_map/ppermute | solution.py:25
  38.3 4.1 %collective-permute-done.8 = f32[3,1,450]{2,0,1:T(4,128)S(1)} collective-permute-done((f32[3,1,450]{2,0,1:T(4,128)S(1)}, f32[3,1,450]{2,0,1:T(4,128)S(1)}, u32[]{:S(2)}, u32[]{:S(2)}) %collective-permute-start.8) | collective-permute-done | bytes 5432 | tf_op jit(solution)/shard_map/ppermute | solution.py:25
  43.1 0.9 fusion.78
  46.4 2.1 %fusion.84 = f32[3,192,130]{1,2,0:T(8,128)} fusion(f32[3,192,450]{2,1,0:T(8,128)S(1)} %fusion.3, f32[65,450]{1,0:T(8,128)S(1)} %get-tuple-element.54, f32[65,450]{1,0:T(8,128)S(1)} %get-tuple-element.53), kind=kOutput, calls=%fused_computation.189 | convolution fusion | flops 404410496 | bytes 1570320 | tf_op jit(solution)/shard_map/fnw,kw->fnk/dot_general | solution.py:59
  48.5 1.4 copy.156
  49.8 1.7 %reshape.459 = f32[16,1,4680]{2,1,0:T(1,128)} reshape(f32[192,3,130]{2,1,0:T(4,128)S(1)} %bitcast.190) | data formatting | bytes 599040
  51.6 7.0 %all-to-all-start = ((f32[16,1,4680]{2,1,0:T(1,128)}), f32[16,1,4680]{2,1,0:T(1,128)S(1)}, u32[]{:S(2)}, u32[]{:S(2)}) async-start(f32[16,1,4680]{2,1,0:T(1,128)} %reshape.459), calls=%async_computation | async-start | bytes 606208 | tf_op jit(solution)/shard_map/all_to_all | solution.py:73
  59.3 7.1 %all-to-all-done = f32[16,1,4680]{2,1,0:T(1,128)S(1)} async-done(((f32[16,1,4680]{2,1,0:T(1,128)}), f32[16,1,4680]{2,1,0:T(1,128)S(1)}, u32[]{:S(2)}, u32[]{:S(2)}) %all-to-all-start) | async-done | bytes 299552 | tf_op jit(solution)/shard_map/all_to_all | solution.py:73
  67.0 1.4 reduce.9
  69.7 1.0 all_to_all.32
  70.7 3.8 %all-to-all-start.1 = ((f32[16,1,5256]{2,1,0:T(1,128)}), f32[16,1,5256]{2,1,0:T(1,128)S(1)}, u32[]{:S(2)}, u32[]{:S(2)}) async-start(f32[16,1,5256]{2,1,0:T(1,128)} %all_to_all.32), calls=%async_computation.1 | async-start | bytes 688128 | tf_op jit(solution)/shard_map/all_to_all | solution.py:81
  75.0 1.3 fusion.92
  76.3 6.3 %all-to-all-done.1 = f32[16,1,5256]{2,1,0:T(1,128)S(1)} async-done(((f32[16,1,5256]{2,1,0:T(1,128)}), f32[16,1,5256]{2,1,0:T(1,128)S(1)}, u32[]{:S(2)}, u32[]{:S(2)}) %all-to-all-start.1) | async-done | bytes 336416 | tf_op jit(solution)/shard_map/all_to_all | solution.py:81
  85.2 1.1 fusion.82
  87.9 2.1 %collective-permute-start.11 = (f32[3,1,450]{2,0,1:T(4,128)S(1)}, f32[3,1,450]{2,0,1:T(4,128)S(1)}, u32[]{:S(2)}, u32[]{:S(2)}) collective-permute-start(f32[3,1,450]{2,0,1:T(4,128)S(1)} %copy.206), channel_id=1, source_target_pairs={{1,0},{2,1},{3,2},{4,3},{5,4},{6,5},{7,6},{8,7},{9,8},{10,9},{11,1... | collective-permute-start | bytes 16208 | tf_op jit(solution)/shard_map/ppermute | solution.py:26
  91.0 0.9 slice_select_fusion.2
  92.7 3.4 %collective-permute-start.10 = (f32[3,1,450]{2,0,1:T(4,128)S(1)}, f32[3,1,450]{2,0,1:T(4,128)S(1)}, u32[]{:S(2)}, u32[]{:S(2)}) collective-permute-start(f32[3,1,450]{2,0,1:T(4,128)S(1)} %get-tuple-element.38), channel_id=1, source_target_pairs={{0,1},{1,2},{2,3},{3,4},{4,5},{5,6},{6,7},{7,8},{8,9},{9,10},{10,1... | collective-permute-start | bytes 16208 | tf_op jit(solution)/shard_map/ppermute | solution.py:25
  96.8 3.9 %collective-permute-done.10 = f32[3,1,450]{2,0,1:T(4,128)S(1)} collective-permute-done((f32[3,1,450]{2,0,1:T(4,128)S(1)}, f32[3,1,450]{2,0,1:T(4,128)S(1)}, u32[]{:S(2)}, u32[]{:S(2)}) %collective-permute-start.10) | collective-permute-done | bytes 5432 | tf_op jit(solution)/shard_map/ppermute | solution.py:25
  103.6 1.9 %collective-permute-start.15 = (f32[3,1,450]{2,1,0:T(1,128)S(1)}, f32[3,1,450]{2,1,0:T(1,128)S(1)}, u32[]{:S(2)}, u32[]{:S(2)}) collective-permute-start(f32[3,1,450]{2,1,0:T(1,128)S(1)} %slice.653), channel_id=1, source_target_pairs={{1,0},{2,1},{3,2},{4,3},{5,4},{6,5},{7,6},{8,7},{9,8},{10,9},{11,1... | collective-permute-start | bytes 16208 | tf_op jit(solution)/shard_map/ppermute | solution.py:26
  105.5 1.4 fusion.110
  106.9 1.1 collective-permute-done.15
  108.0 2.3 %collective-permute-start.14 = (f32[3,1,450]{2,1,0:T(1,128)S(1)}, f32[3,1,450]{2,1,0:T(1,128)S(1)}, u32[]{:S(2)}, u32[]{:S(2)}) collective-permute-start(f32[3,1,450]{2,1,0:T(1,128)S(1)} %get-tuple-element.18), channel_id=1, source_target_pairs={{0,1},{1,2},{2,3},{3,4},{4,5},{5,6},{6,7},{7,8},{8,9},{9,10},{10,1... | collective-permute-start | bytes 16208 | tf_op jit(solution)/shard_map/ppermute | solution.py:25
  110.4 3.3 %collective-permute-start.12 = (f32[3,192,1]{2,1,0:T(8,128)S(1)}, f32[3,192,1]{2,1,0:T(8,128)S(1)}, u32[]{:S(2)}, u32[]{:S(2)}) collective-permute-start(f32[3,192,1]{2,1,0:T(8,128)S(1)} %get-tuple-element.19), channel_id=1, source_target_pairs={{16,0},{32,16},{48,32},{64,48},{80,64},{96,80},{112,96},{128,112},... | collective-permute-start | bytes 6920 | tf_op jit(solution)/shard_map/ppermute | solution.py:26
  114.1 1.9 %collective-permute-done.14 = f32[3,1,450]{2,1,0:T(1,128)S(1)} collective-permute-done((f32[3,1,450]{2,1,0:T(1,128)S(1)}, f32[3,1,450]{2,1,0:T(1,128)S(1)}, u32[]{:S(2)}, u32[]{:S(2)}) %collective-permute-start.14) | collective-permute-done | bytes 5432 | tf_op jit(solution)/shard_map/ppermute | solution.py:25
  116.0 5.7 %collective-permute-done.12 = f32[3,192,1]{2,1,0:T(8,128)S(1)} collective-permute-done((f32[3,192,1]{2,1,0:T(8,128)S(1)}, f32[3,192,1]{2,1,0:T(8,128)S(1)}, u32[]{:S(2)}, u32[]{:S(2)}) %collective-permute-start.12) | collective-permute-done | bytes 2336 | tf_op jit(solution)/shard_map/ppermute | solution.py:26
  125.0 2.2 %fusion.83 = f32[3,192,130]{1,2,0:T(8,128)} fusion(f32[65,450]{1,0:T(8,128)S(1)} %copy-done.12, f32[65,450]{1,0:T(8,128)S(1)} %copy-done.10, f32[3,192,450]{2,1,0:T(8,128)S(1)} %slice_select_fusion, f32[1,192,450]{2,1,0:T(8,128)S(1)} %fusion.25, f32[1,192,450]{2,1,0:T(8,128)S(1)} %fusion.32, f32[1,192,450]{2,1,0:T(8,128)S(1)} %fusion.76), kind=kOutput, calls=%fused_computation.188 | convolution fusion | flops 405447296 | bytes 2607120 | tf_op jit(solution)/shard_map/fnw,kw->fnk/dot_general | solution.py:59
  127.2 1.4 copy.190
  128.6 1.7 %reshape.461 = f32[16,1,4680]{2,1,0:T(1,128)} reshape(f32[192,3,130]{2,1,0:T(4,128)S(1)} %bitcast.192) | data formatting | bytes 599040
  130.3 11.8 %all_to_all.42 = f32[16,1,4680]{2,1,0:T(1,128)S(1)} all-to-all(f32[16,1,4680]{2,1,0:T(1,128)} %reshape.461), channel_id=1, replica_groups=mesh['lon'=16,'lat'=16] {'lon'}, dimensions={0} | all-to-all | bytes 599040 | tf_op jit(solution)/shard_map/all_to_all | solution.py:73
  142.1 2.1 %reduce.10 = f32[16,4680]{1,0:T(8,128)} reduce(f32[16,1,4680]{2,1,0:T(1,128)S(1)} %all_to_all.42, f32[]{:T(128)} %broadcast.433), dimensions={1}, to_apply=%all_to_all.35.reduce_sub_computation | reduce | bytes 599044 | tf_op jit(solution)/shard_map/all_to_all | solution.py:73
  144.2 1.9 %reshape.462 = f32[192,3,130]{2,1,0:T(4,128)S(1)} reshape(f32[16,4680]{1,0:T(8,128)} %reduce.10) | data formatting | bytes 599040
  146.6 10.7 %all_to_all.43 = f32[16,1,4680]{2,1,0:T(1,128)S(1)} all-to-all(f32[16,1,4680]{2,1,0:T(1,128)S(1)} %broadcast_in_dim.150), channel_id=1, replica_groups=mesh['lon'=16,'lat'=16] {'lon'}, dimensions={0} | all-to-all | bytes 599040 | tf_op jit(solution)/shard_map/all_to_all | solution.py:81
  157.3 1.5 reduce.6
  158.8 1.7 %reshape.451 = f32[16,3,12,130]{3,2,1,0:T(8,128)S(1)} reshape(f32[16,4680]{1,0:T(8,128)} %reduce.6) | data formatting | bytes 599040 | tf_op jit(solution)/shard_map/reshape | solution.py:83
  160.4 0.9 copy.192
  161.4 1.2 reshape.452
  162.7 1.2 convolution_select_fusion
  163.9 1.0 slice_bitcast_fusion
  (183 shorter events, 25.0 us)
Async XLA Ops:
  2.0 15.2 %copy-start.39 = (s32[512]{0:T(512)S(1)}, s32[512]{0:T(512)}, u32[]{:S(2)}) copy-start(s32[512]{0:T(512)} %param.12) | copy-start | bytes 6148
  2.0 21.3 %copy-start = (f32[192,450]{1,0:T(8,128)S(1)}, f32[192,450]{1,0:T(8,128)}, u32[]{:S(2)}) copy-start(f32[192,450]{1,0:T(8,128)} %param.11) | copy-start | bytes 1036804
  2.0 21.3 %copy-start.1 = (f32[192,450]{1,0:T(8,128)S(1)}, f32[192,450]{1,0:T(8,128)}, u32[]{:S(2)}) copy-start(f32[192,450]{1,0:T(8,128)} %param.10) | copy-start | bytes 1036804
  2.0 21.3 %copy-start.2 = (f32[192,450]{1,0:T(8,128)S(1)}, f32[192,450]{1,0:T(8,128)}, u32[]{:S(2)}) copy-start(f32[192,450]{1,0:T(8,128)} %param.9) | copy-start | bytes 1036804
  2.0 17.5 %collective-permute-start.4 = (f32[3,1,450]{2,0,1:T(4,128)S(1)}, f32[3,1,450]{2,0,1:T(4,128)S(1)}, u32[]{:S(2)}, u32[]{:S(2)}) collective-permute-start(f32[3,1,450]{2,0,1:T(4,128)S(1)} %copy.237), channel_id=1, source_target_pairs={{1,0},{2,1},{3,2},{4,3},{5,4},{6,5},{7,6},{8,7},{9,8},{10,9},{11,1... | collective-permute-start | bytes 16208 | tf_op jit(solution)/shard_map/ppermute | solution.py:26
  9.4 14.4 %collective-permute-start.2 = (f32[3,450]{1,0:T(4,128)S(1)}, f32[3,450]{1,0:T(4,128)S(1)}, u32[]{:S(2)}, u32[]{:S(2)}) collective-permute-start(f32[3,450]{1,0:T(4,128)S(1)} %bitcast.198), channel_id=1, source_target_pairs={{0,128},{16,144},{32,160},{48,176},{64,192},{80,208},{96,224},{112... | collective-permute-start | bytes 16208 | tf_op jit(solution)/shard_map/ppermute | solution.py:33
  12.4 10.9 %collective-permute-start = (f32[3,192,1]{2,1,0:T(8,128)S(1)}, f32[3,192,1]{2,1,0:T(8,128)S(1)}, u32[]{:S(2)}, u32[]{:S(2)}) collective-permute-start(f32[3,192,1]{2,1,0:T(8,128)S(1)} %get-tuple-element.31), channel_id=1, source_target_pairs={{16,0},{32,16},{48,32},{64,48},{80,64},{96,80},{112,96},{128,112},... | collective-permute-start | bytes 6920 | tf_op jit(solution)/shard_map/ppermute | solution.py:26
  13.7 9.5 %collective-permute-start.1 = (f32[3,192,1]{2,1,0:T(8,128)S(1)}, f32[3,192,1]{2,1,0:T(8,128)S(1)}, u32[]{:S(2)}, u32[]{:S(2)}) collective-permute-start(f32[3,192,1]{2,1,0:T(8,128)S(1)} %get-tuple-element.32), channel_id=1, source_target_pairs={{0,16},{16,32},{32,48},{48,64},{64,80},{80,96},{96,112},{112,128},... | collective-permute-start | bytes 6920 | tf_op jit(solution)/shard_map/ppermute | solution.py:25
  15.7 27.3 %copy-start.31 = (f32[192]{0:T(256)}, f32[192]{0:T(256)S(1)}, u32[]{:S(2)}) copy-start(f32[192]{0:T(256)S(1)} %get-tuple-element.60) | copy-start | bytes 2308
  15.7 27.3 %copy-start.33 = (f32[192]{0:T(256)}, f32[192]{0:T(256)S(1)}, u32[]{:S(2)}) copy-start(f32[192]{0:T(256)S(1)} %get-tuple-element.61) | copy-start | bytes 2308
  15.8 28.3 %copy-start.29 = (f32[192]{0:T(256)}, f32[192]{0:T(256)S(1)}, u32[]{:S(2)}) copy-start(f32[192]{0:T(256)S(1)} %get-tuple-element.10) | copy-start | bytes 2308
  15.8 29.1 %copy-start.17 = (f32[192]{0:T(256)}, f32[192]{0:T(256)S(1)}, u32[]{:S(2)}) copy-start(f32[192]{0:T(256)S(1)} %get-tuple-element.11) | copy-start | bytes 2308
  16.5 28.4 %copy-start.20 = (f32[192]{0:T(256)}, f32[192]{0:T(256)S(1)}, u32[]{:S(2)}) copy-start(f32[192]{0:T(256)S(1)} %get-tuple-element.58) | copy-start | bytes 2308
  16.5 28.4 %copy-start.22 = (f32[192]{0:T(256)}, f32[192]{0:T(256)S(1)}, u32[]{:S(2)}) copy-start(f32[192]{0:T(256)S(1)} %get-tuple-element.59) | copy-start | bytes 2308
  17.1 29.3 %copy-start.9 = (f32[65,450]{1,0:T(8,128)}, f32[65,450]{1,0:T(8,128)S(1)}, u32[]{:S(2)}) copy-start(f32[65,450]{1,0:T(8,128)S(1)} %get-tuple-element.53) | copy-start | bytes 351004
  17.1 29.3 %copy-start.11 = (f32[65,450]{1,0:T(8,128)}, f32[65,450]{1,0:T(8,128)S(1)}, u32[]{:S(2)}) copy-start(f32[65,450]{1,0:T(8,128)S(1)} %get-tuple-element.54) | copy-start | bytes 351004
  17.5 66.8 %copy-start.13 = (f32[192,130]{1,0:T(8,128)}, f32[192,130]{1,0:T(8,128)S(1)}, u32[]{:S(2)}) copy-start(f32[192,130]{1,0:T(8,128)S(1)} %pad_maximum_fusion.46) | copy-start | bytes 299524
  19.5 8.2 %copy-start.35 = (f32[3]{0:T(128)S(1)}, f32[3]{0:T(128)}, u32[]{:S(2)}) copy-start(f32[3]{0:T(128)} %constant.138.clone) | copy-start | bytes 40
  19.5 8.1 %collective-permute-start.3 = (f32[3,1,450]{2,0,1:T(4,128)S(1)}, f32[3,1,450]{2,0,1:T(4,128)S(1)}, u32[]{:S(2)}, u32[]{:S(2)}) collective-permute-start(f32[3,1,450]{2,0,1:T(4,128)S(1)} %get-tuple-element.45), channel_id=1, source_target_pairs={{0,1},{1,2},{2,3},{3,4},{4,5},{5,6},{6,7},{7,8},{8,9},{9,10},{10,1... | collective-permute-start | bytes 16208 | tf_op jit(solution)/shard_map/ppermute | solution.py:25
  27.8 10.5 %copy-start.27 = (f32[3,1,1]{2,0,1:T(4,128)}, f32[3,1,1]{2,0,1:T(4,128)S(1)}, u32[]{:S(2)}) copy-start(f32[3,1,1]{2,0,1:T(4,128)S(1)} %broadcast.383.clone) | copy-start | bytes 40
  29.7 4.7 %collective-permute-start.9 = (f32[3,1,450]{2,0,1:T(4,128)S(1)}, f32[3,1,450]{2,0,1:T(4,128)S(1)}, u32[]{:S(2)}, u32[]{:S(2)}) collective-permute-start(f32[3,1,450]{2,0,1:T(4,128)S(1)} %copy.238), channel_id=1, source_target_pairs={{1,0},{2,1},{3,2},{4,3},{5,4},{6,5},{7,6},{8,7},{9,8},{10,9},{11,1... | collective-permute-start | bytes 16208 | tf_op jit(solution)/shard_map/ppermute | solution.py:26
  31.8 6.5 %collective-permute-start.7 = (f32[3,450]{1,0:T(4,128)S(1)}, f32[3,450]{1,0:T(4,128)S(1)}, u32[]{:S(2)}, u32[]{:S(2)}) collective-permute-start(f32[3,450]{1,0:T(4,128)S(1)} %bitcast.199), channel_id=1, source_target_pairs={{0,128},{16,144},{32,160},{48,176},{64,192},{80,208},{96,224},{112... | collective-permute-start | bytes 16208 | tf_op jit(solution)/shard_map/ppermute | solution.py:33
  32.1 10.4 %collective-permute-start.5 = (f32[3,192,1]{2,1,0:T(8,128)S(1)}, f32[3,192,1]{2,1,0:T(8,128)S(1)}, u32[]{:S(2)}, u32[]{:S(2)}) collective-permute-start(f32[3,192,1]{2,1,0:T(8,128)S(1)} %get-tuple-element.25), channel_id=1, source_target_pairs={{16,0},{32,16},{48,32},{64,48},{80,64},{96,80},{112,96},{128,112},... | collective-permute-start | bytes 6920 | tf_op jit(solution)/shard_map/ppermute | solution.py:26
  34.4 8.1 %collective-permute-start.6 = (f32[3,192,1]{2,1,0:T(8,128)S(1)}, f32[3,192,1]{2,1,0:T(8,128)S(1)}, u32[]{:S(2)}, u32[]{:S(2)}) collective-permute-start(f32[3,192,1]{2,1,0:T(8,128)S(1)} %get-tuple-element.26), channel_id=1, source_target_pairs={{0,16},{16,32},{32,48},{48,64},{64,80},{80,96},{96,112},{112,128},... | collective-permute-start | bytes 6920 | tf_op jit(solution)/shard_map/ppermute | solution.py:25
  34.4 8.0 %collective-permute-start.8 = (f32[3,1,450]{2,0,1:T(4,128)S(1)}, f32[3,1,450]{2,0,1:T(4,128)S(1)}, u32[]{:S(2)}, u32[]{:S(2)}) collective-permute-start(f32[3,1,450]{2,0,1:T(4,128)S(1)} %get-tuple-element.40), channel_id=1, source_target_pairs={{0,1},{1,2},{2,3},{3,4},{4,5},{5,6},{6,7},{7,8},{8,9},{9,10},{10,1... | collective-permute-start | bytes 16208 | tf_op jit(solution)/shard_map/ppermute | solution.py:25
  51.6 14.8 %all-to-all-start = ((f32[16,1,4680]{2,1,0:T(1,128)}), f32[16,1,4680]{2,1,0:T(1,128)S(1)}, u32[]{:S(2)}, u32[]{:S(2)}) async-start(f32[16,1,4680]{2,1,0:T(1,128)} %reshape.459), calls=%async_computation | async-start | bytes 606208 | tf_op jit(solution)/shard_map/all_to_all | solution.py:73
  70.7 12.0 %all-to-all-start.1 = ((f32[16,1,5256]{2,1,0:T(1,128)}), f32[16,1,5256]{2,1,0:T(1,128)S(1)}, u32[]{:S(2)}, u32[]{:S(2)}) async-start(f32[16,1,5256]{2,1,0:T(1,128)} %all_to_all.32), calls=%async_computation.1 | async-start | bytes 688128 | tf_op jit(solution)/shard_map/all_to_all | solution.py:81
  85.2 2.0 %copy-start.4 = (f32[1,192,450]{2,1,0:T(8,128)S(1)}, f32[1,192,450]{2,1,0:T(8,128)}, u32[]{:S(2)}) copy-start(f32[1,192,450]{2,1,0:T(8,128)} %copy-done.3) | copy-start | bytes 1036804
  85.2 2.0 %copy-start.6 = (f32[1,192,450]{2,1,0:T(8,128)S(1)}, f32[1,192,450]{2,1,0:T(8,128)}, u32[]{:S(2)}) copy-start(f32[1,192,450]{2,1,0:T(8,128)} %copy-done.5) | copy-start | bytes 1036804
  85.2 2.1 %copy-start.8 = (f32[1,192,450]{2,1,0:T(8,128)S(1)}, f32[1,192,450]{2,1,0:T(8,128)}, u32[]{:S(2)}) copy-start(f32[1,192,450]{2,1,0:T(8,128)} %copy-done.7) | copy-start | bytes 1036804
  85.2 2.1 %copy-start.37 = (pred[192]{0:T(512)(128)(4,1)S(1)}, pred[192]{0:T(512)(128)(4,1)}, u32[]{:S(2)}) copy-start(pred[192]{0:T(512)(128)(4,1)} %add_compare_fusion) | copy-start | bytes 580
  87.8 4.1 %copy-start.26 = (f32[3,1,452]{2,1,0:T(1,128)S(1)}, f32[3,1,452]{2,1,0:T(1,128)}, u32[]{:S(2)}) copy-start(f32[3,1,452]{2,1,0:T(1,128)} %slice_multiply_fusion) | copy-start | bytes 16276
  87.8 12.9 %copy-start.36 = (f32[3]{0:T(128)S(1)}, f32[3]{0:T(128)}, u32[]{:S(2)}) copy-start(f32[3]{0:T(128)} %constant.138.clone) | copy-start | bytes 40
  87.9 13.0 %copy-start.28 = (f32[3,1,1]{2,0,1:T(4,128)S(1)}, f32[3,1,1]{2,0,1:T(4,128)}, u32[]{:S(2)}) copy-start(f32[3,1,1]{2,0,1:T(4,128)} %copy-done.27) | copy-start | bytes 40
  87.9 13.1 %copy-start.18 = (f32[192]{0:T(256)S(1)}, f32[192]{0:T(256)}, u32[]{:S(2)}) copy-start(f32[192]{0:T(256)} %copy-done.17) | copy-start | bytes 2308
  87.9 13.1 %copy-start.32 = (f32[192]{0:T(256)S(1)}, f32[192]{0:T(256)}, u32[]{:S(2)}) copy-start(f32[192]{0:T(256)} %copy-done.31) | copy-start | bytes 2308
  87.9 13.1 %copy-start.34 = (f32[192]{0:T(256)S(1)}, f32[192]{0:T(256)}, u32[]{:S(2)}) copy-start(f32[192]{0:T(256)} %copy-done.33) | copy-start | bytes 2308
  87.9 4.8 %collective-permute-start.11 = (f32[3,1,450]{2,0,1:T(4,128)S(1)}, f32[3,1,450]{2,0,1:T(4,128)S(1)}, u32[]{:S(2)}, u32[]{:S(2)}) collective-permute-start(f32[3,1,450]{2,0,1:T(4,128)S(1)} %copy.206), channel_id=1, source_target_pairs={{1,0},{2,1},{3,2},{4,3},{5,4},{6,5},{7,6},{8,7},{9,8},{10,9},{11,1... | collective-permute-start | bytes 16208 | tf_op jit(solution)/shard_map/ppermute | solution.py:26
  91.9 9.9 %copy-start.21 = (f32[192]{0:T(256)S(1)}, f32[192]{0:T(256)}, u32[]{:S(2)}) copy-start(f32[192]{0:T(256)} %copy-done.20) | copy-start | bytes 2308
  91.9 9.9 %copy-start.23 = (f32[192]{0:T(256)S(1)}, f32[192]{0:T(256)}, u32[]{:S(2)}) copy-start(f32[192]{0:T(256)} %copy-done.22) | copy-start | bytes 2308
  91.9 9.9 %copy-start.30 = (f32[192]{0:T(256)S(1)}, f32[192]{0:T(256)}, u32[]{:S(2)}) copy-start(f32[192]{0:T(256)} %copy-done.29) | copy-start | bytes 2308
  92.7 8.0 %collective-permute-start.10 = (f32[3,1,450]{2,0,1:T(4,128)S(1)}, f32[3,1,450]{2,0,1:T(4,128)S(1)}, u32[]{:S(2)}, u32[]{:S(2)}) collective-permute-start(f32[3,1,450]{2,0,1:T(4,128)S(1)} %get-tuple-element.38), channel_id=1, source_target_pairs={{0,1},{1,2},{2,3},{3,4},{4,5},{5,6},{6,7},{7,8},{8,9},{9,10},{10,1... | collective-permute-start | bytes 16208 | tf_op jit(solution)/shard_map/ppermute | solution.py:25
  103.6 18.2 %copy-start.25 = (f32[3,1,1]{2,1,0:T(1,128)S(1)}, f32[3,1,1]{2,1,0:T(1,128)}, u32[]{:S(2)}) copy-start(f32[3,1,1]{2,1,0:T(1,128)} %copy-done.24) | copy-start | bytes 40
  103.6 4.4 %collective-permute-start.15 = (f32[3,1,450]{2,1,0:T(1,128)S(1)}, f32[3,1,450]{2,1,0:T(1,128)S(1)}, u32[]{:S(2)}, u32[]{:S(2)}) collective-permute-start(f32[3,1,450]{2,1,0:T(1,128)S(1)} %slice.653), channel_id=1, source_target_pairs={{1,0},{2,1},{3,2},{4,3},{5,4},{6,5},{7,6},{8,7},{9,8},{10,9},{11,1... | collective-permute-start | bytes 16208 | tf_op jit(solution)/shard_map/ppermute | solution.py:26
  108.0 8.0 %collective-permute-start.14 = (f32[3,1,450]{2,1,0:T(1,128)S(1)}, f32[3,1,450]{2,1,0:T(1,128)S(1)}, u32[]{:S(2)}, u32[]{:S(2)}) collective-permute-start(f32[3,1,450]{2,1,0:T(1,128)S(1)} %get-tuple-element.18), channel_id=1, source_target_pairs={{0,1},{1,2},{2,3},{3,4},{4,5},{5,6},{6,7},{7,8},{8,9},{9,10},{10,1... | collective-permute-start | bytes 16208 | tf_op jit(solution)/shard_map/ppermute | solution.py:25
  110.4 11.3 %collective-permute-start.12 = (f32[3,192,1]{2,1,0:T(8,128)S(1)}, f32[3,192,1]{2,1,0:T(8,128)S(1)}, u32[]{:S(2)}, u32[]{:S(2)}) collective-permute-start(f32[3,192,1]{2,1,0:T(8,128)S(1)} %get-tuple-element.19), channel_id=1, source_target_pairs={{16,0},{32,16},{48,32},{64,48},{80,64},{96,80},{112,96},{128,112},... | collective-permute-start | bytes 6920 | tf_op jit(solution)/shard_map/ppermute | solution.py:26
  113.8 8.0 %collective-permute-start.13 = (f32[3,192,1]{2,1,0:T(8,128)S(1)}, f32[3,192,1]{2,1,0:T(8,128)S(1)}, u32[]{:S(2)}, u32[]{:S(2)}) collective-permute-start(f32[3,192,1]{2,1,0:T(8,128)S(1)} %get-tuple-element.20), channel_id=1, source_target_pairs={{0,16},{16,32},{32,48},{48,64},{64,80},{80,96},{96,112},{112,128},... | collective-permute-start | bytes 6920 | tf_op jit(solution)/shard_map/ppermute | solution.py:25
  160.4 2.2 %copy-start.38 = (pred[192]{0:T(512)(128)(4,1)S(1)}, pred[192]{0:T(512)(128)(4,1)}, u32[]{:S(2)}) copy-start(pred[192]{0:T(512)(128)(4,1)} %add_compare_fusion) | copy-start | bytes 580
  (10 other events, 9.4 us)

commit v5 on v3

--- a/solution.py
+++ b/solution.py
@@ -56,11 +56,11 @@
 
 
 def project(fields, table):
-    return jnp.einsum("fnw,kw->fnk", fields, table, precision=lax.Precision.HIGHEST)
+    return jnp.einsum("fnw,kw->fnk", fields, table, precision=lax.Precision.HIGH)
 
 
 def expand(coeffs, table):
-    return jnp.einsum("fnk,kw->fnw", coeffs, table, precision=lax.Precision.HIGHEST)
+    return jnp.einsum("fnk,kw->fnw", coeffs, table, precision=lax.Precision.HIGH)
 
 
 def low_pass(fields, cut_rows, active, table, wide_table, with_halos):

time: 164 us -> 161 us (0.982)
  matrix products: 8.04 us -> 5.8 us
    dot_general x5, matrix products: 8.04 us -> 5.8 us  [the longest x2 3.05 us: project(): jnp.einsum('fnw,kw->fnk', fields, table, precision=lax.Precision.HIGH)]
  transfers between devices with their start and end apart: 18 -> 18, of which waited for: 10 -> 9; matrix products, arithmetic and copies ran while one was open for 7% -> 7% of each run, Pallas kernels for 0% -> 0%
where the time goes in v5:
time: 161 us; the launch traced here: 160 us
  starting transfers between devices  49.3 us (31%)
  waiting for transfers between devices  31 us (19%)
  other arithmetic  24.3 us (15%)
  blocking collectives  24.2 us (15%)
  local copies, waits for them, and re-layouts  22.8 us (14%)
  matrix products  5.8 us (4%)
  between operations  2.96 us (2%)
    ppermute x7, starting transfers between devices, with_halo(): after = lax.ppermute(first, axis, down)  22 us
    ppermute x7, starting transfers between devices, with_halo(): before = lax.ppermute(last, axis, up)  13.6 us
    all_to_all x1, blocking collectives, low_pass(): lax.all_to_all(partial, 'lon', split_axis=1, concat_axis=0, tiled=True)  13.5 us
    ppermute x7, waiting for transfers between devices, with_halo(): before = lax.ppermute(last, axis, up)  11.5 us
    all_to_all x1, blocking collectives, low_pass(): lax.all_to_all(jnp.concatenate(payload, axis=1), 'lon', split_axis=0, con...  10.7 us
    all_to_all x1, waiting for transfers between devices, low_pass(): lax.all_to_all(partial, 'lon', split_axis=1, concat_axis=0, tiled=True)  7.45 us
    unnamed x99, local copies, waits for them, and re-layouts  7.14 us
    all_to_all x1, starting transfers between devices, low_pass(): lax.all_to_all(partial, 'lon', split_axis=1, concat_axis=0, tiled=True)  6.94 us
  transfers between devices with their start and end apart: 18, of which 9 were waited for; matrix products, arithmetic and copies ran while one was open for 7% of the time, Pallas kernels for 0%

profile of v5, /device:TPU:17, one launch (start us, length us, event | category | flops | bytes accessed | tf_op | source)
XLA Modules:
  0.0 160.3 jit_solution(8817150550655238799)
XLA Ops:
  0.6 1.3 pad_maximum_fusion.4
  2.0 7.4 %collective-permute-start.4 = (f32[3,1,450]{2,0,1:T(4,128)S(1)}, f32[3,1,450]{2,0,1:T(4,128)S(1)}, u32[]{:S(2)}, u32[]{:S(2)}) collective-permute-start(f32[3,1,450]{2,0,1:T(4,128)S(1)} %copy.237), channel_id=1, source_target_pairs={{1,0},{2,1},{3,2},{4,3},{5,4},{6,5},{7,6},{8,7},{9,8},{10,9},{11,1... | collective-permute-start | bytes 16208 | tf_op jit(solution)/shard_map/ppermute | solution.py:26
  9.4 2.8 %collective-permute-start.2 = (f32[3,450]{1,0:T(4,128)S(1)}, f32[3,450]{1,0:T(4,128)S(1)}, u32[]{:S(2)}, u32[]{:S(2)}) collective-permute-start(f32[3,450]{1,0:T(4,128)S(1)} %bitcast.208), channel_id=1, source_target_pairs={{0,128},{16,144},{32,160},{48,176},{64,192},{80,208},{96,224},{112... | collective-permute-start | bytes 16208 | tf_op jit(solution)/shard_map/ppermute | solution.py:33
  12.4 1.3 collective-permute-start
  13.7 1.9 %collective-permute-start.1 = (f32[3,192,1]{2,1,0:T(8,128)S(1)}, f32[3,192,1]{2,1,0:T(8,128)S(1)}, u32[]{:S(2)}, u32[]{:S(2)}) collective-permute-start(f32[3,192,1]{2,1,0:T(8,128)S(1)} %get-tuple-element.32), channel_id=1, source_target_pairs={{0,16},{16,32},{32,48},{48,64},{64,80},{80,96},{96,112},{112,128},... | collective-permute-start | bytes 6920 | tf_op jit(solution)/shard_map/ppermute | solution.py:25
  17.5 1.9 %collective-permute-start.3 = (f32[3,1,450]{2,0,1:T(4,128)S(1)}, f32[3,1,450]{2,0,1:T(4,128)S(1)}, u32[]{:S(2)}, u32[]{:S(2)}) collective-permute-start(f32[3,1,450]{2,0,1:T(4,128)S(1)} %get-tuple-element.45), channel_id=1, source_target_pairs={{0,1},{1,2},{2,3},{3,4},{4,5},{5,6},{6,7},{7,8},{8,9},{9,10},{10,1... | collective-permute-start | bytes 16208 | tf_op jit(solution)/shard_map/ppermute | solution.py:25
  19.4 3.9 %collective-permute-done = f32[3,192,1]{2,1,0:T(8,128)S(1)} collective-permute-done((f32[3,192,1]{2,1,0:T(8,128)S(1)}, f32[3,192,1]{2,1,0:T(8,128)S(1)}, u32[]{:S(2)}, u32[]{:S(2)}) %collective-permute-start) | collective-permute-done | bytes 2336 | tf_op jit(solution)/shard_map/ppermute | solution.py:26
  23.8 1.9 %collective-permute-done.3 = f32[3,1,450]{2,0,1:T(4,128)S(1)} collective-permute-done((f32[3,1,450]{2,0,1:T(4,128)S(1)}, f32[3,1,450]{2,0,1:T(4,128)S(1)}, u32[]{:S(2)}, u32[]{:S(2)}) %collective-permute-start.3) | collective-permute-done | bytes 5432 | tf_op jit(solution)/shard_map/ppermute | solution.py:25
  27.7 1.9 %collective-permute-start.9 = (f32[3,1,450]{2,0,1:T(4,128)S(1)}, f32[3,1,450]{2,0,1:T(4,128)S(1)}, u32[]{:S(2)}, u32[]{:S(2)}) collective-permute-start(f32[3,1,450]{2,0,1:T(4,128)S(1)} %copy.238), channel_id=1, source_target_pairs={{1,0},{2,1},{3,2},{4,3},{5,4},{6,5},{7,6},{8,7},{9,8},{10,9},{11,1... | collective-permute-start | bytes 16208 | tf_op jit(solution)/shard_map/ppermute | solution.py:26
  29.9 2.4 %collective-permute-start.5 = (f32[3,192,1]{2,1,0:T(8,128)S(1)}, f32[3,192,1]{2,1,0:T(8,128)S(1)}, u32[]{:S(2)}, u32[]{:S(2)}) collective-permute-start(f32[3,192,1]{2,1,0:T(8,128)S(1)} %get-tuple-element.25), channel_id=1, source_target_pairs={{16,0},{32,16},{48,32},{64,48},{80,64},{96,80},{112,96},{128,112},... | collective-permute-start | bytes 6920 | tf_op jit(solution)/shard_map/ppermute | solution.py:26
  32.4 3.7 %collective-permute-start.8 = (f32[3,1,450]{2,0,1:T(4,128)S(1)}, f32[3,1,450]{2,0,1:T(4,128)S(1)}, u32[]{:S(2)}, u32[]{:S(2)}) collective-permute-start(f32[3,1,450]{2,0,1:T(4,128)S(1)} %get-tuple-element.40), channel_id=1, source_target_pairs={{0,1},{1,2},{2,3},{3,4},{4,5},{5,6},{6,7},{7,8},{8,9},{9,10},{10,1... | collective-permute-start | bytes 16208 | tf_op jit(solution)/shard_map/ppermute | solution.py:25
  36.2 4.2 %collective-permute-done.8 = f32[3,1,450]{2,0,1:T(4,128)S(1)} collective-permute-done((f32[3,1,450]{2,0,1:T(4,128)S(1)}, f32[3,1,450]{2,0,1:T(4,128)S(1)}, u32[]{:S(2)}, u32[]{:S(2)}) %collective-permute-start.8) | collective-permute-done | bytes 5432 | tf_op jit(solution)/shard_map/ppermute | solution.py:25
  41.1 0.9 fusion.78
  44.8 1.5 fusion.84
  46.3 1.4 copy.156
  47.7 1.7 %reshape.465 = f32[16,1,4680]{2,1,0:T(1,128)} reshape(f32[192,3,130]{2,1,0:T(4,128)S(1)} %bitcast.198) | data formatting | bytes 599040
  49.4 6.9 %all-to-all-start = ((f32[16,1,4680]{2,1,0:T(1,128)}), f32[16,1,4680]{2,1,0:T(1,128)S(1)}, u32[]{:S(2)}, u32[]{:S(2)}) async-start(f32[16,1,4680]{2,1,0:T(1,128)} %reshape.465), calls=%async_computation | async-start | bytes 606208 | tf_op jit(solution)/shard_map/all_to_all | solution.py:73
  56.7 7.4 %all-to-all-done = f32[16,1,4680]{2,1,0:T(1,128)S(1)} async-done(((f32[16,1,4680]{2,1,0:T(1,128)}), f32[16,1,4680]{2,1,0:T(1,128)S(1)}, u32[]{:S(2)}, u32[]{:S(2)}) %all-to-all-start) | async-done | bytes 299552 | tf_op jit(solution)/shard_map/all_to_all | solution.py:73
  64.6 1.3 reduce.11
  65.9 0.9 reshape.466
  67.3 1.1 all_to_all.32
  68.4 3.8 %all-to-all-start.1 = ((f32[16,1,6606]{2,1,0:T(1,128)}), f32[16,1,6606]{2,1,0:T(1,128)S(1)}, u32[]{:S(2)}, u32[]{:S(2)}) async-start(f32[16,1,6606]{2,1,0:T(1,128)} %all_to_all.32), calls=%async_computation.1 | async-start | bytes 851968 | tf_op jit(solution)/shard_map/all_to_all | solution.py:81
  74.5 1.3 fusion.92
  75.9 5.2 %all-to-all-done.1 = f32[16,1,6606]{2,1,0:T(1,128)S(1)} async-done(((f32[16,1,6606]{2,1,0:T(1,128)}), f32[16,1,6606]{2,1,0:T(1,128)S(1)}, u32[]{:S(2)}, u32[]{:S(2)}) %all-to-all-start.1) | async-done | bytes 422816 | tf_op jit(solution)/shard_map/all_to_all | solution.py:81
  86.6 1.9 %collective-permute-start.11 = (f32[3,1,450]{2,0,1:T(4,128)S(1)}, f32[3,1,450]{2,0,1:T(4,128)S(1)}, u32[]{:S(2)}, u32[]{:S(2)}) collective-permute-start(f32[3,1,450]{2,0,1:T(4,128)S(1)} %copy.206), channel_id=1, source_target_pairs={{1,0},{2,1},{3,2},{4,3},{5,4},{6,5},{7,6},{8,7},{9,8},{10,9},{11,1... | collective-permute-start | bytes 16208 | tf_op jit(solution)/shard_map/ppermute | solution.py:26
  89.4 0.9 slice_select_fusion.2
  91.0 3.6 %collective-permute-start.10 = (f32[3,1,450]{2,0,1:T(4,128)S(1)}, f32[3,1,450]{2,0,1:T(4,128)S(1)}, u32[]{:S(2)}, u32[]{:S(2)}) collective-permute-start(f32[3,1,450]{2,0,1:T(4,128)S(1)} %get-tuple-element.38), channel_id=1, source_target_pairs={{0,1},{1,2},{2,3},{3,4},{4,5},{5,6},{6,7},{7,8},{8,9},{9,10},{10,1... | collective-permute-start | bytes 16208 | tf_op jit(solution)/shard_map/ppermute | solution.py:25
  95.2 1.0 slice.634
  96.4 2.6 %collective-permute-done.10 = f32[3,1,450]{2,0,1:T(4,128)S(1)} collective-permute-done((f32[3,1,450]{2,0,1:T(4,128)S(1)}, f32[3,1,450]{2,0,1:T(4,128)S(1)}, u32[]{:S(2)}, u32[]{:S(2)}) %collective-permute-start.10) | collective-permute-done | bytes 5432 | tf_op jit(solution)/shard_map/ppermute | solution.py:25
  101.8 3.0 %collective-permute-start.15 = (f32[3,1,450]{2,1,0:T(1,128)S(1)}, f32[3,1,450]{2,1,0:T(1,128)S(1)}, u32[]{:S(2)}, u32[]{:S(2)}) collective-permute-start(f32[3,1,450]{2,1,0:T(1,128)S(1)} %slice.667), channel_id=1, source_target_pairs={{1,0},{2,1},{3,2},{4,3},{5,4},{6,5},{7,6},{8,7},{9,8},{10,9},{11,1... | collective-permute-start | bytes 16208 | tf_op jit(solution)/shard_map/ppermute | solution.py:26
  104.8 1.4 fusion.112
  106.3 2.3 %collective-permute-start.14 = (f32[3,1,450]{2,1,0:T(1,128)S(1)}, f32[3,1,450]{2,1,0:T(1,128)S(1)}, u32[]{:S(2)}, u32[]{:S(2)}) collective-permute-start(f32[3,1,450]{2,1,0:T(1,128)S(1)} %get-tuple-element.18), channel_id=1, source_target_pairs={{0,1},{1,2},{2,3},{3,4},{4,5},{5,6},{6,7},{7,8},{8,9},{9,10},{10,1... | collective-permute-start | bytes 16208 | tf_op jit(solution)/shard_map/ppermute | solution.py:25
  108.7 4.2 %collective-permute-start.12 = (f32[3,192,1]{2,1,0:T(8,128)S(1)}, f32[3,192,1]{2,1,0:T(8,128)S(1)}, u32[]{:S(2)}, u32[]{:S(2)}) collective-permute-start(f32[3,192,1]{2,1,0:T(8,128)S(1)} %get-tuple-element.19), channel_id=1, source_target_pairs={{16,0},{32,16},{48,32},{64,48},{80,64},{96,80},{112,96},{128,112},... | collective-permute-start | bytes 6920 | tf_op jit(solution)/shard_map/ppermute | solution.py:26
  113.0 1.3 collective-permute-done.14
  114.3 2.9 %collective-permute-done.12 = f32[3,192,1]{2,1,0:T(8,128)S(1)} collective-permute-done((f32[3,192,1]{2,1,0:T(8,128)S(1)}, f32[3,192,1]{2,1,0:T(8,128)S(1)}, u32[]{:S(2)}, u32[]{:S(2)}) %collective-permute-start.12) | collective-permute-done | bytes 2336 | tf_op jit(solution)/shard_map/ppermute | solution.py:26
  117.3 1.5 collective-permute-done.13
  119.3 0.9 fusion.76
  122.1 1.6 fusion.83
  123.6 1.4 copy.190
  125.0 1.0 reshape.467
  126.0 13.5 %all_to_all.42 = f32[16,1,4680]{2,1,0:T(1,128)S(1)} all-to-all(f32[16,1,4680]{2,1,0:T(1,128)S(1)} %reshape.467), channel_id=1, replica_groups=mesh['lon'=16,'lat'=16] {'lon'}, dimensions={0} | all-to-all | bytes 599040 | tf_op jit(solution)/shard_map/all_to_all | solution.py:73
  139.5 1.3 reduce.12
  140.7 0.9 reshape.468
  142.2 10.7 %all_to_all.43 = f32[16,1,4680]{2,1,0:T(1,128)S(1)} all-to-all(f32[16,1,4680]{2,1,0:T(1,128)S(1)} %broadcast_in_dim.159), channel_id=1, replica_groups=mesh['lon'=16,'lat'=16] {'lon'}, dimensions={0} | all-to-all | bytes 599040 | tf_op jit(solution)/shard_map/all_to_all | solution.py:81
  154.3 1.0 copy.192
  155.3 2.0 %reshape.458 = f32[3,192,130]{2,1,0:T(8,128)} reshape(f32[3,16,12,130]{3,2,1,0:T(8,128)} %copy.192) | data formatting | bytes 599040 | tf_op jit(solution)/shard_map/reshape | solution.py:84
  157.3 1.9 %convolution_select_fusion = f32[3,192,450]{2,1,0:T(8,128)S(1)} fusion(f32[3,192,130]{2,1,0:T(8,128)} %reshape.458, pred[192]{0:T(512)(128)(4,1)S(1)} %copy-done.43, f32[192,130]{1,0:T(8,128)} %copy-done.13, f32[65,450]{1,0:T(8,128)} %copy-done.11, f32[65,450]{1,0:T(8,128)} %copy-done.9, f32[3,192,450]{2,1,0:T(8,128)S(1)} %slice_select_fusion, ...), kind=kOutput, calls=%fused_computation.16 | convolution fusion | flops 203605376 | bytes 3743952 | tf_op jit(solution)/shard_map/fnk,kw->fnw/dot_general | solution.py:63
  159.2 1.0 slice_bitcast_fusion
  (198 shorter events, 25.6 us)
Async XLA Ops:
  2.0 15.3 %copy-start.44 = (s32[512]{0:T(512)S(1)}, s32[512]{0:T(512)}, u32[]{:S(2)}) copy-start(s32[512]{0:T(512)} %param.12) | copy-start | bytes 6148
  2.0 21.3 %copy-start = (f32[192,450]{1,0:T(8,128)S(1)}, f32[192,450]{1,0:T(8,128)}, u32[]{:S(2)}) copy-start(f32[192,450]{1,0:T(8,128)} %param.11) | copy-start | bytes 1036804
  2.0 21.3 %copy-start.1 = (f32[192,450]{1,0:T(8,128)S(1)}, f32[192,450]{1,0:T(8,128)}, u32[]{:S(2)}) copy-start(f32[192,450]{1,0:T(8,128)} %param.10) | copy-start | bytes 1036804
  2.0 21.3 %copy-start.2 = (f32[192,450]{1,0:T(8,128)S(1)}, f32[192,450]{1,0:T(8,128)}, u32[]{:S(2)}) copy-start(f32[192,450]{1,0:T(8,128)} %param.9) | copy-start | bytes 1036804
  2.0 15.4 %collective-permute-start.4 = (f32[3,1,450]{2,0,1:T(4,128)S(1)}, f32[3,1,450]{2,0,1:T(4,128)S(1)}, u32[]{:S(2)}, u32[]{:S(2)}) collective-permute-start(f32[3,1,450]{2,0,1:T(4,128)S(1)} %copy.237), channel_id=1, source_target_pairs={{1,0},{2,1},{3,2},{4,3},{5,4},{6,5},{7,6},{8,7},{9,8},{10,9},{11,1... | collective-permute-start | bytes 16208 | tf_op jit(solution)/shard_map/ppermute | solution.py:26
  9.4 14.4 %collective-permute-start.2 = (f32[3,450]{1,0:T(4,128)S(1)}, f32[3,450]{1,0:T(4,128)S(1)}, u32[]{:S(2)}, u32[]{:S(2)}) collective-permute-start(f32[3,450]{1,0:T(4,128)S(1)} %bitcast.208), channel_id=1, source_target_pairs={{0,128},{16,144},{32,160},{48,176},{64,192},{80,208},{96,224},{112... | collective-permute-start | bytes 16208 | tf_op jit(solution)/shard_map/ppermute | solution.py:33
  12.4 10.9 %collective-permute-start = (f32[3,192,1]{2,1,0:T(8,128)S(1)}, f32[3,192,1]{2,1,0:T(8,128)S(1)}, u32[]{:S(2)}, u32[]{:S(2)}) collective-permute-start(f32[3,192,1]{2,1,0:T(8,128)S(1)} %get-tuple-element.31), channel_id=1, source_target_pairs={{16,0},{32,16},{48,32},{64,48},{80,64},{96,80},{112,96},{128,112},... | collective-permute-start | bytes 6920 | tf_op jit(solution)/shard_map/ppermute | solution.py:26
  13.7 9.5 %collective-permute-start.1 = (f32[3,192,1]{2,1,0:T(8,128)S(1)}, f32[3,192,1]{2,1,0:T(8,128)S(1)}, u32[]{:S(2)}, u32[]{:S(2)}) collective-permute-start(f32[3,192,1]{2,1,0:T(8,128)S(1)} %get-tuple-element.32), channel_id=1, source_target_pairs={{0,16},{16,32},{32,48},{48,64},{64,80},{80,96},{96,112},{112,128},... | collective-permute-start | bytes 6920 | tf_op jit(solution)/shard_map/ppermute | solution.py:25
  15.7 25.3 %copy-start.32 = (f32[192]{0:T(256)}, f32[192]{0:T(256)S(1)}, u32[]{:S(2)}) copy-start(f32[192]{0:T(256)S(1)} %get-tuple-element.60) | copy-start | bytes 2308
  15.7 25.3 %copy-start.35 = (f32[192]{0:T(256)}, f32[192]{0:T(256)S(1)}, u32[]{:S(2)}) copy-start(f32[192]{0:T(256)S(1)} %get-tuple-element.61) | copy-start | bytes 2308
  15.8 26.3 %copy-start.30 = (f32[192]{0:T(256)}, f32[192]{0:T(256)S(1)}, u32[]{:S(2)}) copy-start(f32[192]{0:T(256)S(1)} %get-tuple-element.10) | copy-start | bytes 2308
  15.8 27.1 %copy-start.17 = (f32[192]{0:T(256)}, f32[192]{0:T(256)S(1)}, u32[]{:S(2)}) copy-start(f32[192]{0:T(256)S(1)} %get-tuple-element.11) | copy-start | bytes 2308
  16.5 26.4 %copy-start.20 = (f32[192]{0:T(256)}, f32[192]{0:T(256)S(1)}, u32[]{:S(2)}) copy-start(f32[192]{0:T(256)S(1)} %get-tuple-element.58) | copy-start | bytes 2308
  16.5 26.4 %copy-start.22 = (f32[192]{0:T(256)}, f32[192]{0:T(256)S(1)}, u32[]{:S(2)}) copy-start(f32[192]{0:T(256)S(1)} %get-tuple-element.59) | copy-start | bytes 2308
  17.1 27.7 %copy-start.9 = (f32[65,450]{1,0:T(8,128)}, f32[65,450]{1,0:T(8,128)S(1)}, u32[]{:S(2)}) copy-start(f32[65,450]{1,0:T(8,128)S(1)} %get-tuple-element.53) | copy-start | bytes 351004
  17.1 27.7 %copy-start.11 = (f32[65,450]{1,0:T(8,128)}, f32[65,450]{1,0:T(8,128)S(1)}, u32[]{:S(2)}) copy-start(f32[65,450]{1,0:T(8,128)S(1)} %get-tuple-element.54) | copy-start | bytes 351004
  17.5 8.2 %copy-start.38 = (f32[3]{0:T(128)S(1)}, f32[3]{0:T(128)}, u32[]{:S(2)}) copy-start(f32[3]{0:T(128)} %constant.144.clone) | copy-start | bytes 40
  17.5 8.2 %collective-permute-start.3 = (f32[3,1,450]{2,0,1:T(4,128)S(1)}, f32[3,1,450]{2,0,1:T(4,128)S(1)}, u32[]{:S(2)}, u32[]{:S(2)}) collective-permute-start(f32[3,1,450]{2,0,1:T(4,128)S(1)} %get-tuple-element.45), channel_id=1, source_target_pairs={{0,1},{1,2},{2,3},{3,4},{4,5},{5,6},{6,7},{7,8},{8,9},{9,10},{10,1... | collective-permute-start | bytes 16208 | tf_op jit(solution)/shard_map/ppermute | solution.py:25
  25.8 10.4 %copy-start.28 = (f32[3,1,1]{2,0,1:T(4,128)}, f32[3,1,1]{2,0,1:T(4,128)S(1)}, u32[]{:S(2)}) copy-start(f32[3,1,1]{2,0,1:T(4,128)S(1)} %broadcast.385.clone) | copy-start | bytes 40
  27.7 4.7 %collective-permute-start.9 = (f32[3,1,450]{2,0,1:T(4,128)S(1)}, f32[3,1,450]{2,0,1:T(4,128)S(1)}, u32[]{:S(2)}, u32[]{:S(2)}) collective-permute-start(f32[3,1,450]{2,0,1:T(4,128)S(1)} %copy.238), channel_id=1, source_target_pairs={{1,0},{2,1},{3,2},{4,3},{5,4},{6,5},{7,6},{8,7},{9,8},{10,9},{11,1... | collective-permute-start | bytes 16208 | tf_op jit(solution)/shard_map/ppermute | solution.py:26
  29.8 6.4 %collective-permute-start.7 = (f32[3,450]{1,0:T(4,128)S(1)}, f32[3,450]{1,0:T(4,128)S(1)}, u32[]{:S(2)}, u32[]{:S(2)}) collective-permute-start(f32[3,450]{1,0:T(4,128)S(1)} %bitcast.209), channel_id=1, source_target_pairs={{0,128},{16,144},{32,160},{48,176},{64,192},{80,208},{96,224},{112... | collective-permute-start | bytes 16208 | tf_op jit(solution)/shard_map/ppermute | solution.py:33
  29.9 10.6 %collective-permute-start.5 = (f32[3,192,1]{2,1,0:T(8,128)S(1)}, f32[3,192,1]{2,1,0:T(8,128)S(1)}, u32[]{:S(2)}, u32[]{:S(2)}) collective-permute-start(f32[3,192,1]{2,1,0:T(8,128)S(1)} %get-tuple-element.25), channel_id=1, source_target_pairs={{16,0},{32,16},{48,32},{64,48},{80,64},{96,80},{112,96},{128,112},... | collective-permute-start | bytes 6920 | tf_op jit(solution)/shard_map/ppermute | solution.py:26
  32.3 8.3 %collective-permute-start.6 = (f32[3,192,1]{2,1,0:T(8,128)S(1)}, f32[3,192,1]{2,1,0:T(8,128)S(1)}, u32[]{:S(2)}, u32[]{:S(2)}) collective-permute-start(f32[3,192,1]{2,1,0:T(8,128)S(1)} %get-tuple-element.26), channel_id=1, source_target_pairs={{0,16},{16,32},{32,48},{48,64},{64,80},{80,96},{96,112},{112,128},... | collective-permute-start | bytes 6920 | tf_op jit(solution)/shard_map/ppermute | solution.py:25
  32.4 8.0 %collective-permute-start.8 = (f32[3,1,450]{2,0,1:T(4,128)S(1)}, f32[3,1,450]{2,0,1:T(4,128)S(1)}, u32[]{:S(2)}, u32[]{:S(2)}) collective-permute-start(f32[3,1,450]{2,0,1:T(4,128)S(1)} %get-tuple-element.40), channel_id=1, source_target_pairs={{0,1},{1,2},{2,3},{3,4},{4,5},{5,6},{6,7},{7,8},{8,9},{9,10},{10,1... | collective-permute-start | bytes 16208 | tf_op jit(solution)/shard_map/ppermute | solution.py:25
  49.4 14.7 %all-to-all-start = ((f32[16,1,4680]{2,1,0:T(1,128)}), f32[16,1,4680]{2,1,0:T(1,128)S(1)}, u32[]{:S(2)}, u32[]{:S(2)}) async-start(f32[16,1,4680]{2,1,0:T(1,128)} %reshape.465), calls=%async_computation | async-start | bytes 606208 | tf_op jit(solution)/shard_map/all_to_all | solution.py:73
  68.4 12.7 %all-to-all-start.1 = ((f32[16,1,6606]{2,1,0:T(1,128)}), f32[16,1,6606]{2,1,0:T(1,128)S(1)}, u32[]{:S(2)}, u32[]{:S(2)}) async-start(f32[16,1,6606]{2,1,0:T(1,128)} %all_to_all.32), calls=%async_computation.1 | async-start | bytes 851968 | tf_op jit(solution)/shard_map/all_to_all | solution.py:81
  74.5 8.9 %copy-start.13 = (f32[192,130]{1,0:T(8,128)}, f32[192,130]{1,0:T(8,128)S(1)}, u32[]{:S(2)}) copy-start(f32[192,130]{1,0:T(8,128)S(1)} %pad_maximum_fusion.45) | copy-start | bytes 299524
  86.5 3.8 %copy-start.26 = (f32[3,1,452]{2,1,0:T(1,128)S(1)}, f32[3,1,452]{2,1,0:T(1,128)}, u32[]{:S(2)}) copy-start(f32[3,1,452]{2,1,0:T(1,128)} %slice_multiply_fusion) | copy-start | bytes 16276
  86.5 12.5 %copy-start.39 = (f32[3]{0:T(128)S(1)}, f32[3]{0:T(128)}, u32[]{:S(2)}) copy-start(f32[3]{0:T(128)} %constant.144.clone) | copy-start | bytes 40
  86.5 12.5 %copy-start.42 = (pred[192]{0:T(512)(128)(4,1)S(1)}, pred[192]{0:T(512)(128)(4,1)}, u32[]{:S(2)}) copy-start(pred[192]{0:T(512)(128)(4,1)} %add_compare_fusion) | copy-start | bytes 580
  86.5 12.6 %copy-start.29 = (f32[3,1,1]{2,0,1:T(4,128)S(1)}, f32[3,1,1]{2,0,1:T(4,128)}, u32[]{:S(2)}) copy-start(f32[3,1,1]{2,0,1:T(4,128)} %copy-done.28) | copy-start | bytes 40
  86.5 12.7 %copy-start.18 = (f32[192]{0:T(256)S(1)}, f32[192]{0:T(256)}, u32[]{:S(2)}) copy-start(f32[192]{0:T(256)} %copy-done.17) | copy-start | bytes 2308
  86.5 12.7 %copy-start.33 = (f32[192]{0:T(256)S(1)}, f32[192]{0:T(256)}, u32[]{:S(2)}) copy-start(f32[192]{0:T(256)} %copy-done.32) | copy-start | bytes 2308
  86.5 12.7 %copy-start.36 = (f32[192]{0:T(256)S(1)}, f32[192]{0:T(256)}, u32[]{:S(2)}) copy-start(f32[192]{0:T(256)} %copy-done.35) | copy-start | bytes 2308
  86.6 4.4 %collective-permute-start.11 = (f32[3,1,450]{2,0,1:T(4,128)S(1)}, f32[3,1,450]{2,0,1:T(4,128)S(1)}, u32[]{:S(2)}, u32[]{:S(2)}) collective-permute-start(f32[3,1,450]{2,0,1:T(4,128)S(1)} %copy.206), channel_id=1, source_target_pairs={{1,0},{2,1},{3,2},{4,3},{5,4},{6,5},{7,6},{8,7},{9,8},{10,9},{11,1... | collective-permute-start | bytes 16208 | tf_op jit(solution)/shard_map/ppermute | solution.py:26
  91.0 8.0 %collective-permute-start.10 = (f32[3,1,450]{2,0,1:T(4,128)S(1)}, f32[3,1,450]{2,0,1:T(4,128)S(1)}, u32[]{:S(2)}, u32[]{:S(2)}) collective-permute-start(f32[3,1,450]{2,0,1:T(4,128)S(1)} %get-tuple-element.38), channel_id=1, source_target_pairs={{0,1},{1,2},{2,3},{3,4},{4,5},{5,6},{6,7},{7,8},{8,9},{9,10},{10,1... | collective-permute-start | bytes 16208 | tf_op jit(solution)/shard_map/ppermute | solution.py:25
  96.3 3.7 %copy-start.21 = (f32[192]{0:T(256)S(1)}, f32[192]{0:T(256)}, u32[]{:S(2)}) copy-start(f32[192]{0:T(256)} %copy-done.20) | copy-start | bytes 2308
  96.4 3.7 %copy-start.23 = (f32[192]{0:T(256)S(1)}, f32[192]{0:T(256)}, u32[]{:S(2)}) copy-start(f32[192]{0:T(256)} %copy-done.22) | copy-start | bytes 2308
  96.4 3.7 %copy-start.31 = (f32[192]{0:T(256)S(1)}, f32[192]{0:T(256)}, u32[]{:S(2)}) copy-start(f32[192]{0:T(256)} %copy-done.30) | copy-start | bytes 2308
  101.8 12.4 %copy-start.40 = (f32[3]{0:T(128)S(1)}, f32[3]{0:T(128)}, u32[]{:S(2)}) copy-start(f32[3]{0:T(128)} %constant.144.clone) | copy-start | bytes 40
  101.8 16.9 %copy-start.25 = (f32[3,1,1]{2,1,0:T(1,128)S(1)}, f32[3,1,1]{2,1,0:T(1,128)}, u32[]{:S(2)}) copy-start(f32[3,1,1]{2,1,0:T(1,128)} %copy-done.24) | copy-start | bytes 40
  101.8 4.4 %collective-permute-start.15 = (f32[3,1,450]{2,1,0:T(1,128)S(1)}, f32[3,1,450]{2,1,0:T(1,128)S(1)}, u32[]{:S(2)}, u32[]{:S(2)}) collective-permute-start(f32[3,1,450]{2,1,0:T(1,128)S(1)} %slice.667), channel_id=1, source_target_pairs={{1,0},{2,1},{3,2},{4,3},{5,4},{6,5},{7,6},{8,7},{9,8},{10,9},{11,1... | collective-permute-start | bytes 16208 | tf_op jit(solution)/shard_map/ppermute | solution.py:26
  106.3 8.0 %collective-permute-start.14 = (f32[3,1,450]{2,1,0:T(1,128)S(1)}, f32[3,1,450]{2,1,0:T(1,128)S(1)}, u32[]{:S(2)}, u32[]{:S(2)}) collective-permute-start(f32[3,1,450]{2,1,0:T(1,128)S(1)} %get-tuple-element.18), channel_id=1, source_target_pairs={{0,1},{1,2},{2,3},{3,4},{4,5},{5,6},{6,7},{7,8},{8,9},{9,10},{10,1... | collective-permute-start | bytes 16208 | tf_op jit(solution)/shard_map/ppermute | solution.py:25
  108.7 8.5 %collective-permute-start.12 = (f32[3,192,1]{2,1,0:T(8,128)S(1)}, f32[3,192,1]{2,1,0:T(8,128)S(1)}, u32[]{:S(2)}, u32[]{:S(2)}) collective-permute-start(f32[3,192,1]{2,1,0:T(8,128)S(1)} %get-tuple-element.19), channel_id=1, source_target_pairs={{16,0},{32,16},{48,32},{64,48},{80,64},{96,80},{112,96},{128,112},... | collective-permute-start | bytes 6920 | tf_op jit(solution)/shard_map/ppermute | solution.py:26
  112.9 5.8 %collective-permute-start.13 = (f32[3,192,1]{2,1,0:T(8,128)S(1)}, f32[3,192,1]{2,1,0:T(8,128)S(1)}, u32[]{:S(2)}, u32[]{:S(2)}) collective-permute-start(f32[3,192,1]{2,1,0:T(8,128)S(1)} %get-tuple-element.20), channel_id=1, source_target_pairs={{0,16},{16,32},{32,48},{48,64},{64,80},{80,96},{96,112},{112,128},... | collective-permute-start | bytes 6920 | tf_op jit(solution)/shard_map/ppermute | solution.py:25
  114.3 5.0 %copy-start.19 = (f32[192]{0:T(256)S(1)}, f32[192]{0:T(256)}, u32[]{:S(2)}) copy-start(f32[192]{0:T(256)} %copy-done.17) | copy-start | bytes 2308
  114.3 5.0 %copy-start.34 = (f32[192]{0:T(256)S(1)}, f32[192]{0:T(256)}, u32[]{:S(2)}) copy-start(f32[192]{0:T(256)} %copy-done.32) | copy-start | bytes 2308
  114.3 5.0 %copy-start.37 = (f32[192]{0:T(256)S(1)}, f32[192]{0:T(256)}, u32[]{:S(2)}) copy-start(f32[192]{0:T(256)} %copy-done.35) | copy-start | bytes 2308
  (15 other events, 20.5 us)

commit v6 on v5

--- a/solution.py
+++ b/solution.py
@@ -235,8 +235,8 @@
     sin_all = jnp.cos((index + 0.5) * lat_step)
     sinlat = sin_all[1:-1][:, None]
     width = height.shape[1]
-    table = local_table(0, width)
     wide_table = local_table(-1, width + 2)
+    table = wide_table[:, 1:-1]
     state = jnp.stack([height, east_wind, north_wind], axis=0)
     lon_halos = None
     pole = None

time: 161 us -> 167 us (1.037)
  local copies, waits for them, and re-layouts: 22.8 us -> 26.5 us
  waiting for transfers between devices: 31 us -> 33.4 us
    cos x2 -> x0, other arithmetic: 1.94 us -> none  [local_table(): return jnp.concatenate([jnp.cos(angle), jnp.sin(angle)], axis=0)]
    unnamed x99 -> x59, local copies, waits for them, and re-layouts: 7.14 us -> 8.01 us
  transfers between devices with their start and end apart: 18 -> 18, of which waited for: 9 -> 11; matrix products, arithmetic and copies ran while one was open for 7% -> 6% of each run, Pallas kernels for 0% -> 0%
where the time goes in v6:
time: 167 us; the launch traced here: 166 us
  starting transfers between devices  49.4 us (30%)
  waiting for transfers between devices  33.4 us (20%)
  local copies, waits for them, and re-layouts  26.5 us (16%)
  blocking collectives  24.2 us (14%)
  other arithmetic  23.6 us (14%)
  matrix products  6 us (4%)
  between operations  2.82 us (2%)
    ppermute x7, starting transfers between devices, with_halo(): after = lax.ppermute(first, axis, down)  22.2 us
    all_to_all x1, blocking collectives, low_pass(): lax.all_to_all(partial, 'lon', split_axis=1, concat_axis=0, tiled=True)  13.5 us
    ppermute x7, starting transfers between devices, with_halo(): before = lax.ppermute(last, axis, up)  12.8 us
    ppermute x7, waiting for transfers between devices, with_halo(): before = lax.ppermute(last, axis, up)  12.3 us
    all_to_all x1, blocking collectives, low_pass(): lax.all_to_all(jnp.concatenate(payload, axis=1), 'lon', split_axis=0, con...  10.7 us
    unnamed x59, local copies, waits for them, and re-layouts  8.01 us
    all_to_all x1, waiting for transfers between devices, low_pass(): lax.all_to_all(partial, 'lon', split_axis=1, concat_axis=0, tiled=True)  7.55 us
    ppermute x7, waiting for transfers between devices, with_halo(): after = lax.ppermute(first, axis, down)  7.26 us
  transfers between devices with their start and end apart: 18, of which 11 were waited for; matrix products, arithmetic and copies ran while one was open for 6% of the time, Pallas kernels for 0%

profile of v6, /device:TPU:17, one launch (start us, length us, event | category | flops | bytes accessed | tf_op | source)
XLA Modules:
  0.0 166.0 jit_solution(13789621141697905799)
XLA Ops:
  0.6 1.3 pad_maximum_fusion.4
  2.0 7.4 %collective-permute-start.4 = (f32[3,1,450]{2,0,1:T(4,128)S(1)}, f32[3,1,450]{2,0,1:T(4,128)S(1)}, u32[]{:S(2)}, u32[]{:S(2)}) collective-permute-start(f32[3,1,450]{2,0,1:T(4,128)S(1)} %copy.237), channel_id=1, source_target_pairs={{1,0},{2,1},{3,2},{4,3},{5,4},{6,5},{7,6},{8,7},{9,8},{10,9},{11,1... | collective-permute-start | bytes 16208 | tf_op jit(solution)/shard_map/ppermute | solution.py:26
  9.4 2.8 %collective-permute-start.2 = (f32[3,450]{1,0:T(4,128)S(1)}, f32[3,450]{1,0:T(4,128)S(1)}, u32[]{:S(2)}, u32[]{:S(2)}) collective-permute-start(f32[3,450]{1,0:T(4,128)S(1)} %bitcast.208), channel_id=1, source_target_pairs={{0,128},{16,144},{32,160},{48,176},{64,192},{80,208},{96,224},{112... | collective-permute-start | bytes 16208 | tf_op jit(solution)/shard_map/ppermute | solution.py:33
  12.4 1.3 collective-permute-start
  13.7 1.9 %collective-permute-start.1 = (f32[3,192,1]{2,1,0:T(8,128)S(1)}, f32[3,192,1]{2,1,0:T(8,128)S(1)}, u32[]{:S(2)}, u32[]{:S(2)}) collective-permute-start(f32[3,192,1]{2,1,0:T(8,128)S(1)} %get-tuple-element.32), channel_id=1, source_target_pairs={{0,16},{16,32},{32,48},{48,64},{64,80},{80,96},{96,112},{112,128},... | collective-permute-start | bytes 6920 | tf_op jit(solution)/shard_map/ppermute | solution.py:25
  17.9 1.9 %collective-permute-start.3 = (f32[3,1,450]{2,0,1:T(4,128)S(1)}, f32[3,1,450]{2,0,1:T(4,128)S(1)}, u32[]{:S(2)}, u32[]{:S(2)}) collective-permute-start(f32[3,1,450]{2,0,1:T(4,128)S(1)} %get-tuple-element.45), channel_id=1, source_target_pairs={{0,1},{1,2},{2,3},{3,4},{4,5},{5,6},{6,7},{7,8},{8,9},{9,10},{10,1... | collective-permute-start | bytes 16208 | tf_op jit(solution)/shard_map/ppermute | solution.py:25
  19.8 3.5 %collective-permute-done = f32[3,192,1]{2,1,0:T(8,128)S(1)} collective-permute-done((f32[3,192,1]{2,1,0:T(8,128)S(1)}, f32[3,192,1]{2,1,0:T(8,128)S(1)}, u32[]{:S(2)}, u32[]{:S(2)}) %collective-permute-start) | collective-permute-done | bytes 2336 | tf_op jit(solution)/shard_map/ppermute | solution.py:26
  23.8 2.2 %collective-permute-done.3 = f32[3,1,450]{2,0,1:T(4,128)S(1)} collective-permute-done((f32[3,1,450]{2,0,1:T(4,128)S(1)}, f32[3,1,450]{2,0,1:T(4,128)S(1)}, u32[]{:S(2)}, u32[]{:S(2)}) %collective-permute-start.3) | collective-permute-done | bytes 5432 | tf_op jit(solution)/shard_map/ppermute | solution.py:25
  28.1 1.9 %collective-permute-start.9 = (f32[3,1,450]{2,0,1:T(4,128)S(1)}, f32[3,1,450]{2,0,1:T(4,128)S(1)}, u32[]{:S(2)}, u32[]{:S(2)}) collective-permute-start(f32[3,1,450]{2,0,1:T(4,128)S(1)} %copy.238), channel_id=1, source_target_pairs={{1,0},{2,1},{3,2},{4,3},{5,4},{6,5},{7,6},{8,7},{9,8},{10,9},{11,1... | collective-permute-start | bytes 16208 | tf_op jit(solution)/shard_map/ppermute | solution.py:26
  30.3 2.4 %collective-permute-start.5 = (f32[3,192,1]{2,1,0:T(8,128)S(1)}, f32[3,192,1]{2,1,0:T(8,128)S(1)}, u32[]{:S(2)}, u32[]{:S(2)}) collective-permute-start(f32[3,192,1]{2,1,0:T(8,128)S(1)} %get-tuple-element.25), channel_id=1, source_target_pairs={{16,0},{32,16},{48,32},{64,48},{80,64},{96,80},{112,96},{128,112},... | collective-permute-start | bytes 6920 | tf_op jit(solution)/shard_map/ppermute | solution.py:26
  32.7 3.8 %collective-permute-start.8 = (f32[3,1,450]{2,0,1:T(4,128)S(1)}, f32[3,1,450]{2,0,1:T(4,128)S(1)}, u32[]{:S(2)}, u32[]{:S(2)}) collective-permute-start(f32[3,1,450]{2,0,1:T(4,128)S(1)} %get-tuple-element.40), channel_id=1, source_target_pairs={{0,1},{1,2},{2,3},{3,4},{4,5},{5,6},{6,7},{7,8},{8,9},{9,10},{10,1... | collective-permute-start | bytes 16208 | tf_op jit(solution)/shard_map/ppermute | solution.py:25
  36.7 4.1 %collective-permute-done.8 = f32[3,1,450]{2,0,1:T(4,128)S(1)} collective-permute-done((f32[3,1,450]{2,0,1:T(4,128)S(1)}, f32[3,1,450]{2,0,1:T(4,128)S(1)}, u32[]{:S(2)}, u32[]{:S(2)}) %collective-permute-start.8) | collective-permute-done | bytes 5432 | tf_op jit(solution)/shard_map/ppermute | solution.py:25
  42.2 0.9 fusion.78
  45.0 1.5 fusion.120
  46.5 2.2 %copy.156 = f32[3,192,130]{2,0,1:T(4,128)} copy(f32[3,192,130]{1,2,0:T(8,128)} %fusion.120) | data formatting | bytes 599040 | tf_op jit(solution)/shard_map/fnw,kw->fnk/dot_general | solution.py:59
  48.7 2.9 %reshape.455 = f32[16,1,4680]{2,1,0:T(1,128)} reshape(f32[192,3,130]{2,1,0:T(4,128)} %bitcast.198) | data formatting | bytes 599040
  51.6 7.0 %all-to-all-start = ((f32[16,1,4680]{2,1,0:T(1,128)}), f32[16,1,4680]{2,1,0:T(1,128)}, u32[]{:S(2)}, u32[]{:S(2)}) async-start(f32[16,1,4680]{2,1,0:T(1,128)} %reshape.455), calls=%async_computation | async-start | bytes 606208 | tf_op jit(solution)/shard_map/all_to_all | solution.py:73
  58.9 7.5 %all-to-all-done = f32[16,1,4680]{2,1,0:T(1,128)} async-done(((f32[16,1,4680]{2,1,0:T(1,128)}), f32[16,1,4680]{2,1,0:T(1,128)}, u32[]{:S(2)}, u32[]{:S(2)}) %all-to-all-start) | async-done | bytes 299552 | tf_op jit(solution)/shard_map/all_to_all | solution.py:73
  67.0 2.3 %reduce.11 = f32[16,4680]{1,0:T(8,128)S(1)} reduce(f32[16,1,4680]{2,1,0:T(1,128)} %all-to-all-done, f32[]{:T(128)} %broadcast.410), dimensions={1}, to_apply=%all_to_all.30.reduce_sub_computation | reduce | bytes 599044 | tf_op jit(solution)/shard_map/all_to_all | solution.py:73
  69.3 0.9 reshape.456
  70.7 1.1 all_to_all.32
  71.8 4.4 %all-to-all-start.1 = ((f32[16,1,6606]{2,1,0:T(1,128)}), f32[16,1,6606]{2,1,0:T(1,128)}, u32[]{:S(2)}, u32[]{:S(2)}) async-start(f32[16,1,6606]{2,1,0:T(1,128)} %all_to_all.32), calls=%async_computation.1 | async-start | bytes 851968 | tf_op jit(solution)/shard_map/all_to_all | solution.py:81
  78.9 6.3 %all-to-all-done.1 = f32[16,1,6606]{2,1,0:T(1,128)} async-done(((f32[16,1,6606]{2,1,0:T(1,128)}), f32[16,1,6606]{2,1,0:T(1,128)}, u32[]{:S(2)}, u32[]{:S(2)}) %all-to-all-start.1) | async-done | bytes 422816 | tf_op jit(solution)/shard_map/all_to_all | solution.py:81
  85.2 1.0 copy.236
  88.4 1.0 copy.158
  89.4 1.2 reshape.444
  92.3 1.9 %collective-permute-start.11 = (f32[3,1,450]{2,0,1:T(4,128)S(1)}, f32[3,1,450]{2,0,1:T(4,128)S(1)}, u32[]{:S(2)}, u32[]{:S(2)}) collective-permute-start(f32[3,1,450]{2,0,1:T(4,128)S(1)} %copy.206), channel_id=1, source_target_pairs={{1,0},{2,1},{3,2},{4,3},{5,4},{6,5},{7,6},{8,7},{9,8},{10,9},{11,1... | collective-permute-start | bytes 16208 | tf_op jit(solution)/shard_map/ppermute | solution.py:26
  96.7 2.9 %collective-permute-start.10 = (f32[3,1,450]{2,0,1:T(4,128)S(1)}, f32[3,1,450]{2,0,1:T(4,128)S(1)}, u32[]{:S(2)}, u32[]{:S(2)}) collective-permute-start(f32[3,1,450]{2,0,1:T(4,128)S(1)} %get-tuple-element.38), channel_id=1, source_target_pairs={{0,1},{1,2},{2,3},{3,4},{4,5},{5,6},{6,7},{7,8},{8,9},{9,10},{10,1... | collective-permute-start | bytes 16208 | tf_op jit(solution)/shard_map/ppermute | solution.py:25
  100.3 1.0 slice.640
  101.4 3.2 %collective-permute-done.10 = f32[3,1,450]{2,0,1:T(4,128)S(1)} collective-permute-done((f32[3,1,450]{2,0,1:T(4,128)S(1)}, f32[3,1,450]{2,0,1:T(4,128)S(1)}, u32[]{:S(2)}, u32[]{:S(2)}) %collective-permute-start.10) | collective-permute-done | bytes 5432 | tf_op jit(solution)/shard_map/ppermute | solution.py:25
  107.5 3.0 %collective-permute-start.15 = (f32[3,1,450]{2,1,0:T(1,128)S(1)}, f32[3,1,450]{2,1,0:T(1,128)S(1)}, u32[]{:S(2)}, u32[]{:S(2)}) collective-permute-start(f32[3,1,450]{2,1,0:T(1,128)S(1)} %slice.673), channel_id=1, source_target_pairs={{1,0},{2,1},{3,2},{4,3},{5,4},{6,5},{7,6},{8,7},{9,8},{10,9},{11,1... | collective-permute-start | bytes 16208 | tf_op jit(solution)/shard_map/ppermute | solution.py:26
  110.5 1.3 fusion.109
  111.9 2.3 %collective-permute-start.14 = (f32[3,1,450]{2,1,0:T(1,128)S(1)}, f32[3,1,450]{2,1,0:T(1,128)S(1)}, u32[]{:S(2)}, u32[]{:S(2)}) collective-permute-start(f32[3,1,450]{2,1,0:T(1,128)S(1)} %get-tuple-element.18), channel_id=1, source_target_pairs={{0,1},{1,2},{2,3},{3,4},{4,5},{5,6},{6,7},{7,8},{8,9},{9,10},{10,1... | collective-permute-start | bytes 16208 | tf_op jit(solution)/shard_map/ppermute | solution.py:25
  114.3 4.3 %collective-permute-start.12 = (f32[3,192,1]{2,1,0:T(8,128)S(1)}, f32[3,192,1]{2,1,0:T(8,128)S(1)}, u32[]{:S(2)}, u32[]{:S(2)}) collective-permute-start(f32[3,192,1]{2,1,0:T(8,128)S(1)} %get-tuple-element.19), channel_id=1, source_target_pairs={{16,0},{32,16},{48,32},{64,48},{80,64},{96,80},{112,96},{128,112},... | collective-permute-start | bytes 6920 | tf_op jit(solution)/shard_map/ppermute | solution.py:26
  118.6 1.2 collective-permute-done.14
  120.0 3.0 %collective-permute-done.12 = f32[3,192,1]{2,1,0:T(8,128)S(1)} collective-permute-done((f32[3,192,1]{2,1,0:T(8,128)S(1)}, f32[3,192,1]{2,1,0:T(8,128)S(1)}, u32[]{:S(2)}, u32[]{:S(2)}) %collective-permute-start.12) | collective-permute-done | bytes 2336 | tf_op jit(solution)/shard_map/ppermute | solution.py:26
  123.0 1.5 collective-permute-done.13
  125.0 0.9 fusion.76
  127.5 1.6 fusion.95
  129.1 1.4 copy.190
  130.4 1.0 reshape.457
  131.4 13.5 %all_to_all.42 = f32[16,1,4680]{2,1,0:T(1,128)S(1)} all-to-all(f32[16,1,4680]{2,1,0:T(1,128)S(1)} %reshape.457), channel_id=1, replica_groups=mesh['lon'=16,'lat'=16] {'lon'}, dimensions={0} | all-to-all | bytes 599040 | tf_op jit(solution)/shard_map/all_to_all | solution.py:73
  145.0 1.3 reduce.12
  147.7 10.7 %all_to_all.43 = f32[16,1,4680]{2,1,0:T(1,128)S(1)} all-to-all(f32[16,1,4680]{2,1,0:T(1,128)S(1)} %broadcast_in_dim.157), channel_id=1, replica_groups=mesh['lon'=16,'lat'=16] {'lon'}, dimensions={0} | all-to-all | bytes 599040 | tf_op jit(solution)/shard_map/all_to_all | solution.py:81
  159.9 1.0 copy.192
  160.8 2.0 %reshape.448 = f32[3,192,130]{2,1,0:T(8,128)} reshape(f32[3,16,12,130]{3,2,1,0:T(8,128)} %copy.192) | data formatting | bytes 599040 | tf_op jit(solution)/shard_map/reshape | solution.py:84
  162.8 2.1 %convolution_select_fusion = f32[3,192,450]{2,1,0:T(8,128)S(1)} fusion(f32[3,192,130]{2,1,0:T(8,128)} %reshape.448, pred[192]{0:T(512)(128)(4,1)S(1)} %copy-done.22, f32[192,130]{1,0:T(8,128)} %copy-done.6, f32[3,192,450]{2,1,0:T(8,128)S(1)} %slice_select_fusion, f32[1,192,450]{2,1,0:T(8,128)S(1)} %fusion.25, f32[1,192,450]{2,1,0:T(8,128)S(1)} %fusion.32, ...), kind=kOutput, calls=%fused_computation.16 | convolution fusion | flops 203605376 | bytes 3744992 | tf_op jit(solution)/shard_map/fnk,kw->fnw/dot_general | solution.py:63
  165.0 1.0 slice_bitcast_fusion
  (156 shorter events, 26.2 us)
Async XLA Ops:
  2.0 15.8 %copy-start.23 = (s32[512]{0:T(512)S(1)}, s32[512]{0:T(512)}, u32[]{:S(2)}) copy-start(s32[512]{0:T(512)} %param.12) | copy-start | bytes 6148
  2.0 21.3 %copy-start = (f32[192,450]{1,0:T(8,128)S(1)}, f32[192,450]{1,0:T(8,128)}, u32[]{:S(2)}) copy-start(f32[192,450]{1,0:T(8,128)} %param.11) | copy-start | bytes 1036804
  2.0 21.3 %copy-start.1 = (f32[192,450]{1,0:T(8,128)S(1)}, f32[192,450]{1,0:T(8,128)}, u32[]{:S(2)}) copy-start(f32[192,450]{1,0:T(8,128)} %param.10) | copy-start | bytes 1036804
  2.0 21.3 %copy-start.2 = (f32[192,450]{1,0:T(8,128)S(1)}, f32[192,450]{1,0:T(8,128)}, u32[]{:S(2)}) copy-start(f32[192,450]{1,0:T(8,128)} %param.9) | copy-start | bytes 1036804
  2.0 15.8 %collective-permute-start.4 = (f32[3,1,450]{2,0,1:T(4,128)S(1)}, f32[3,1,450]{2,0,1:T(4,128)S(1)}, u32[]{:S(2)}, u32[]{:S(2)}) collective-permute-start(f32[3,1,450]{2,0,1:T(4,128)S(1)} %copy.237), channel_id=1, source_target_pairs={{1,0},{2,1},{3,2},{4,3},{5,4},{6,5},{7,6},{8,7},{9,8},{10,9},{11,1... | collective-permute-start | bytes 16208 | tf_op jit(solution)/shard_map/ppermute | solution.py:26
  9.4 14.4 %collective-permute-start.2 = (f32[3,450]{1,0:T(4,128)S(1)}, f32[3,450]{1,0:T(4,128)S(1)}, u32[]{:S(2)}, u32[]{:S(2)}) collective-permute-start(f32[3,450]{1,0:T(4,128)S(1)} %bitcast.208), channel_id=1, source_target_pairs={{0,128},{16,144},{32,160},{48,176},{64,192},{80,208},{96,224},{112... | collective-permute-start | bytes 16208 | tf_op jit(solution)/shard_map/ppermute | solution.py:33
  12.4 10.9 %collective-permute-start = (f32[3,192,1]{2,1,0:T(8,128)S(1)}, f32[3,192,1]{2,1,0:T(8,128)S(1)}, u32[]{:S(2)}, u32[]{:S(2)}) collective-permute-start(f32[3,192,1]{2,1,0:T(8,128)S(1)} %get-tuple-element.31), channel_id=1, source_target_pairs={{16,0},{32,16},{48,32},{64,48},{80,64},{96,80},{112,96},{128,112},... | collective-permute-start | bytes 6920 | tf_op jit(solution)/shard_map/ppermute | solution.py:26
  13.7 9.5 %collective-permute-start.1 = (f32[3,192,1]{2,1,0:T(8,128)S(1)}, f32[3,192,1]{2,1,0:T(8,128)S(1)}, u32[]{:S(2)}, u32[]{:S(2)}) collective-permute-start(f32[3,192,1]{2,1,0:T(8,128)S(1)} %get-tuple-element.32), channel_id=1, source_target_pairs={{0,16},{16,32},{32,48},{48,64},{64,80},{80,96},{96,112},{112,128},... | collective-permute-start | bytes 6920 | tf_op jit(solution)/shard_map/ppermute | solution.py:25
  16.4 25.0 %copy-start.14 = (f32[192]{0:T(256)}, f32[192]{0:T(256)S(1)}, u32[]{:S(2)}) copy-start(f32[192]{0:T(256)S(1)} %get-tuple-element.10) | copy-start | bytes 2308
  16.4 25.8 %copy-start.16 = (f32[192]{0:T(256)}, f32[192]{0:T(256)S(1)}, u32[]{:S(2)}) copy-start(f32[192]{0:T(256)S(1)} %get-tuple-element.58) | copy-start | bytes 2308
  16.4 25.8 %copy-start.18 = (f32[192]{0:T(256)}, f32[192]{0:T(256)S(1)}, u32[]{:S(2)}) copy-start(f32[192]{0:T(256)S(1)} %get-tuple-element.59) | copy-start | bytes 2308
  17.1 26.0 %copy-start.8 = (f32[192]{0:T(256)}, f32[192]{0:T(256)S(1)}, u32[]{:S(2)}) copy-start(f32[192]{0:T(256)S(1)} %get-tuple-element.57) | copy-start | bytes 2308
  17.9 8.2 %copy-start.20 = (f32[3]{0:T(128)S(1)}, f32[3]{0:T(128)}, u32[]{:S(2)}) copy-start(f32[3]{0:T(128)} %constant.127.clone) | copy-start | bytes 40
  17.9 8.2 %collective-permute-start.3 = (f32[3,1,450]{2,0,1:T(4,128)S(1)}, f32[3,1,450]{2,0,1:T(4,128)S(1)}, u32[]{:S(2)}, u32[]{:S(2)}) collective-permute-start(f32[3,1,450]{2,0,1:T(4,128)S(1)} %get-tuple-element.45), channel_id=1, source_target_pairs={{0,1},{1,2},{2,3},{3,4},{4,5},{5,6},{6,7},{7,8},{8,9},{9,10},{10,1... | collective-permute-start | bytes 16208 | tf_op jit(solution)/shard_map/ppermute | solution.py:25
  26.1 10.4 %copy-start.12 = (f32[3,1,1]{2,0,1:T(4,128)}, f32[3,1,1]{2,0,1:T(4,128)S(1)}, u32[]{:S(2)}) copy-start(f32[3,1,1]{2,0,1:T(4,128)S(1)} %broadcast.361.clone) | copy-start | bytes 40
  28.1 4.6 %collective-permute-start.9 = (f32[3,1,450]{2,0,1:T(4,128)S(1)}, f32[3,1,450]{2,0,1:T(4,128)S(1)}, u32[]{:S(2)}, u32[]{:S(2)}) collective-permute-start(f32[3,1,450]{2,0,1:T(4,128)S(1)} %copy.238), channel_id=1, source_target_pairs={{1,0},{2,1},{3,2},{4,3},{5,4},{6,5},{7,6},{8,7},{9,8},{10,9},{11,1... | collective-permute-start | bytes 16208 | tf_op jit(solution)/shard_map/ppermute | solution.py:26
  30.2 6.5 %collective-permute-start.7 = (f32[3,450]{1,0:T(4,128)S(1)}, f32[3,450]{1,0:T(4,128)S(1)}, u32[]{:S(2)}, u32[]{:S(2)}) collective-permute-start(f32[3,450]{1,0:T(4,128)S(1)} %bitcast.209), channel_id=1, source_target_pairs={{0,128},{16,144},{32,160},{48,176},{64,192},{80,208},{96,224},{112... | collective-permute-start | bytes 16208 | tf_op jit(solution)/shard_map/ppermute | solution.py:33
  30.3 10.5 %collective-permute-start.5 = (f32[3,192,1]{2,1,0:T(8,128)S(1)}, f32[3,192,1]{2,1,0:T(8,128)S(1)}, u32[]{:S(2)}, u32[]{:S(2)}) collective-permute-start(f32[3,192,1]{2,1,0:T(8,128)S(1)} %get-tuple-element.25), channel_id=1, source_target_pairs={{16,0},{32,16},{48,32},{64,48},{80,64},{96,80},{112,96},{128,112},... | collective-permute-start | bytes 6920 | tf_op jit(solution)/shard_map/ppermute | solution.py:26
  32.7 8.1 %collective-permute-start.6 = (f32[3,192,1]{2,1,0:T(8,128)S(1)}, f32[3,192,1]{2,1,0:T(8,128)S(1)}, u32[]{:S(2)}, u32[]{:S(2)}) collective-permute-start(f32[3,192,1]{2,1,0:T(8,128)S(1)} %get-tuple-element.26), channel_id=1, source_target_pairs={{0,16},{16,32},{32,48},{48,64},{64,80},{80,96},{96,112},{112,128},... | collective-permute-start | bytes 6920 | tf_op jit(solution)/shard_map/ppermute | solution.py:25
  32.7 8.0 %collective-permute-start.8 = (f32[3,1,450]{2,0,1:T(4,128)S(1)}, f32[3,1,450]{2,0,1:T(4,128)S(1)}, u32[]{:S(2)}, u32[]{:S(2)}) collective-permute-start(f32[3,1,450]{2,0,1:T(4,128)S(1)} %get-tuple-element.40), channel_id=1, source_target_pairs={{0,1},{1,2},{2,3},{3,4},{4,5},{5,6},{6,7},{7,8},{8,9},{9,10},{10,1... | collective-permute-start | bytes 16208 | tf_op jit(solution)/shard_map/ppermute | solution.py:25
  40.8 0.5 copy-start.10
  43.8 0.7 copy-start.3
  51.6 14.9 %all-to-all-start = ((f32[16,1,4680]{2,1,0:T(1,128)}), f32[16,1,4680]{2,1,0:T(1,128)}, u32[]{:S(2)}, u32[]{:S(2)}) async-start(f32[16,1,4680]{2,1,0:T(1,128)} %reshape.455), calls=%async_computation | async-start | bytes 606208 | tf_op jit(solution)/shard_map/all_to_all | solution.py:73
  71.8 13.4 %all-to-all-start.1 = ((f32[16,1,6606]{2,1,0:T(1,128)}), f32[16,1,6606]{2,1,0:T(1,128)}, u32[]{:S(2)}, u32[]{:S(2)}) async-start(f32[16,1,6606]{2,1,0:T(1,128)} %all_to_all.32), calls=%async_computation.1 | async-start | bytes 851968 | tf_op jit(solution)/shard_map/all_to_all | solution.py:81
  78.9 11.7 %copy-start.6 = (f32[192,130]{1,0:T(8,128)}, f32[192,130]{1,0:T(8,128)S(1)}, u32[]{:S(2)}) copy-start(f32[192,130]{1,0:T(8,128)S(1)} %pad_maximum_fusion.46) | copy-start | bytes 299524
  86.2 0.7 copy-start.7
  90.6 0.7 copy-start.24
  90.7 0.9 copy-start.21
  90.7 1.0 copy-start.4
  90.7 1.0 copy-start.22
  92.2 12.6 %copy-start.13 = (f32[3,1,1]{2,0,1:T(4,128)S(1)}, f32[3,1,1]{2,0,1:T(4,128)}, u32[]{:S(2)}) copy-start(f32[3,1,1]{2,0,1:T(4,128)} %copy-done.12) | copy-start | bytes 40
  92.2 12.7 %copy-start.9 = (f32[192]{0:T(256)S(1)}, f32[192]{0:T(256)}, u32[]{:S(2)}) copy-start(f32[192]{0:T(256)} %copy-done.8) | copy-start | bytes 2308
  92.3 4.4 %collective-permute-start.11 = (f32[3,1,450]{2,0,1:T(4,128)S(1)}, f32[3,1,450]{2,0,1:T(4,128)S(1)}, u32[]{:S(2)}, u32[]{:S(2)}) collective-permute-start(f32[3,1,450]{2,0,1:T(4,128)S(1)} %copy.206), channel_id=1, source_target_pairs={{1,0},{2,1},{3,2},{4,3},{5,4},{6,5},{7,6},{8,7},{9,8},{10,9},{11,1... | collective-permute-start | bytes 16208 | tf_op jit(solution)/shard_map/ppermute | solution.py:26
  96.7 8.0 %collective-permute-start.10 = (f32[3,1,450]{2,0,1:T(4,128)S(1)}, f32[3,1,450]{2,0,1:T(4,128)S(1)}, u32[]{:S(2)}, u32[]{:S(2)}) collective-permute-start(f32[3,1,450]{2,0,1:T(4,128)S(1)} %get-tuple-element.38), channel_id=1, source_target_pairs={{0,1},{1,2},{2,3},{3,4},{4,5},{5,6},{6,7},{7,8},{8,9},{9,10},{10,1... | collective-permute-start | bytes 16208 | tf_op jit(solution)/shard_map/ppermute | solution.py:25
  104.9 0.7 copy-start.17
  104.9 0.7 copy-start.19
  105.6 0.8 copy-start.15
  107.5 17.0 %copy-start.11 = (f32[3,1,1]{2,1,0:T(1,128)S(1)}, f32[3,1,1]{2,1,0:T(1,128)}, u32[]{:S(2)}) copy-start(f32[3,1,1]{2,1,0:T(1,128)} %copy-done.10) | copy-start | bytes 40
  107.5 4.4 %collective-permute-start.15 = (f32[3,1,450]{2,1,0:T(1,128)S(1)}, f32[3,1,450]{2,1,0:T(1,128)S(1)}, u32[]{:S(2)}, u32[]{:S(2)}) collective-permute-start(f32[3,1,450]{2,1,0:T(1,128)S(1)} %slice.673), channel_id=1, source_target_pairs={{1,0},{2,1},{3,2},{4,3},{5,4},{6,5},{7,6},{8,7},{9,8},{10,9},{11,1... | collective-permute-start | bytes 16208 | tf_op jit(solution)/shard_map/ppermute | solution.py:26
  111.9 8.0 %collective-permute-start.14 = (f32[3,1,450]{2,1,0:T(1,128)S(1)}, f32[3,1,450]{2,1,0:T(1,128)S(1)}, u32[]{:S(2)}, u32[]{:S(2)}) collective-permute-start(f32[3,1,450]{2,1,0:T(1,128)S(1)} %get-tuple-element.18), channel_id=1, source_target_pairs={{0,1},{1,2},{2,3},{3,4},{4,5},{5,6},{6,7},{7,8},{8,9},{9,10},{10,1... | collective-permute-start | bytes 16208 | tf_op jit(solution)/shard_map/ppermute | solution.py:25
  114.3 8.6 %collective-permute-start.12 = (f32[3,192,1]{2,1,0:T(8,128)S(1)}, f32[3,192,1]{2,1,0:T(8,128)S(1)}, u32[]{:S(2)}, u32[]{:S(2)}) collective-permute-start(f32[3,192,1]{2,1,0:T(8,128)S(1)} %get-tuple-element.19), channel_id=1, source_target_pairs={{16,0},{32,16},{48,32},{64,48},{80,64},{96,80},{112,96},{128,112},... | collective-permute-start | bytes 6920 | tf_op jit(solution)/shard_map/ppermute | solution.py:26
  118.6 5.9 %collective-permute-start.13 = (f32[3,192,1]{2,1,0:T(8,128)S(1)}, f32[3,192,1]{2,1,0:T(8,128)S(1)}, u32[]{:S(2)}, u32[]{:S(2)}) collective-permute-start(f32[3,192,1]{2,1,0:T(8,128)S(1)} %get-tuple-element.20), channel_id=1, source_target_pairs={{0,16},{16,32},{32,48},{48,64},{64,80},{80,96},{96,112},{112,128},... | collective-permute-start | bytes 6920 | tf_op jit(solution)/shard_map/ppermute | solution.py:25
  125.9 1.6 copy-start.5

commit v7 on v5

--- a/solution.py
+++ b/solution.py
@@ -87,7 +87,9 @@
     if not with_halos:
         smooth = expand(scaled, table)
         return jnp.where(active[None, :, None], smooth, fields), None, None
-    wide = expand(scaled, wide_table)
+    pole_coeffs = scaled[:, :2, :] * half_turn_signs()[None, None, :]
+    both = expand(jnp.concatenate([scaled, pole_coeffs], axis=1), wide_table)
+    wide = both[:, :rows, :]
     smooth = wide[:, :, 1:-1]
     filtered = jnp.where(active[None, :, None], smooth, fields)
     edges = spread[:, block:block + count * rows].reshape(devices, count, rows)
@@ -97,7 +99,7 @@
     far_raw = rows_far[(lon_index + devices // 2) % devices]
     west = jnp.where(active[None, :], wide[:, :, 0], west_raw)[:, :, None]
     east = jnp.where(active[None, :], wide[:, :, -1], east_raw)[:, :, None]
-    far_wide = expand(scaled[:, :2, :] * half_turn_signs()[None, None, :], wide_table)
+    far_wide = both[:, rows:, :]
     far = jnp.where(active[0], far_wide[:, 0, 1:-1], far_raw)
     return filtered, (west, east, far), (far_wide, wide[:, 0, :])
 

time: 161 us -> 174 us (1.081)
  local copies, waits for them, and re-layouts: 22.8 us -> 31.9 us
  other arithmetic: 24.3 us -> 33.2 us
  waiting for transfers between devices: 31 us -> 26.5 us
    all_to_all x1, waiting for transfers between devices: 7.45 us -> 4.25 us  [low_pass(): lax.all_to_all(partial, 'lon', split_axis=1, concat_axis=0, tiled=True)]
    ppermute x7, waiting for transfers between devices: 6.83 us -> 4.08 us  [with_halo(): after = lax.ppermute(first, axis, down)]
    reshape x2 -> x4, local copies, waits for them, and re-layouts: 2.09 us -> 3.64 us  [low_pass(): coeffs = jnp.moveaxis(coeffs, 0, 1).reshape(count, rows, modes)]
    unnamed x99 -> x75, local copies, waits for them, and re-layouts: 7.14 us -> 7 us
  transfers between devices with their start and end apart: 18 -> 18, of which waited for: 9 -> 8; matrix products, arithmetic and copies ran while one was open for 7% -> 13% of each run, Pallas kernels for 0% -> 0%
where the time goes in v7:
time: 174 us; the launch traced here: 172 us
  starting transfers between devices  49.2 us (28%)
  other arithmetic  33.2 us (19%)
  local copies, waits for them, and re-layouts  31.9 us (18%)
  waiting for transfers between devices  26.5 us (15%)
  blocking collectives  22.5 us (13%)
  matrix products  5.97 us (3%)
  between operations  2.89 us (2%)
    ppermute x7, starting transfers between devices, with_halo(): after = lax.ppermute(first, axis, down)  21.4 us
    ppermute x7, starting transfers between devices, with_halo(): before = lax.ppermute(last, axis, up)  13.8 us
    ppermute x7, waiting for transfers between devices, with_halo(): before = lax.ppermute(last, axis, up)  13.1 us
    all_to_all x1, blocking collectives, low_pass(): lax.all_to_all(partial, 'lon', split_axis=1, concat_axis=0, tiled=True)  11.8 us
    all_to_all x1, blocking collectives, low_pass(): lax.all_to_all(jnp.concatenate(payload, axis=1), 'lon', split_axis=0, con...  10.7 us
    all_to_all x1, starting transfers between devices, low_pass(): lax.all_to_all(partial, 'lon', split_axis=1, concat_axis=0, tiled=True)  7.04 us
    unnamed x75, local copies, waits for them, and re-layouts  7 us
    all_to_all x1, waiting for transfers between devices, low_pass(): lax.all_to_all(jnp.concatenate(payload, axis=1), 'lon', split_axis=0, con...  5.07 us
  transfers between devices with their start and end apart: 18, of which 8 were waited for; matrix products, arithmetic and copies ran while one was open for 13% of the time, Pallas kernels for 0%

profile of v7, /device:TPU:17, one launch (start us, length us, event | category | flops | bytes accessed | tf_op | source)
XLA Modules:
  0.0 172.1 jit_solution(958507655544824600)
XLA Ops:
  0.6 1.3 pad_maximum_fusion.4
  2.0 7.4 %collective-permute-start.4 = (f32[3,1,450]{2,0,1:T(4,128)S(1)}, f32[3,1,450]{2,0,1:T(4,128)S(1)}, u32[]{:S(2)}, u32[]{:S(2)}) collective-permute-start(f32[3,1,450]{2,0,1:T(4,128)S(1)} %copy.181), channel_id=1, source_target_pairs={{1,0},{2,1},{3,2},{4,3},{5,4},{6,5},{7,6},{8,7},{9,8},{10,9},{11,1... | collective-permute-start | bytes 16208 | tf_op jit(solution)/shard_map/ppermute | solution.py:26
  9.4 2.8 %collective-permute-start.2 = (f32[3,450]{1,0:T(4,128)S(1)}, f32[3,450]{1,0:T(4,128)S(1)}, u32[]{:S(2)}, u32[]{:S(2)}) collective-permute-start(f32[3,450]{1,0:T(4,128)S(1)} %bitcast.128), channel_id=1, source_target_pairs={{0,128},{16,144},{32,160},{48,176},{64,192},{80,208},{96,224},{112... | collective-permute-start | bytes 16208 | tf_op jit(solution)/shard_map/ppermute | solution.py:33
  12.4 1.3 collective-permute-start
  13.7 1.9 %collective-permute-start.1 = (f32[3,192,1]{2,1,0:T(8,128)S(1)}, f32[3,192,1]{2,1,0:T(8,128)S(1)}, u32[]{:S(2)}, u32[]{:S(2)}) collective-permute-start(f32[3,192,1]{2,1,0:T(8,128)S(1)} %get-tuple-element.32), channel_id=1, source_target_pairs={{0,16},{16,32},{32,48},{48,64},{64,80},{80,96},{96,112},{112,128},... | collective-permute-start | bytes 6920 | tf_op jit(solution)/shard_map/ppermute | solution.py:25
  16.5 1.3 fusion.100
  20.5 1.9 %collective-permute-start.3 = (f32[3,1,450]{2,0,1:T(4,128)S(1)}, f32[3,1,450]{2,0,1:T(4,128)S(1)}, u32[]{:S(2)}, u32[]{:S(2)}) collective-permute-start(f32[3,1,450]{2,0,1:T(4,128)S(1)} %get-tuple-element.43), channel_id=1, source_target_pairs={{0,1},{1,2},{2,3},{3,4},{4,5},{5,6},{6,7},{7,8},{8,9},{9,10},{10,1... | collective-permute-start | bytes 16208 | tf_op jit(solution)/shard_map/ppermute | solution.py:25
  23.8 4.8 %collective-permute-done.3 = f32[3,1,450]{2,0,1:T(4,128)S(1)} collective-permute-done((f32[3,1,450]{2,0,1:T(4,128)S(1)}, f32[3,1,450]{2,0,1:T(4,128)S(1)}, u32[]{:S(2)}, u32[]{:S(2)}) %collective-permute-start.3) | collective-permute-done | bytes 5432 | tf_op jit(solution)/shard_map/ppermute | solution.py:25
  30.6 1.9 %collective-permute-start.9 = (f32[3,1,450]{2,0,1:T(4,128)S(1)}, f32[3,1,450]{2,0,1:T(4,128)S(1)}, u32[]{:S(2)}, u32[]{:S(2)}) collective-permute-start(f32[3,1,450]{2,0,1:T(4,128)S(1)} %copy.182), channel_id=1, source_target_pairs={{1,0},{2,1},{3,2},{4,3},{5,4},{6,5},{7,6},{8,7},{9,8},{10,9},{11,1... | collective-permute-start | bytes 16208 | tf_op jit(solution)/shard_map/ppermute | solution.py:26
  33.0 2.3 %collective-permute-start.5 = (f32[3,192,1]{2,1,0:T(8,128)S(1)}, f32[3,192,1]{2,1,0:T(8,128)S(1)}, u32[]{:S(2)}, u32[]{:S(2)}) collective-permute-start(f32[3,192,1]{2,1,0:T(8,128)S(1)} %get-tuple-element.25), channel_id=1, source_target_pairs={{16,0},{32,16},{48,32},{64,48},{80,64},{96,80},{112,96},{128,112},... | collective-permute-start | bytes 6920 | tf_op jit(solution)/shard_map/ppermute | solution.py:26
  35.3 3.8 %collective-permute-start.8 = (f32[3,1,450]{2,0,1:T(4,128)S(1)}, f32[3,1,450]{2,0,1:T(4,128)S(1)}, u32[]{:S(2)}, u32[]{:S(2)}) collective-permute-start(f32[3,1,450]{2,0,1:T(4,128)S(1)} %get-tuple-element.38), channel_id=1, source_target_pairs={{0,1},{1,2},{2,3},{3,4},{4,5},{5,6},{6,7},{7,8},{8,9},{9,10},{10,1... | collective-permute-start | bytes 16208 | tf_op jit(solution)/shard_map/ppermute | solution.py:25
  39.3 4.1 %collective-permute-done.8 = f32[3,1,450]{2,0,1:T(4,128)S(1)} collective-permute-done((f32[3,1,450]{2,0,1:T(4,128)S(1)}, f32[3,1,450]{2,0,1:T(4,128)S(1)}, u32[]{:S(2)}, u32[]{:S(2)}) %collective-permute-start.8) | collective-permute-done | bytes 5432 | tf_op jit(solution)/shard_map/ppermute | solution.py:25
  46.7 1.0 slice_reduce_fusion.1
  47.7 1.5 fusion.88
  49.2 2.2 %copy.123 = f32[3,192,130]{2,0,1:T(4,128)} copy(f32[3,192,130]{1,2,0:T(8,128)} %fusion.88) | data formatting | bytes 599040 | tf_op jit(solution)/shard_map/fnw,kw->fnk/dot_general | solution.py:59
  51.4 2.9 %reshape.465 = f32[16,1,4680]{2,1,0:T(1,128)} reshape(f32[192,3,130]{2,1,0:T(4,128)} %bitcast.118) | data formatting | bytes 599040
  54.3 7.0 %all-to-all-start = ((f32[16,1,4680]{2,1,0:T(1,128)}), f32[16,1,4680]{2,1,0:T(1,128)}, u32[]{:S(2)}, u32[]{:S(2)}) async-start(f32[16,1,4680]{2,1,0:T(1,128)} %reshape.465), calls=%async_computation | async-start | bytes 606208 | tf_op jit(solution)/shard_map/all_to_all | solution.py:73
  65.0 4.2 %all-to-all-done = f32[16,1,4680]{2,1,0:T(1,128)} async-done(((f32[16,1,4680]{2,1,0:T(1,128)}), f32[16,1,4680]{2,1,0:T(1,128)}, u32[]{:S(2)}, u32[]{:S(2)}) %all-to-all-start) | async-done | bytes 299552 | tf_op jit(solution)/shard_map/all_to_all | solution.py:73
  69.8 2.4 %reduce.11 = f32[16,4680]{1,0:T(8,128)S(1)} reduce(f32[16,1,4680]{2,1,0:T(1,128)} %all-to-all-done, f32[]{:T(128)} %broadcast.434), dimensions={1}, to_apply=%all_to_all.30.reduce_sub_computation | reduce | bytes 599044 | tf_op jit(solution)/shard_map/all_to_all | solution.py:73
  73.6 1.1 all_to_all.32
  74.6 3.8 %all-to-all-start.1 = ((f32[16,1,6606]{2,1,0:T(1,128)}), f32[16,1,6606]{2,1,0:T(1,128)S(1)}, u32[]{:S(2)}, u32[]{:S(2)}) async-start(f32[16,1,6606]{2,1,0:T(1,128)} %all_to_all.32), calls=%async_computation.1 | async-start | bytes 851968 | tf_op jit(solution)/shard_map/all_to_all | solution.py:81
  81.0 1.3 fusion.96
  82.3 5.1 %all-to-all-done.1 = f32[16,1,6606]{2,1,0:T(1,128)S(1)} async-done(((f32[16,1,6606]{2,1,0:T(1,128)}), f32[16,1,6606]{2,1,0:T(1,128)S(1)}, u32[]{:S(2)}, u32[]{:S(2)}) %all-to-all-start.1) | async-done | bytes 422816 | tf_op jit(solution)/shard_map/all_to_all | solution.py:81
  89.0 1.7 reshape.453
  91.6 1.2 reshape.454
  96.4 1.9 %collective-permute-start.11 = (f32[3,1,450]{2,0,1:T(4,128)S(1)}, f32[3,1,450]{2,0,1:T(4,128)S(1)}, u32[]{:S(2)}, u32[]{:S(2)}) collective-permute-start(f32[3,1,450]{2,0,1:T(4,128)S(1)} %copy.161), channel_id=1, source_target_pairs={{1,0},{2,1},{3,2},{4,3},{5,4},{6,5},{7,6},{8,7},{9,8},{10,9},{11,1... | collective-permute-start | bytes 16208 | tf_op jit(solution)/shard_map/ppermute | solution.py:26
  99.2 1.4 slice_select_fusion.2
  100.6 1.6 multiply_subtract_fusion
  102.2 3.6 %collective-permute-start.10 = (f32[3,1,450]{2,0,1:T(4,128)S(1)}, f32[3,1,450]{2,0,1:T(4,128)S(1)}, u32[]{:S(2)}, u32[]{:S(2)}) collective-permute-start(f32[3,1,450]{2,0,1:T(4,128)S(1)} %get-tuple-element.36), channel_id=1, source_target_pairs={{0,1},{1,2},{2,3},{3,4},{4,5},{5,6},{6,7},{7,8},{8,9},{9,10},{10,1... | collective-permute-start | bytes 16208 | tf_op jit(solution)/shard_map/ppermute | solution.py:25
  105.8 1.6 multiply_subtract_fusion.1
  108.3 1.0 slice.643
  113.0 4.7 %collective-permute-start.15 = (f32[3,1,450]{2,1,0:T(1,128)S(1)}, f32[3,1,450]{2,1,0:T(1,128)S(1)}, u32[]{:S(2)}, u32[]{:S(2)}) collective-permute-start(f32[3,1,450]{2,1,0:T(1,128)S(1)} %slice.676), channel_id=1, source_target_pairs={{1,0},{2,1},{3,2},{4,3},{5,4},{6,5},{7,6},{8,7},{9,8},{10,9},{11,1... | collective-permute-start | bytes 16208 | tf_op jit(solution)/shard_map/ppermute | solution.py:26
  117.8 2.0 %fusion.113 = f32[1,1,450]{2,1,0:T(1,128)S(1)} fusion(f32[3,194,452]{2,1,0:T(8,128)} %copy-done.3, f32[3,1,452]{2,1,0:T(1,128)S(1)} %copy-done.13, f32[]{:T(128)} %bitcast.24, f32[]{:T(128)} %bitcast.23, f32[]{:T(128)} %bitcast.22), kind=kLoop, calls=%fused_computation.248 | loop fusion | flops 5400 | bytes 16212 | tf_op jit(solution)/shard_map/mul | solution.py:141
  119.9 1.9 %collective-permute-start.14 = (f32[3,1,450]{2,1,0:T(1,128)S(1)}, f32[3,1,450]{2,1,0:T(1,128)S(1)}, u32[]{:S(2)}, u32[]{:S(2)}) collective-permute-start(f32[3,1,450]{2,1,0:T(1,128)S(1)} %get-tuple-element.18), channel_id=1, source_target_pairs={{0,1},{1,2},{2,3},{3,4},{4,5},{5,6},{6,7},{7,8},{8,9},{9,10},{10,1... | collective-permute-start | bytes 16208 | tf_op jit(solution)/shard_map/ppermute | solution.py:25
  122.0 1.8 %collective-permute-start.12 = (f32[3,192,1]{2,1,0:T(8,128)S(1)}, f32[3,192,1]{2,1,0:T(8,128)S(1)}, u32[]{:S(2)}, u32[]{:S(2)}) collective-permute-start(f32[3,192,1]{2,1,0:T(8,128)S(1)} %get-tuple-element.19), channel_id=1, source_target_pairs={{16,0},{32,16},{48,32},{64,48},{80,64},{96,80},{112,96},{128,112},... | collective-permute-start | bytes 6920 | tf_op jit(solution)/shard_map/ppermute | solution.py:26
  124.4 3.4 %collective-permute-done.14 = f32[3,1,450]{2,1,0:T(1,128)S(1)} collective-permute-done((f32[3,1,450]{2,1,0:T(1,128)S(1)}, f32[3,1,450]{2,1,0:T(1,128)S(1)}, u32[]{:S(2)}, u32[]{:S(2)}) %collective-permute-start.14) | collective-permute-done | bytes 5432 | tf_op jit(solution)/shard_map/ppermute | solution.py:25
  128.7 3.2 %collective-permute-done.12 = f32[3,192,1]{2,1,0:T(8,128)S(1)} collective-permute-done((f32[3,192,1]{2,1,0:T(8,128)S(1)}, f32[3,192,1]{2,1,0:T(8,128)S(1)}, u32[]{:S(2)}, u32[]{:S(2)}) %collective-permute-start.12) | collective-permute-done | bytes 2336 | tf_op jit(solution)/shard_map/ppermute | solution.py:26
  135.2 1.6 fusion.87
  136.7 1.4 copy.146
  138.1 1.0 reshape.467
  139.1 11.8 %all_to_all.42 = f32[16,1,4680]{2,1,0:T(1,128)S(1)} all-to-all(f32[16,1,4680]{2,1,0:T(1,128)S(1)} %reshape.467), channel_id=1, replica_groups=mesh['lon'=16,'lat'=16] {'lon'}, dimensions={0} | all-to-all | bytes 599040 | tf_op jit(solution)/shard_map/all_to_all | solution.py:73
  150.9 1.4 reduce.12
  153.7 10.7 %all_to_all.43 = f32[16,1,4680]{2,1,0:T(1,128)S(1)} all-to-all(f32[16,1,4680]{2,1,0:T(1,128)S(1)} %broadcast_in_dim.159), channel_id=1, replica_groups=mesh['lon'=16,'lat'=16] {'lon'}, dimensions={0} | all-to-all | bytes 599040 | tf_op jit(solution)/shard_map/all_to_all | solution.py:81
  165.9 1.0 copy.148
  166.8 1.2 reshape.458
  168.1 1.0 copy.149
  169.1 2.0 %convolution_select_fusion = f32[3,192,450]{2,1,0:T(8,128)S(1)} fusion(pred[192]{0:T(512)(128)(4,1)S(1)} %copy-done.27, f32[3,192,130]{1,2,0:T(8,128)} %copy.149, f32[192,130]{0,1:T(8,128)} %copy-done.9, f32[65,450]{1,0:T(8,128)} %get-tuple-element.52, f32[65,450]{1,0:T(8,128)} %get-tuple-element.51, f32[3,192,450]{2,1,0:T(8,128)S(1)} %slice_select_fusion, ...), kind=kOutput, calls=%fused_computation.16 | convolution fusion | flops 203605376 | bytes 3743952 | tf_op jit(solution)/shard_map/fnk,kw->fnw/dot_general | solution.py:63
  171.1 1.0 slice_bitcast_fusion
  (176 shorter events, 36.8 us)
Async XLA Ops:
  2.0 17.1 %copy-start.31 = (s32[512]{0:T(512)S(1)}, s32[512]{0:T(512)}, u32[]{:S(2)}) copy-start(s32[512]{0:T(512)} %param.12) | copy-start | bytes 6148
  2.0 21.3 %copy-start = (f32[192,450]{1,0:T(8,128)S(1)}, f32[192,450]{1,0:T(8,128)}, u32[]{:S(2)}) copy-start(f32[192,450]{1,0:T(8,128)} %param.11) | copy-start | bytes 1036804
  2.0 21.3 %copy-start.1 = (f32[192,450]{1,0:T(8,128)S(1)}, f32[192,450]{1,0:T(8,128)}, u32[]{:S(2)}) copy-start(f32[192,450]{1,0:T(8,128)} %param.10) | copy-start | bytes 1036804
  2.0 21.3 %copy-start.2 = (f32[192,450]{1,0:T(8,128)S(1)}, f32[192,450]{1,0:T(8,128)}, u32[]{:S(2)}) copy-start(f32[192,450]{1,0:T(8,128)} %param.9) | copy-start | bytes 1036804
  2.0 18.4 %collective-permute-start.4 = (f32[3,1,450]{2,0,1:T(4,128)S(1)}, f32[3,1,450]{2,0,1:T(4,128)S(1)}, u32[]{:S(2)}, u32[]{:S(2)}) collective-permute-start(f32[3,1,450]{2,0,1:T(4,128)S(1)} %copy.181), channel_id=1, source_target_pairs={{1,0},{2,1},{3,2},{4,3},{5,4},{6,5},{7,6},{8,7},{9,8},{10,9},{11,1... | collective-permute-start | bytes 16208 | tf_op jit(solution)/shard_map/ppermute | solution.py:26
  9.4 14.4 %collective-permute-start.2 = (f32[3,450]{1,0:T(4,128)S(1)}, f32[3,450]{1,0:T(4,128)S(1)}, u32[]{:S(2)}, u32[]{:S(2)}) collective-permute-start(f32[3,450]{1,0:T(4,128)S(1)} %bitcast.128), channel_id=1, source_target_pairs={{0,128},{16,144},{32,160},{48,176},{64,192},{80,208},{96,224},{112... | collective-permute-start | bytes 16208 | tf_op jit(solution)/shard_map/ppermute | solution.py:33
  12.4 10.9 %collective-permute-start = (f32[3,192,1]{2,1,0:T(8,128)S(1)}, f32[3,192,1]{2,1,0:T(8,128)S(1)}, u32[]{:S(2)}, u32[]{:S(2)}) collective-permute-start(f32[3,192,1]{2,1,0:T(8,128)S(1)} %get-tuple-element.31), channel_id=1, source_target_pairs={{16,0},{32,16},{48,32},{64,48},{80,64},{96,80},{112,96},{128,112},... | collective-permute-start | bytes 6920 | tf_op jit(solution)/shard_map/ppermute | solution.py:26
  13.7 9.5 %collective-permute-start.1 = (f32[3,192,1]{2,1,0:T(8,128)S(1)}, f32[3,192,1]{2,1,0:T(8,128)S(1)}, u32[]{:S(2)}, u32[]{:S(2)}) collective-permute-start(f32[3,192,1]{2,1,0:T(8,128)S(1)} %get-tuple-element.32), channel_id=1, source_target_pairs={{0,16},{16,32},{32,48},{48,64},{64,80},{80,96},{96,112},{112,128},... | collective-permute-start | bytes 6920 | tf_op jit(solution)/shard_map/ppermute | solution.py:25
  15.7 4.8 %copy-start.29 = (f32[194]{0:T(256)}, f32[194]{0:T(256)S(1)}, u32[]{:S(2)}) copy-start(f32[194]{0:T(256)S(1)} %get-tuple-element.63) | copy-start | bytes 2332
  15.8 28.2 %copy-start.18 = (f32[192]{0:T(256)}, f32[192]{0:T(256)S(1)}, u32[]{:S(2)}) copy-start(f32[192]{0:T(256)S(1)} %get-tuple-element.58) | copy-start | bytes 2308
  15.8 28.2 %copy-start.20 = (f32[192]{0:T(256)}, f32[192]{0:T(256)S(1)}, u32[]{:S(2)}) copy-start(f32[192]{0:T(256)S(1)} %get-tuple-element.59) | copy-start | bytes 2308
  15.8 29.1 %copy-start.16 = (f32[192]{0:T(256)}, f32[192]{0:T(256)S(1)}, u32[]{:S(2)}) copy-start(f32[192]{0:T(256)S(1)} %get-tuple-element.10) | copy-start | bytes 2308
  20.5 8.2 %copy-start.22 = (f32[3]{0:T(128)S(1)}, f32[3]{0:T(128)}, u32[]{:S(2)}) copy-start(f32[3]{0:T(128)} %constant.144.clone) | copy-start | bytes 40
  20.5 8.1 %collective-permute-start.3 = (f32[3,1,450]{2,0,1:T(4,128)S(1)}, f32[3,1,450]{2,0,1:T(4,128)S(1)}, u32[]{:S(2)}, u32[]{:S(2)}) collective-permute-start(f32[3,1,450]{2,0,1:T(4,128)S(1)} %get-tuple-element.43), channel_id=1, source_target_pairs={{0,1},{1,2},{2,3},{3,4},{4,5},{5,6},{6,7},{7,8},{8,9},{9,10},{10,1... | collective-permute-start | bytes 16208 | tf_op jit(solution)/shard_map/ppermute | solution.py:25
  28.7 10.5 %copy-start.14 = (f32[3,1,1]{2,0,1:T(4,128)}, f32[3,1,1]{2,0,1:T(4,128)S(1)}, u32[]{:S(2)}) copy-start(f32[3,1,1]{2,0,1:T(4,128)S(1)} %broadcast.385.clone) | copy-start | bytes 40
  30.6 4.7 %collective-permute-start.9 = (f32[3,1,450]{2,0,1:T(4,128)S(1)}, f32[3,1,450]{2,0,1:T(4,128)S(1)}, u32[]{:S(2)}, u32[]{:S(2)}) collective-permute-start(f32[3,1,450]{2,0,1:T(4,128)S(1)} %copy.182), channel_id=1, source_target_pairs={{1,0},{2,1},{3,2},{4,3},{5,4},{6,5},{7,6},{8,7},{9,8},{10,9},{11,1... | collective-permute-start | bytes 16208 | tf_op jit(solution)/shard_map/ppermute | solution.py:26
  32.7 6.5 %collective-permute-start.7 = (f32[3,450]{1,0:T(4,128)S(1)}, f32[3,450]{1,0:T(4,128)S(1)}, u32[]{:S(2)}, u32[]{:S(2)}) collective-permute-start(f32[3,450]{1,0:T(4,128)S(1)} %bitcast.129), channel_id=1, source_target_pairs={{0,128},{16,144},{32,160},{48,176},{64,192},{80,208},{96,224},{112... | collective-permute-start | bytes 16208 | tf_op jit(solution)/shard_map/ppermute | solution.py:33
  33.0 10.4 %collective-permute-start.5 = (f32[3,192,1]{2,1,0:T(8,128)S(1)}, f32[3,192,1]{2,1,0:T(8,128)S(1)}, u32[]{:S(2)}, u32[]{:S(2)}) collective-permute-start(f32[3,192,1]{2,1,0:T(8,128)S(1)} %get-tuple-element.25), channel_id=1, source_target_pairs={{16,0},{32,16},{48,32},{64,48},{80,64},{96,80},{112,96},{128,112},... | collective-permute-start | bytes 6920 | tf_op jit(solution)/shard_map/ppermute | solution.py:26
  35.3 8.1 %collective-permute-start.6 = (f32[3,192,1]{2,1,0:T(8,128)S(1)}, f32[3,192,1]{2,1,0:T(8,128)S(1)}, u32[]{:S(2)}, u32[]{:S(2)}) collective-permute-start(f32[3,192,1]{2,1,0:T(8,128)S(1)} %get-tuple-element.26), channel_id=1, source_target_pairs={{0,16},{16,32},{32,48},{48,64},{64,80},{80,96},{96,112},{112,128},... | collective-permute-start | bytes 6920 | tf_op jit(solution)/shard_map/ppermute | solution.py:25
  35.3 8.0 %collective-permute-start.8 = (f32[3,1,450]{2,0,1:T(4,128)S(1)}, f32[3,1,450]{2,0,1:T(4,128)S(1)}, u32[]{:S(2)}, u32[]{:S(2)}) collective-permute-start(f32[3,1,450]{2,0,1:T(4,128)S(1)} %get-tuple-element.38), channel_id=1, source_target_pairs={{0,1},{1,2},{2,3},{3,4},{4,5},{5,6},{6,7},{7,8},{8,9},{9,10},{10,1... | collective-permute-start | bytes 16208 | tf_op jit(solution)/shard_map/ppermute | solution.py:25
  46.4 1.3 copy-start.4
  46.4 1.3 copy-start.6
  54.3 14.9 %all-to-all-start = ((f32[16,1,4680]{2,1,0:T(1,128)}), f32[16,1,4680]{2,1,0:T(1,128)}, u32[]{:S(2)}, u32[]{:S(2)}) async-start(f32[16,1,4680]{2,1,0:T(1,128)} %reshape.465), calls=%async_computation | async-start | bytes 606208 | tf_op jit(solution)/shard_map/all_to_all | solution.py:73
  73.4 5.6 %copy-start.30 = (f32[194]{0:T(256)S(1)}, f32[194]{0:T(256)}, u32[]{:S(2)}) copy-start(f32[194]{0:T(256)} %copy-done.29) | copy-start | bytes 2332
  73.4 7.5 %copy-start.12 = (f32[192,65]{0,1:T(8,128)S(1)}, f32[192,65]{0,1:T(8,128)}, u32[]{:S(2)}) copy-start(f32[192,65]{0,1:T(8,128)} %fusion.104) | copy-start | bytes 149764
  73.6 7.4 %copy-start.28 = (s32[452]{0:T(512)S(1)}, s32[452]{0:T(512)}, u32[]{:S(2)}) copy-start(s32[452]{0:T(512)} %add_select_fusion.2) | copy-start | bytes 5428
  74.6 12.7 %all-to-all-start.1 = ((f32[16,1,6606]{2,1,0:T(1,128)}), f32[16,1,6606]{2,1,0:T(1,128)S(1)}, u32[]{:S(2)}, u32[]{:S(2)}) async-start(f32[16,1,6606]{2,1,0:T(1,128)} %all_to_all.32), calls=%async_computation.1 | async-start | bytes 851968 | tf_op jit(solution)/shard_map/all_to_all | solution.py:81
  81.0 12.1 %copy-start.9 = (f32[192,130]{0,1:T(8,128)}, f32[192,130]{0,1:T(8,128)S(1)}, u32[]{:S(2)}) copy-start(f32[192,130]{0,1:T(8,128)S(1)} %pad_maximum_fusion.45) | copy-start | bytes 299524
  93.1 1.0 copy-start.11
  93.6 1.4 copy-start.23
  93.6 2.2 %copy-start.25 = (pred[192]{0:T(512)(128)(4,1)S(1)}, pred[192]{0:T(512)(128)(4,1)}, u32[]{:S(2)}) copy-start(pred[192]{0:T(512)(128)(4,1)} %add_compare_fusion) | copy-start | bytes 580
  95.0 1.3 copy-start.3
  96.3 4.3 %copy-start.13 = (f32[3,1,452]{2,1,0:T(1,128)S(1)}, f32[3,1,452]{2,1,0:T(1,128)}, u32[]{:S(2)}) copy-start(f32[3,1,452]{2,1,0:T(1,128)} %slice_multiply_fusion.1) | copy-start | bytes 16276
  96.3 13.9 %copy-start.24 = (f32[3]{0:T(128)S(1)}, f32[3]{0:T(128)}, u32[]{:S(2)}) copy-start(f32[3]{0:T(128)} %constant.144.clone) | copy-start | bytes 40
  96.3 13.9 %copy-start.26 = (pred[192]{0:T(512)(128)(4,1)S(1)}, pred[192]{0:T(512)(128)(4,1)}, u32[]{:S(2)}) copy-start(pred[192]{0:T(512)(128)(4,1)} %add_compare_fusion) | copy-start | bytes 580
  96.3 14.0 %copy-start.15 = (f32[3,1,1]{2,0,1:T(4,128)S(1)}, f32[3,1,1]{2,0,1:T(4,128)}, u32[]{:S(2)}) copy-start(f32[3,1,1]{2,0,1:T(4,128)} %copy-done.14) | copy-start | bytes 40
  96.3 14.1 %copy-start.19 = (f32[192]{0:T(256)S(1)}, f32[192]{0:T(256)}, u32[]{:S(2)}) copy-start(f32[192]{0:T(256)} %copy-done.18) | copy-start | bytes 2308
  96.4 14.1 %copy-start.21 = (f32[192]{0:T(256)S(1)}, f32[192]{0:T(256)}, u32[]{:S(2)}) copy-start(f32[192]{0:T(256)} %copy-done.20) | copy-start | bytes 2308
  96.4 5.8 %collective-permute-start.11 = (f32[3,1,450]{2,0,1:T(4,128)S(1)}, f32[3,1,450]{2,0,1:T(4,128)S(1)}, u32[]{:S(2)}, u32[]{:S(2)}) collective-permute-start(f32[3,1,450]{2,0,1:T(4,128)S(1)} %copy.161), channel_id=1, source_target_pairs={{1,0},{2,1},{3,2},{4,3},{5,4},{6,5},{7,6},{8,7},{9,8},{10,9},{11,1... | collective-permute-start | bytes 16208 | tf_op jit(solution)/shard_map/ppermute | solution.py:26
  102.2 8.0 %collective-permute-start.10 = (f32[3,1,450]{2,0,1:T(4,128)S(1)}, f32[3,1,450]{2,0,1:T(4,128)S(1)}, u32[]{:S(2)}, u32[]{:S(2)}) collective-permute-start(f32[3,1,450]{2,0,1:T(4,128)S(1)} %get-tuple-element.36), channel_id=1, source_target_pairs={{0,1},{1,2},{2,3},{3,4},{4,5},{5,6},{6,7},{7,8},{8,9},{9,10},{10,1... | collective-permute-start | bytes 16208 | tf_op jit(solution)/shard_map/ppermute | solution.py:25
  109.4 1.9 %copy-start.17 = (f32[192]{0:T(256)S(1)}, f32[192]{0:T(256)}, u32[]{:S(2)}) copy-start(f32[192]{0:T(256)} %copy-done.16) | copy-start | bytes 2308
  113.0 6.8 %collective-permute-start.15 = (f32[3,1,450]{2,1,0:T(1,128)S(1)}, f32[3,1,450]{2,1,0:T(1,128)S(1)}, u32[]{:S(2)}, u32[]{:S(2)}) collective-permute-start(f32[3,1,450]{2,1,0:T(1,128)S(1)} %slice.676), channel_id=1, source_target_pairs={{1,0},{2,1},{3,2},{4,3},{5,4},{6,5},{7,6},{8,7},{9,8},{10,9},{11,1... | collective-permute-start | bytes 16208 | tf_op jit(solution)/shard_map/ppermute | solution.py:26
  119.9 8.0 %collective-permute-start.14 = (f32[3,1,450]{2,1,0:T(1,128)S(1)}, f32[3,1,450]{2,1,0:T(1,128)S(1)}, u32[]{:S(2)}, u32[]{:S(2)}) collective-permute-start(f32[3,1,450]{2,1,0:T(1,128)S(1)} %get-tuple-element.18), channel_id=1, source_target_pairs={{0,1},{1,2},{2,3},{3,4},{4,5},{5,6},{6,7},{7,8},{8,9},{9,10},{10,1... | collective-permute-start | bytes 16208 | tf_op jit(solution)/shard_map/ppermute | solution.py:25
  122.0 10.0 %collective-permute-start.12 = (f32[3,192,1]{2,1,0:T(8,128)S(1)}, f32[3,192,1]{2,1,0:T(8,128)S(1)}, u32[]{:S(2)}, u32[]{:S(2)}) collective-permute-start(f32[3,192,1]{2,1,0:T(8,128)S(1)} %get-tuple-element.19), channel_id=1, source_target_pairs={{16,0},{32,16},{48,32},{64,48},{80,64},{96,80},{112,96},{128,112},... | collective-permute-start | bytes 6920 | tf_op jit(solution)/shard_map/ppermute | solution.py:26
  123.8 8.1 %collective-permute-start.13 = (f32[3,192,1]{2,1,0:T(8,128)S(1)}, f32[3,192,1]{2,1,0:T(8,128)S(1)}, u32[]{:S(2)}, u32[]{:S(2)}) collective-permute-start(f32[3,192,1]{2,1,0:T(8,128)S(1)} %get-tuple-element.20), channel_id=1, source_target_pairs={{0,16},{16,32},{32,48},{48,64},{64,80},{80,96},{96,112},{112,128},... | collective-permute-start | bytes 6920 | tf_op jit(solution)/shard_map/ppermute | solution.py:25
  134.2 0.9 copy-start.5
  134.2 1.0 copy-start.7
  166.8 2.2 %copy-start.27 = (pred[192]{0:T(512)(128)(4,1)S(1)}, pred[192]{0:T(512)(128)(4,1)}, u32[]{:S(2)}) copy-start(pred[192]{0:T(512)(128)(4,1)} %add_compare_fusion) | copy-start | bytes 580
  (3 other events, 2.5 us)

commit v8 on v4

--- a/solution.py
+++ b/solution.py
@@ -56,11 +56,11 @@
 
 
 def project(fields, table):
-    return jnp.einsum("fnw,kw->fnk", fields, table, precision=lax.Precision.HIGHEST)
+    return jnp.einsum("fnw,kw->fnk", fields, table, precision=lax.Precision.HIGH)
 
 
 def expand(coeffs, table):
-    return jnp.einsum("fnk,kw->fnw", coeffs, table, precision=lax.Precision.HIGHEST)
+    return jnp.einsum("fnk,kw->fnw", coeffs, table, precision=lax.Precision.HIGH)
 
 
 def low_pass(fields, cut_rows, active, table, wide_table, with_halos):

time: 166 us -> 164 us (0.988)
  matrix products: 6.8 us -> 4.58 us
    dot_general x5, matrix products: 6.8 us -> 4.58 us  [the longest x2 3.01 us: project(): jnp.einsum('fnw,kw->fnk', fields, table, precision=lax.Precision.HIGH)]
where the time goes in v8:
time: 164 us; the launch traced here: 163 us
  starting transfers between devices  48.1 us (29%)
  waiting for transfers between devices  35.6 us (22%)
  other arithmetic  26.3 us (16%)
  local copies, waits for them, and re-layouts  22.6 us (14%)
  blocking collectives  22.5 us (14%)
  matrix products  4.58 us (3%)
  between operations  3.01 us (2%)
    ppermute x7, starting transfers between devices, with_halo(): after = lax.ppermute(first, axis, down)  20.3 us
    ppermute x7, starting transfers between devices, with_halo(): before = lax.ppermute(last, axis, up)  13.8 us
    ppermute x7, waiting for transfers between devices, with_halo(): before = lax.ppermute(last, axis, up)  13.3 us
    all_to_all x1, blocking collectives, low_pass(): lax.all_to_all(partial, 'lon', split_axis=1, concat_axis=0, tiled=True)  11.8 us
    all_to_all x1, blocking collectives, low_pass(): lax.all_to_all(jnp.concatenate(payload, axis=1), 'lon', split_axis=0, con...  10.7 us
    ppermute x7, waiting for transfers between devices, with_halo(): after = lax.ppermute(first, axis, down)  8.86 us
    unnamed x89, local copies, waits for them, and re-layouts  8.09 us
    all_to_all x1, waiting for transfers between devices, low_pass(): lax.all_to_all(partial, 'lon', split_axis=1, concat_axis=0, tiled=True)  7.13 us
  transfers between devices with their start and end apart: 18, of which 9 were waited for; matrix products, arithmetic and copies ran while one was open for 7% of the time, Pallas kernels for 0%

profile of v8, /device:TPU:17, one launch (start us, length us, event | category | flops | bytes accessed | tf_op | source)
XLA Modules:
  0.0 162.7 jit_solution(14371609041293456670)
XLA Ops:
  0.6 1.3 pad_maximum_fusion.4
  2.0 7.4 %collective-permute-start.4 = (f32[3,1,450]{2,0,1:T(4,128)S(1)}, f32[3,1,450]{2,0,1:T(4,128)S(1)}, u32[]{:S(2)}, u32[]{:S(2)}) collective-permute-start(f32[3,1,450]{2,0,1:T(4,128)S(1)} %copy.237), channel_id=1, source_target_pairs={{1,0},{2,1},{3,2},{4,3},{5,4},{6,5},{7,6},{8,7},{9,8},{10,9},{11,1... | collective-permute-start | bytes 16208 | tf_op jit(solution)/shard_map/ppermute | solution.py:26
  9.4 2.8 %collective-permute-start.2 = (f32[3,450]{1,0:T(4,128)S(1)}, f32[3,450]{1,0:T(4,128)S(1)}, u32[]{:S(2)}, u32[]{:S(2)}) collective-permute-start(f32[3,450]{1,0:T(4,128)S(1)} %bitcast.198), channel_id=1, source_target_pairs={{0,128},{16,144},{32,160},{48,176},{64,192},{80,208},{96,224},{112... | collective-permute-start | bytes 16208 | tf_op jit(solution)/shard_map/ppermute | solution.py:33
  12.4 1.3 collective-permute-start
  13.7 1.9 %collective-permute-start.1 = (f32[3,192,1]{2,1,0:T(8,128)S(1)}, f32[3,192,1]{2,1,0:T(8,128)S(1)}, u32[]{:S(2)}, u32[]{:S(2)}) collective-permute-start(f32[3,192,1]{2,1,0:T(8,128)S(1)} %get-tuple-element.32), channel_id=1, source_target_pairs={{0,16},{16,32},{32,48},{48,64},{64,80},{80,96},{96,112},{112,128},... | collective-permute-start | bytes 6920 | tf_op jit(solution)/shard_map/ppermute | solution.py:25
  19.5 1.9 %collective-permute-start.3 = (f32[3,1,450]{2,0,1:T(4,128)S(1)}, f32[3,1,450]{2,0,1:T(4,128)S(1)}, u32[]{:S(2)}, u32[]{:S(2)}) collective-permute-start(f32[3,1,450]{2,0,1:T(4,128)S(1)} %get-tuple-element.45), channel_id=1, source_target_pairs={{0,1},{1,2},{2,3},{3,4},{4,5},{5,6},{6,7},{7,8},{8,9},{9,10},{10,1... | collective-permute-start | bytes 16208 | tf_op jit(solution)/shard_map/ppermute | solution.py:25
  21.5 1.8 %collective-permute-done = f32[3,192,1]{2,1,0:T(8,128)S(1)} collective-permute-done((f32[3,192,1]{2,1,0:T(8,128)S(1)}, f32[3,192,1]{2,1,0:T(8,128)S(1)}, u32[]{:S(2)}, u32[]{:S(2)}) %collective-permute-start) | collective-permute-done | bytes 2336 | tf_op jit(solution)/shard_map/ppermute | solution.py:26
  23.8 3.9 %collective-permute-done.3 = f32[3,1,450]{2,0,1:T(4,128)S(1)} collective-permute-done((f32[3,1,450]{2,0,1:T(4,128)S(1)}, f32[3,1,450]{2,0,1:T(4,128)S(1)}, u32[]{:S(2)}, u32[]{:S(2)}) %collective-permute-start.3) | collective-permute-done | bytes 5432 | tf_op jit(solution)/shard_map/ppermute | solution.py:25
  29.7 1.9 %collective-permute-start.9 = (f32[3,1,450]{2,0,1:T(4,128)S(1)}, f32[3,1,450]{2,0,1:T(4,128)S(1)}, u32[]{:S(2)}, u32[]{:S(2)}) collective-permute-start(f32[3,1,450]{2,0,1:T(4,128)S(1)} %copy.238), channel_id=1, source_target_pairs={{1,0},{2,1},{3,2},{4,3},{5,4},{6,5},{7,6},{8,7},{9,8},{10,9},{11,1... | collective-permute-start | bytes 16208 | tf_op jit(solution)/shard_map/ppermute | solution.py:26
  32.1 2.3 %collective-permute-start.5 = (f32[3,192,1]{2,1,0:T(8,128)S(1)}, f32[3,192,1]{2,1,0:T(8,128)S(1)}, u32[]{:S(2)}, u32[]{:S(2)}) collective-permute-start(f32[3,192,1]{2,1,0:T(8,128)S(1)} %get-tuple-element.25), channel_id=1, source_target_pairs={{16,0},{32,16},{48,32},{64,48},{80,64},{96,80},{112,96},{128,112},... | collective-permute-start | bytes 6920 | tf_op jit(solution)/shard_map/ppermute | solution.py:26
  34.4 3.8 %collective-permute-start.8 = (f32[3,1,450]{2,0,1:T(4,128)S(1)}, f32[3,1,450]{2,0,1:T(4,128)S(1)}, u32[]{:S(2)}, u32[]{:S(2)}) collective-permute-start(f32[3,1,450]{2,0,1:T(4,128)S(1)} %get-tuple-element.40), channel_id=1, source_target_pairs={{0,1},{1,2},{2,3},{3,4},{4,5},{5,6},{6,7},{7,8},{8,9},{9,10},{10,1... | collective-permute-start | bytes 16208 | tf_op jit(solution)/shard_map/ppermute | solution.py:25
  38.3 4.1 %collective-permute-done.8 = f32[3,1,450]{2,0,1:T(4,128)S(1)} collective-permute-done((f32[3,1,450]{2,0,1:T(4,128)S(1)}, f32[3,1,450]{2,0,1:T(4,128)S(1)}, u32[]{:S(2)}, u32[]{:S(2)}) %collective-permute-start.8) | collective-permute-done | bytes 5432 | tf_op jit(solution)/shard_map/ppermute | solution.py:25
  43.1 0.9 fusion.78
  46.4 1.5 fusion.84
  47.9 1.4 copy.156
  49.2 1.7 %reshape.459 = f32[16,1,4680]{2,1,0:T(1,128)} reshape(f32[192,3,130]{2,1,0:T(4,128)S(1)} %bitcast.190) | data formatting | bytes 599040
  51.0 7.0 %all-to-all-start = ((f32[16,1,4680]{2,1,0:T(1,128)}), f32[16,1,4680]{2,1,0:T(1,128)S(1)}, u32[]{:S(2)}, u32[]{:S(2)}) async-start(f32[16,1,4680]{2,1,0:T(1,128)} %reshape.459), calls=%async_computation | async-start | bytes 606208 | tf_op jit(solution)/shard_map/all_to_all | solution.py:73
  58.7 7.1 %all-to-all-done = f32[16,1,4680]{2,1,0:T(1,128)S(1)} async-done(((f32[16,1,4680]{2,1,0:T(1,128)}), f32[16,1,4680]{2,1,0:T(1,128)S(1)}, u32[]{:S(2)}, u32[]{:S(2)}) %all-to-all-start) | async-done | bytes 299552 | tf_op jit(solution)/shard_map/all_to_all | solution.py:73
  66.4 1.4 reduce.9
  67.8 0.9 reshape.460
  69.1 1.0 all_to_all.32
  70.1 3.8 %all-to-all-start.1 = ((f32[16,1,5256]{2,1,0:T(1,128)}), f32[16,1,5256]{2,1,0:T(1,128)S(1)}, u32[]{:S(2)}, u32[]{:S(2)}) async-start(f32[16,1,5256]{2,1,0:T(1,128)} %all_to_all.32), calls=%async_computation.1 | async-start | bytes 688128 | tf_op jit(solution)/shard_map/all_to_all | solution.py:81
  74.4 1.3 fusion.92
  75.7 6.3 %all-to-all-done.1 = f32[16,1,5256]{2,1,0:T(1,128)S(1)} async-done(((f32[16,1,5256]{2,1,0:T(1,128)}), f32[16,1,5256]{2,1,0:T(1,128)S(1)}, u32[]{:S(2)}, u32[]{:S(2)}) %all-to-all-start.1) | async-done | bytes 336416 | tf_op jit(solution)/shard_map/all_to_all | solution.py:81
  86.8 1.9 %collective-permute-start.11 = (f32[3,1,450]{2,0,1:T(4,128)S(1)}, f32[3,1,450]{2,0,1:T(4,128)S(1)}, u32[]{:S(2)}, u32[]{:S(2)}) collective-permute-start(f32[3,1,450]{2,0,1:T(4,128)S(1)} %copy.206), channel_id=1, source_target_pairs={{1,0},{2,1},{3,2},{4,3},{5,4},{6,5},{7,6},{8,7},{9,8},{10,9},{11,1... | collective-permute-start | bytes 16208 | tf_op jit(solution)/shard_map/ppermute | solution.py:26
  89.6 0.9 slice_select_fusion.2
  91.4 3.6 %collective-permute-start.10 = (f32[3,1,450]{2,0,1:T(4,128)S(1)}, f32[3,1,450]{2,0,1:T(4,128)S(1)}, u32[]{:S(2)}, u32[]{:S(2)}) collective-permute-start(f32[3,1,450]{2,0,1:T(4,128)S(1)} %get-tuple-element.38), channel_id=1, source_target_pairs={{0,1},{1,2},{2,3},{3,4},{4,5},{5,6},{6,7},{7,8},{8,9},{9,10},{10,1... | collective-permute-start | bytes 16208 | tf_op jit(solution)/shard_map/ppermute | solution.py:25
  95.7 3.7 %collective-permute-done.10 = f32[3,1,450]{2,0,1:T(4,128)S(1)} collective-permute-done((f32[3,1,450]{2,0,1:T(4,128)S(1)}, f32[3,1,450]{2,0,1:T(4,128)S(1)}, u32[]{:S(2)}, u32[]{:S(2)}) %collective-permute-start.10) | collective-permute-done | bytes 5432 | tf_op jit(solution)/shard_map/ppermute | solution.py:25
  102.2 1.9 %collective-permute-start.15 = (f32[3,1,450]{2,1,0:T(1,128)S(1)}, f32[3,1,450]{2,1,0:T(1,128)S(1)}, u32[]{:S(2)}, u32[]{:S(2)}) collective-permute-start(f32[3,1,450]{2,1,0:T(1,128)S(1)} %slice.653), channel_id=1, source_target_pairs={{1,0},{2,1},{3,2},{4,3},{5,4},{6,5},{7,6},{8,7},{9,8},{10,9},{11,1... | collective-permute-start | bytes 16208 | tf_op jit(solution)/shard_map/ppermute | solution.py:26
  104.2 1.4 fusion.110
  105.5 1.1 collective-permute-done.15
  106.6 2.3 %collective-permute-start.14 = (f32[3,1,450]{2,1,0:T(1,128)S(1)}, f32[3,1,450]{2,1,0:T(1,128)S(1)}, u32[]{:S(2)}, u32[]{:S(2)}) collective-permute-start(f32[3,1,450]{2,1,0:T(1,128)S(1)} %get-tuple-element.18), channel_id=1, source_target_pairs={{0,1},{1,2},{2,3},{3,4},{4,5},{5,6},{6,7},{7,8},{8,9},{9,10},{10,1... | collective-permute-start | bytes 16208 | tf_op jit(solution)/shard_map/ppermute | solution.py:25
  109.1 3.6 %collective-permute-start.12 = (f32[3,192,1]{2,1,0:T(8,128)S(1)}, f32[3,192,1]{2,1,0:T(8,128)S(1)}, u32[]{:S(2)}, u32[]{:S(2)}) collective-permute-start(f32[3,192,1]{2,1,0:T(8,128)S(1)} %get-tuple-element.19), channel_id=1, source_target_pairs={{16,0},{32,16},{48,32},{64,48},{80,64},{96,80},{112,96},{128,112},... | collective-permute-start | bytes 6920 | tf_op jit(solution)/shard_map/ppermute | solution.py:26
  113.0 1.6 %collective-permute-done.14 = f32[3,1,450]{2,1,0:T(1,128)S(1)} collective-permute-done((f32[3,1,450]{2,1,0:T(1,128)S(1)}, f32[3,1,450]{2,1,0:T(1,128)S(1)}, u32[]{:S(2)}, u32[]{:S(2)}) %collective-permute-start.14) | collective-permute-done | bytes 5432 | tf_op jit(solution)/shard_map/ppermute | solution.py:25
  114.7 6.0 %collective-permute-done.12 = f32[3,192,1]{2,1,0:T(8,128)S(1)} collective-permute-done((f32[3,192,1]{2,1,0:T(8,128)S(1)}, f32[3,192,1]{2,1,0:T(8,128)S(1)}, u32[]{:S(2)}, u32[]{:S(2)}) %collective-permute-start.12) | collective-permute-done | bytes 2336 | tf_op jit(solution)/shard_map/ppermute | solution.py:26
  121.2 0.9 fusion.76
  123.9 1.5 fusion.83
  125.4 1.4 copy.190
  126.8 1.7 %reshape.461 = f32[16,1,4680]{2,1,0:T(1,128)} reshape(f32[192,3,130]{2,1,0:T(4,128)S(1)} %bitcast.192) | data formatting | bytes 599040
  128.5 11.8 %all_to_all.42 = f32[16,1,4680]{2,1,0:T(1,128)S(1)} all-to-all(f32[16,1,4680]{2,1,0:T(1,128)} %reshape.461), channel_id=1, replica_groups=mesh['lon'=16,'lat'=16] {'lon'}, dimensions={0} | all-to-all | bytes 599040 | tf_op jit(solution)/shard_map/all_to_all | solution.py:73
  140.3 2.1 %reduce.10 = f32[16,4680]{1,0:T(8,128)} reduce(f32[16,1,4680]{2,1,0:T(1,128)S(1)} %all_to_all.42, f32[]{:T(128)} %broadcast.433), dimensions={1}, to_apply=%all_to_all.35.reduce_sub_computation | reduce | bytes 599044 | tf_op jit(solution)/shard_map/all_to_all | solution.py:73
  142.4 1.9 %reshape.462 = f32[192,3,130]{2,1,0:T(4,128)S(1)} reshape(f32[16,4680]{1,0:T(8,128)} %reduce.10) | data formatting | bytes 599040
  144.8 10.7 %all_to_all.43 = f32[16,1,4680]{2,1,0:T(1,128)S(1)} all-to-all(f32[16,1,4680]{2,1,0:T(1,128)S(1)} %broadcast_in_dim.150), channel_id=1, replica_groups=mesh['lon'=16,'lat'=16] {'lon'}, dimensions={0} | all-to-all | bytes 599040 | tf_op jit(solution)/shard_map/all_to_all | solution.py:81
  155.5 1.5 reduce.6
  157.0 1.7 %reshape.451 = f32[16,3,12,130]{3,2,1,0:T(8,128)S(1)} reshape(f32[16,4680]{1,0:T(8,128)} %reduce.6) | data formatting | bytes 599040 | tf_op jit(solution)/shard_map/reshape | solution.py:83
  158.7 0.9 copy.192
  159.6 1.2 reshape.452
  161.6 1.0 slice_bitcast_fusion
  (183 shorter events, 24.5 us)
Async XLA Ops:
  2.0 15.2 %copy-start.39 = (s32[512]{0:T(512)S(1)}, s32[512]{0:T(512)}, u32[]{:S(2)}) copy-start(s32[512]{0:T(512)} %param.12) | copy-start | bytes 6148
  2.0 21.3 %copy-start = (f32[192,450]{1,0:T(8,128)S(1)}, f32[192,450]{1,0:T(8,128)}, u32[]{:S(2)}) copy-start(f32[192,450]{1,0:T(8,128)} %param.11) | copy-start | bytes 1036804
  2.0 21.3 %copy-start.1 = (f32[192,450]{1,0:T(8,128)S(1)}, f32[192,450]{1,0:T(8,128)}, u32[]{:S(2)}) copy-start(f32[192,450]{1,0:T(8,128)} %param.10) | copy-start | bytes 1036804
  2.0 21.3 %copy-start.2 = (f32[192,450]{1,0:T(8,128)S(1)}, f32[192,450]{1,0:T(8,128)}, u32[]{:S(2)}) copy-start(f32[192,450]{1,0:T(8,128)} %param.9) | copy-start | bytes 1036804
  2.0 17.5 %collective-permute-start.4 = (f32[3,1,450]{2,0,1:T(4,128)S(1)}, f32[3,1,450]{2,0,1:T(4,128)S(1)}, u32[]{:S(2)}, u32[]{:S(2)}) collective-permute-start(f32[3,1,450]{2,0,1:T(4,128)S(1)} %copy.237), channel_id=1, source_target_pairs={{1,0},{2,1},{3,2},{4,3},{5,4},{6,5},{7,6},{8,7},{9,8},{10,9},{11,1... | collective-permute-start | bytes 16208 | tf_op jit(solution)/shard_map/ppermute | solution.py:26
  9.4 14.4 %collective-permute-start.2 = (f32[3,450]{1,0:T(4,128)S(1)}, f32[3,450]{1,0:T(4,128)S(1)}, u32[]{:S(2)}, u32[]{:S(2)}) collective-permute-start(f32[3,450]{1,0:T(4,128)S(1)} %bitcast.198), channel_id=1, source_target_pairs={{0,128},{16,144},{32,160},{48,176},{64,192},{80,208},{96,224},{112... | collective-permute-start | bytes 16208 | tf_op jit(solution)/shard_map/ppermute | solution.py:33
  12.4 10.9 %collective-permute-start = (f32[3,192,1]{2,1,0:T(8,128)S(1)}, f32[3,192,1]{2,1,0:T(8,128)S(1)}, u32[]{:S(2)}, u32[]{:S(2)}) collective-permute-start(f32[3,192,1]{2,1,0:T(8,128)S(1)} %get-tuple-element.31), channel_id=1, source_target_pairs={{16,0},{32,16},{48,32},{64,48},{80,64},{96,80},{112,96},{128,112},... | collective-permute-start | bytes 6920 | tf_op jit(solution)/shard_map/ppermute | solution.py:26
  13.7 9.5 %collective-permute-start.1 = (f32[3,192,1]{2,1,0:T(8,128)S(1)}, f32[3,192,1]{2,1,0:T(8,128)S(1)}, u32[]{:S(2)}, u32[]{:S(2)}) collective-permute-start(f32[3,192,1]{2,1,0:T(8,128)S(1)} %get-tuple-element.32), channel_id=1, source_target_pairs={{0,16},{16,32},{32,48},{48,64},{64,80},{80,96},{96,112},{112,128},... | collective-permute-start | bytes 6920 | tf_op jit(solution)/shard_map/ppermute | solution.py:25
  15.7 27.3 %copy-start.31 = (f32[192]{0:T(256)}, f32[192]{0:T(256)S(1)}, u32[]{:S(2)}) copy-start(f32[192]{0:T(256)S(1)} %get-tuple-element.60) | copy-start | bytes 2308
  15.7 27.3 %copy-start.33 = (f32[192]{0:T(256)}, f32[192]{0:T(256)S(1)}, u32[]{:S(2)}) copy-start(f32[192]{0:T(256)S(1)} %get-tuple-element.61) | copy-start | bytes 2308
  15.8 28.3 %copy-start.29 = (f32[192]{0:T(256)}, f32[192]{0:T(256)S(1)}, u32[]{:S(2)}) copy-start(f32[192]{0:T(256)S(1)} %get-tuple-element.10) | copy-start | bytes 2308
  15.8 29.1 %copy-start.17 = (f32[192]{0:T(256)}, f32[192]{0:T(256)S(1)}, u32[]{:S(2)}) copy-start(f32[192]{0:T(256)S(1)} %get-tuple-element.11) | copy-start | bytes 2308
  16.5 28.4 %copy-start.20 = (f32[192]{0:T(256)}, f32[192]{0:T(256)S(1)}, u32[]{:S(2)}) copy-start(f32[192]{0:T(256)S(1)} %get-tuple-element.58) | copy-start | bytes 2308
  16.5 28.4 %copy-start.22 = (f32[192]{0:T(256)}, f32[192]{0:T(256)S(1)}, u32[]{:S(2)}) copy-start(f32[192]{0:T(256)S(1)} %get-tuple-element.59) | copy-start | bytes 2308
  17.1 29.3 %copy-start.9 = (f32[65,450]{1,0:T(8,128)}, f32[65,450]{1,0:T(8,128)S(1)}, u32[]{:S(2)}) copy-start(f32[65,450]{1,0:T(8,128)S(1)} %get-tuple-element.53) | copy-start | bytes 351004
  17.1 29.3 %copy-start.11 = (f32[65,450]{1,0:T(8,128)}, f32[65,450]{1,0:T(8,128)S(1)}, u32[]{:S(2)}) copy-start(f32[65,450]{1,0:T(8,128)S(1)} %get-tuple-element.54) | copy-start | bytes 351004
  17.5 66.2 %copy-start.13 = (f32[192,130]{1,0:T(8,128)}, f32[192,130]{1,0:T(8,128)S(1)}, u32[]{:S(2)}) copy-start(f32[192,130]{1,0:T(8,128)S(1)} %pad_maximum_fusion.46) | copy-start | bytes 299524
  19.5 8.2 %copy-start.35 = (f32[3]{0:T(128)S(1)}, f32[3]{0:T(128)}, u32[]{:S(2)}) copy-start(f32[3]{0:T(128)} %constant.138.clone) | copy-start | bytes 40
  19.5 8.1 %collective-permute-start.3 = (f32[3,1,450]{2,0,1:T(4,128)S(1)}, f32[3,1,450]{2,0,1:T(4,128)S(1)}, u32[]{:S(2)}, u32[]{:S(2)}) collective-permute-start(f32[3,1,450]{2,0,1:T(4,128)S(1)} %get-tuple-element.45), channel_id=1, source_target_pairs={{0,1},{1,2},{2,3},{3,4},{4,5},{5,6},{6,7},{7,8},{8,9},{9,10},{10,1... | collective-permute-start | bytes 16208 | tf_op jit(solution)/shard_map/ppermute | solution.py:25
  27.8 10.5 %copy-start.27 = (f32[3,1,1]{2,0,1:T(4,128)}, f32[3,1,1]{2,0,1:T(4,128)S(1)}, u32[]{:S(2)}) copy-start(f32[3,1,1]{2,0,1:T(4,128)S(1)} %broadcast.383.clone) | copy-start | bytes 40
  29.7 4.7 %collective-permute-start.9 = (f32[3,1,450]{2,0,1:T(4,128)S(1)}, f32[3,1,450]{2,0,1:T(4,128)S(1)}, u32[]{:S(2)}, u32[]{:S(2)}) collective-permute-start(f32[3,1,450]{2,0,1:T(4,128)S(1)} %copy.238), channel_id=1, source_target_pairs={{1,0},{2,1},{3,2},{4,3},{5,4},{6,5},{7,6},{8,7},{9,8},{10,9},{11,1... | collective-permute-start | bytes 16208 | tf_op jit(solution)/shard_map/ppermute | solution.py:26
  31.8 6.5 %collective-permute-start.7 = (f32[3,450]{1,0:T(4,128)S(1)}, f32[3,450]{1,0:T(4,128)S(1)}, u32[]{:S(2)}, u32[]{:S(2)}) collective-permute-start(f32[3,450]{1,0:T(4,128)S(1)} %bitcast.199), channel_id=1, source_target_pairs={{0,128},{16,144},{32,160},{48,176},{64,192},{80,208},{96,224},{112... | collective-permute-start | bytes 16208 | tf_op jit(solution)/shard_map/ppermute | solution.py:33
  32.1 10.4 %collective-permute-start.5 = (f32[3,192,1]{2,1,0:T(8,128)S(1)}, f32[3,192,1]{2,1,0:T(8,128)S(1)}, u32[]{:S(2)}, u32[]{:S(2)}) collective-permute-start(f32[3,192,1]{2,1,0:T(8,128)S(1)} %get-tuple-element.25), channel_id=1, source_target_pairs={{16,0},{32,16},{48,32},{64,48},{80,64},{96,80},{112,96},{128,112},... | collective-permute-start | bytes 6920 | tf_op jit(solution)/shard_map/ppermute | solution.py:26
  34.4 8.1 %collective-permute-start.6 = (f32[3,192,1]{2,1,0:T(8,128)S(1)}, f32[3,192,1]{2,1,0:T(8,128)S(1)}, u32[]{:S(2)}, u32[]{:S(2)}) collective-permute-start(f32[3,192,1]{2,1,0:T(8,128)S(1)} %get-tuple-element.26), channel_id=1, source_target_pairs={{0,16},{16,32},{32,48},{48,64},{64,80},{80,96},{96,112},{112,128},... | collective-permute-start | bytes 6920 | tf_op jit(solution)/shard_map/ppermute | solution.py:25
  34.4 8.0 %collective-permute-start.8 = (f32[3,1,450]{2,0,1:T(4,128)S(1)}, f32[3,1,450]{2,0,1:T(4,128)S(1)}, u32[]{:S(2)}, u32[]{:S(2)}) collective-permute-start(f32[3,1,450]{2,0,1:T(4,128)S(1)} %get-tuple-element.40), channel_id=1, source_target_pairs={{0,1},{1,2},{2,3},{3,4},{4,5},{5,6},{6,7},{7,8},{8,9},{9,10},{10,1... | collective-permute-start | bytes 16208 | tf_op jit(solution)/shard_map/ppermute | solution.py:25
  44.0 1.6 copy-start.3
  51.0 14.8 %all-to-all-start = ((f32[16,1,4680]{2,1,0:T(1,128)}), f32[16,1,4680]{2,1,0:T(1,128)S(1)}, u32[]{:S(2)}, u32[]{:S(2)}) async-start(f32[16,1,4680]{2,1,0:T(1,128)} %reshape.459), calls=%async_computation | async-start | bytes 606208 | tf_op jit(solution)/shard_map/all_to_all | solution.py:73
  70.1 12.0 %all-to-all-start.1 = ((f32[16,1,5256]{2,1,0:T(1,128)}), f32[16,1,5256]{2,1,0:T(1,128)S(1)}, u32[]{:S(2)}, u32[]{:S(2)}) async-start(f32[16,1,5256]{2,1,0:T(1,128)} %all_to_all.32), calls=%async_computation.1 | async-start | bytes 688128 | tf_op jit(solution)/shard_map/all_to_all | solution.py:81
  84.6 1.5 copy-start.6
  84.6 1.5 copy-start.8
  84.6 1.5 copy-start.37
  86.7 3.9 %copy-start.26 = (f32[3,1,452]{2,1,0:T(1,128)S(1)}, f32[3,1,452]{2,1,0:T(1,128)}, u32[]{:S(2)}) copy-start(f32[3,1,452]{2,1,0:T(1,128)} %slice_multiply_fusion) | copy-start | bytes 16276
  86.7 12.7 %copy-start.36 = (f32[3]{0:T(128)S(1)}, f32[3]{0:T(128)}, u32[]{:S(2)}) copy-start(f32[3]{0:T(128)} %constant.138.clone) | copy-start | bytes 40
  86.7 12.7 %copy-start.28 = (f32[3,1,1]{2,0,1:T(4,128)S(1)}, f32[3,1,1]{2,0,1:T(4,128)}, u32[]{:S(2)}) copy-start(f32[3,1,1]{2,0,1:T(4,128)} %copy-done.27) | copy-start | bytes 40
  86.7 12.8 %copy-start.18 = (f32[192]{0:T(256)S(1)}, f32[192]{0:T(256)}, u32[]{:S(2)}) copy-start(f32[192]{0:T(256)} %copy-done.17) | copy-start | bytes 2308
  86.7 12.8 %copy-start.32 = (f32[192]{0:T(256)S(1)}, f32[192]{0:T(256)}, u32[]{:S(2)}) copy-start(f32[192]{0:T(256)} %copy-done.31) | copy-start | bytes 2308
  86.8 12.8 %copy-start.34 = (f32[192]{0:T(256)S(1)}, f32[192]{0:T(256)}, u32[]{:S(2)}) copy-start(f32[192]{0:T(256)} %copy-done.33) | copy-start | bytes 2308
  86.8 4.6 %collective-permute-start.11 = (f32[3,1,450]{2,0,1:T(4,128)S(1)}, f32[3,1,450]{2,0,1:T(4,128)S(1)}, u32[]{:S(2)}, u32[]{:S(2)}) collective-permute-start(f32[3,1,450]{2,0,1:T(4,128)S(1)} %copy.206), channel_id=1, source_target_pairs={{1,0},{2,1},{3,2},{4,3},{5,4},{6,5},{7,6},{8,7},{9,8},{10,9},{11,1... | collective-permute-start | bytes 16208 | tf_op jit(solution)/shard_map/ppermute | solution.py:26
  90.6 9.9 %copy-start.21 = (f32[192]{0:T(256)S(1)}, f32[192]{0:T(256)}, u32[]{:S(2)}) copy-start(f32[192]{0:T(256)} %copy-done.20) | copy-start | bytes 2308
  90.6 9.9 %copy-start.23 = (f32[192]{0:T(256)S(1)}, f32[192]{0:T(256)}, u32[]{:S(2)}) copy-start(f32[192]{0:T(256)} %copy-done.22) | copy-start | bytes 2308
  90.6 9.9 %copy-start.30 = (f32[192]{0:T(256)S(1)}, f32[192]{0:T(256)}, u32[]{:S(2)}) copy-start(f32[192]{0:T(256)} %copy-done.29) | copy-start | bytes 2308
  91.4 8.0 %collective-permute-start.10 = (f32[3,1,450]{2,0,1:T(4,128)S(1)}, f32[3,1,450]{2,0,1:T(4,128)S(1)}, u32[]{:S(2)}, u32[]{:S(2)}) collective-permute-start(f32[3,1,450]{2,0,1:T(4,128)S(1)} %get-tuple-element.38), channel_id=1, source_target_pairs={{0,1},{1,2},{2,3},{3,4},{4,5},{5,6},{6,7},{7,8},{8,9},{9,10},{10,1... | collective-permute-start | bytes 16208 | tf_op jit(solution)/shard_map/ppermute | solution.py:25
  102.2 18.4 %copy-start.25 = (f32[3,1,1]{2,1,0:T(1,128)S(1)}, f32[3,1,1]{2,1,0:T(1,128)}, u32[]{:S(2)}) copy-start(f32[3,1,1]{2,1,0:T(1,128)} %copy-done.24) | copy-start | bytes 40
  102.2 4.4 %collective-permute-start.15 = (f32[3,1,450]{2,1,0:T(1,128)S(1)}, f32[3,1,450]{2,1,0:T(1,128)S(1)}, u32[]{:S(2)}, u32[]{:S(2)}) collective-permute-start(f32[3,1,450]{2,1,0:T(1,128)S(1)} %slice.653), channel_id=1, source_target_pairs={{1,0},{2,1},{3,2},{4,3},{5,4},{6,5},{7,6},{8,7},{9,8},{10,9},{11,1... | collective-permute-start | bytes 16208 | tf_op jit(solution)/shard_map/ppermute | solution.py:26
  106.6 8.0 %collective-permute-start.14 = (f32[3,1,450]{2,1,0:T(1,128)S(1)}, f32[3,1,450]{2,1,0:T(1,128)S(1)}, u32[]{:S(2)}, u32[]{:S(2)}) collective-permute-start(f32[3,1,450]{2,1,0:T(1,128)S(1)} %get-tuple-element.18), channel_id=1, source_target_pairs={{0,1},{1,2},{2,3},{3,4},{4,5},{5,6},{6,7},{7,8},{8,9},{9,10},{10,1... | collective-permute-start | bytes 16208 | tf_op jit(solution)/shard_map/ppermute | solution.py:25
  109.1 11.6 %collective-permute-start.12 = (f32[3,192,1]{2,1,0:T(8,128)S(1)}, f32[3,192,1]{2,1,0:T(8,128)S(1)}, u32[]{:S(2)}, u32[]{:S(2)}) collective-permute-start(f32[3,192,1]{2,1,0:T(8,128)S(1)} %get-tuple-element.19), channel_id=1, source_target_pairs={{16,0},{32,16},{48,32},{64,48},{80,64},{96,80},{112,96},{128,112},... | collective-permute-start | bytes 6920 | tf_op jit(solution)/shard_map/ppermute | solution.py:26
  112.6 8.0 %collective-permute-start.13 = (f32[3,192,1]{2,1,0:T(8,128)S(1)}, f32[3,192,1]{2,1,0:T(8,128)S(1)}, u32[]{:S(2)}, u32[]{:S(2)}) collective-permute-start(f32[3,192,1]{2,1,0:T(8,128)S(1)} %get-tuple-element.20), channel_id=1, source_target_pairs={{0,16},{16,32},{32,48},{48,64},{64,80},{80,96},{96,112},{112,128},... | collective-permute-start | bytes 6920 | tf_op jit(solution)/shard_map/ppermute | solution.py:25
  158.7 2.2 %copy-start.38 = (pred[192]{0:T(512)(128)(4,1)S(1)}, pred[192]{0:T(512)(128)(4,1)}, u32[]{:S(2)}) copy-start(pred[192]{0:T(512)(128)(4,1)} %add_compare_fusion) | copy-start | bytes 580
  (10 other events, 9.4 us)

commit v9 on v5

--- a/solution.py
+++ b/solution.py
@@ -68,10 +68,10 @@
     lon_index = lax.axis_index("lon")
     count, rows, width = fields.shape
     share = rows // devices
-    partial = project(fields, table)
+    partial = jnp.einsum("fnw,kw->nfk", fields, table, precision=lax.Precision.HIGH)
     modes = partial.shape[2]
-    gathered = lax.all_to_all(partial, "lon", split_axis=1, concat_axis=0, tiled=True)
-    reduced = gathered.reshape(devices, count, share, modes).sum(axis=0)
+    gathered = lax.all_to_all(partial, "lon", split_axis=0, concat_axis=0, tiled=True)
+    reduced = gathered.reshape(devices, share, count, modes).sum(axis=0)
     payload = [jnp.broadcast_to(reduced.reshape(1, -1), (devices, count * share * modes))]
     if with_halos:
         targets = jnp.arange(devices, dtype=jnp.int32)[:, None]
@@ -80,8 +80,8 @@
         payload += [edge, jnp.broadcast_to(fields[:, 0, :].reshape(1, -1), (devices, count * width))]
     spread = lax.all_to_all(jnp.concatenate(payload, axis=1), "lon", split_axis=0, concat_axis=0, tiled=True)
     block = count * share * modes
-    coeffs = spread[:, :block].reshape(devices, count, share, modes)
-    coeffs = jnp.moveaxis(coeffs, 0, 1).reshape(count, rows, modes)
+    coeffs = spread[:, :block].reshape(devices, share, count, modes)
+    coeffs = coeffs.transpose(2, 0, 1, 3).reshape(count, rows, modes)
     weights = spectral_weights(cut_rows)
     scaled = coeffs * weights[None]
     if not with_halos:

time: 161 us -> 163 us (1.012)
  other arithmetic: 24.3 us -> 26 us
    dot_general x2 -> x0, local copies, waits for them, and re-layouts: 2.73 us -> none  [project(): jnp.einsum('fnw,kw->fnk', fields, table, precision=lax.Precision.HIGH)]
    transpose x2, local copies, waits for them, and re-layouts: 1.03 us -> 2.73 us  [low_pass(): jnp.einsum('fnw,kw->nfk', fields, table, precision=lax.Precision.HIGH)]
    unnamed x99 -> x91, local copies, waits for them, and re-layouts: 7.14 us -> 8.77 us
    reshape x4 -> x2, local copies, waits for them, and re-layouts: 3.49 us -> 2.81 us  [low_pass(): coeffs = spread[:, :block].reshape(devices, share, count, modes)]
where the time goes in v9:
time: 163 us; the launch traced here: 162 us
  starting transfers between devices  49.3 us (30%)
  waiting for transfers between devices  30.6 us (19%)
  other arithmetic  26 us (16%)
  blocking collectives  24.4 us (15%)
  local copies, waits for them, and re-layouts  22.9 us (14%)
  matrix products  5.5 us (3%)
  between operations  3.06 us (2%)
    ppermute x7, starting transfers between devices, with_halo(): after = lax.ppermute(first, axis, down)  22.1 us
    all_to_all x1, blocking collectives, low_pass(): lax.all_to_all(partial, 'lon', split_axis=0, concat_axis=0, tiled=True)  13.7 us
    ppermute x7, starting transfers between devices, with_halo(): before = lax.ppermute(last, axis, up)  13.4 us
    ppermute x7, waiting for transfers between devices, with_halo(): before = lax.ppermute(last, axis, up)  11.5 us
    all_to_all x1, blocking collectives, low_pass(): lax.all_to_all(jnp.concatenate(payload, axis=1), 'lon', split_axis=0, con...  10.7 us
    unnamed x91, local copies, waits for them, and re-layouts  8.77 us
    all_to_all x1, waiting for transfers between devices, low_pass(): lax.all_to_all(partial, 'lon', split_axis=0, concat_axis=0, tiled=True)  7.45 us
    all_to_all x1, starting transfers between devices, low_pass(): lax.all_to_all(partial, 'lon', split_axis=0, concat_axis=0, tiled=True)  6.94 us
  transfers between devices with their start and end apart: 18, of which 9 were waited for; matrix products, arithmetic and copies ran while one was open for 7% of the time, Pallas kernels for 0%

profile of v9, /device:TPU:17, one launch (start us, length us, event | category | flops | bytes accessed | tf_op | source)
XLA Modules:
  0.0 161.7 jit_solution(15529982525896697263)
XLA Ops:
  0.6 1.3 pad_maximum_fusion.4
  2.0 7.4 %collective-permute-start.4 = (f32[3,1,450]{2,0,1:T(4,128)S(1)}, f32[3,1,450]{2,0,1:T(4,128)S(1)}, u32[]{:S(2)}, u32[]{:S(2)}) collective-permute-start(f32[3,1,450]{2,0,1:T(4,128)S(1)} %copy.293), channel_id=1, source_target_pairs={{1,0},{2,1},{3,2},{4,3},{5,4},{6,5},{7,6},{8,7},{9,8},{10,9},{11,1... | collective-permute-start | bytes 16208 | tf_op jit(solution)/shard_map/ppermute | solution.py:26
  9.4 2.8 %collective-permute-start.2 = (f32[3,450]{1,0:T(4,128)S(1)}, f32[3,450]{1,0:T(4,128)S(1)}, u32[]{:S(2)}, u32[]{:S(2)}) collective-permute-start(f32[3,450]{1,0:T(4,128)S(1)} %bitcast.210), channel_id=1, source_target_pairs={{0,128},{16,144},{32,160},{48,176},{64,192},{80,208},{96,224},{112... | collective-permute-start | bytes 16208 | tf_op jit(solution)/shard_map/ppermute | solution.py:33
  12.4 1.3 collective-permute-start
  13.7 1.9 %collective-permute-start.1 = (f32[3,192,1]{2,1,0:T(8,128)S(1)}, f32[3,192,1]{2,1,0:T(8,128)S(1)}, u32[]{:S(2)}, u32[]{:S(2)}) collective-permute-start(f32[3,192,1]{2,1,0:T(8,128)S(1)} %get-tuple-element.32), channel_id=1, source_target_pairs={{0,16},{16,32},{32,48},{48,64},{64,80},{80,96},{96,112},{112,128},... | collective-permute-start | bytes 6920 | tf_op jit(solution)/shard_map/ppermute | solution.py:25
  17.5 1.9 %collective-permute-start.3 = (f32[3,1,450]{2,0,1:T(4,128)S(1)}, f32[3,1,450]{2,0,1:T(4,128)S(1)}, u32[]{:S(2)}, u32[]{:S(2)}) collective-permute-start(f32[3,1,450]{2,0,1:T(4,128)S(1)} %get-tuple-element.45), channel_id=1, source_target_pairs={{0,1},{1,2},{2,3},{3,4},{4,5},{5,6},{6,7},{7,8},{8,9},{9,10},{10,1... | collective-permute-start | bytes 16208 | tf_op jit(solution)/shard_map/ppermute | solution.py:25
  19.4 3.9 %collective-permute-done = f32[3,192,1]{2,1,0:T(8,128)S(1)} collective-permute-done((f32[3,192,1]{2,1,0:T(8,128)S(1)}, f32[3,192,1]{2,1,0:T(8,128)S(1)}, u32[]{:S(2)}, u32[]{:S(2)}) %collective-permute-start) | collective-permute-done | bytes 2336 | tf_op jit(solution)/shard_map/ppermute | solution.py:26
  23.8 1.9 %collective-permute-done.3 = f32[3,1,450]{2,0,1:T(4,128)S(1)} collective-permute-done((f32[3,1,450]{2,0,1:T(4,128)S(1)}, f32[3,1,450]{2,0,1:T(4,128)S(1)}, u32[]{:S(2)}, u32[]{:S(2)}) %collective-permute-start.3) | collective-permute-done | bytes 5432 | tf_op jit(solution)/shard_map/ppermute | solution.py:25
  27.7 1.9 %collective-permute-start.9 = (f32[3,1,450]{2,0,1:T(4,128)S(1)}, f32[3,1,450]{2,0,1:T(4,128)S(1)}, u32[]{:S(2)}, u32[]{:S(2)}) collective-permute-start(f32[3,1,450]{2,0,1:T(4,128)S(1)} %copy.294), channel_id=1, source_target_pairs={{1,0},{2,1},{3,2},{4,3},{5,4},{6,5},{7,6},{8,7},{9,8},{10,9},{11,1... | collective-permute-start | bytes 16208 | tf_op jit(solution)/shard_map/ppermute | solution.py:26
  29.9 2.4 %collective-permute-start.5 = (f32[3,192,1]{2,1,0:T(8,128)S(1)}, f32[3,192,1]{2,1,0:T(8,128)S(1)}, u32[]{:S(2)}, u32[]{:S(2)}) collective-permute-start(f32[3,192,1]{2,1,0:T(8,128)S(1)} %get-tuple-element.25), channel_id=1, source_target_pairs={{16,0},{32,16},{48,32},{64,48},{80,64},{96,80},{112,96},{128,112},... | collective-permute-start | bytes 6920 | tf_op jit(solution)/shard_map/ppermute | solution.py:26
  32.4 3.7 %collective-permute-start.8 = (f32[3,1,450]{2,0,1:T(4,128)S(1)}, f32[3,1,450]{2,0,1:T(4,128)S(1)}, u32[]{:S(2)}, u32[]{:S(2)}) collective-permute-start(f32[3,1,450]{2,0,1:T(4,128)S(1)} %get-tuple-element.40), channel_id=1, source_target_pairs={{0,1},{1,2},{2,3},{3,4},{4,5},{5,6},{6,7},{7,8},{8,9},{9,10},{10,1... | collective-permute-start | bytes 16208 | tf_op jit(solution)/shard_map/ppermute | solution.py:25
  36.2 4.2 %collective-permute-done.8 = f32[3,1,450]{2,0,1:T(4,128)S(1)} collective-permute-done((f32[3,1,450]{2,0,1:T(4,128)S(1)}, f32[3,1,450]{2,0,1:T(4,128)S(1)}, u32[]{:S(2)}, u32[]{:S(2)}) %collective-permute-start.8) | collective-permute-done | bytes 5432 | tf_op jit(solution)/shard_map/ppermute | solution.py:25
  41.1 0.9 fusion.77
  44.9 1.5 convolution_bitcast_fusion.1
  46.3 1.4 copy.205
  47.7 1.7 %reshape.469 = f32[16,1,4680]{2,1,0:T(1,128)} reshape(f32[192,3,130]{2,1,0:T(4,128)S(1)} %copy.205) | data formatting | bytes 599040
  49.4 6.9 %all-to-all-start = ((f32[16,1,4680]{2,1,0:T(1,128)}), f32[16,1,4680]{2,1,0:T(1,128)S(1)}, u32[]{:S(2)}, u32[]{:S(2)}) async-start(f32[16,1,4680]{2,1,0:T(1,128)} %reshape.469), calls=%async_computation | async-start | bytes 606208 | tf_op jit(solution)/shard_map/all_to_all | solution.py:73
  56.7 7.4 %all-to-all-done = f32[16,1,4680]{2,1,0:T(1,128)S(1)} async-done(((f32[16,1,4680]{2,1,0:T(1,128)}), f32[16,1,4680]{2,1,0:T(1,128)S(1)}, u32[]{:S(2)}, u32[]{:S(2)}) %all-to-all-start) | async-done | bytes 299552 | tf_op jit(solution)/shard_map/all_to_all | solution.py:73
  64.7 1.3 reduce.7
  66.0 0.9 reshape.470
  67.4 1.1 all_to_all.19
  68.5 3.8 %all-to-all-start.1 = ((f32[16,1,6606]{2,1,0:T(1,128)}), f32[16,1,6606]{2,1,0:T(1,128)S(1)}, u32[]{:S(2)}, u32[]{:S(2)}) async-start(f32[16,1,6606]{2,1,0:T(1,128)} %all_to_all.19), calls=%async_computation.1 | async-start | bytes 851968 | tf_op jit(solution)/shard_map/all_to_all | solution.py:81
  74.9 1.3 fusion.89
  76.2 5.0 %all-to-all-done.1 = f32[16,1,6606]{2,1,0:T(1,128)S(1)} async-done(((f32[16,1,6606]{2,1,0:T(1,128)}), f32[16,1,6606]{2,1,0:T(1,128)S(1)}, u32[]{:S(2)}, u32[]{:S(2)}) %all-to-all-start.1) | async-done | bytes 422816 | tf_op jit(solution)/shard_map/all_to_all | solution.py:81
  82.7 0.9 reshape.456
  86.7 1.9 %collective-permute-start.11 = (f32[3,1,450]{2,0,1:T(4,128)S(1)}, f32[3,1,450]{2,0,1:T(4,128)S(1)}, u32[]{:S(2)}, u32[]{:S(2)}) collective-permute-start(f32[3,1,450]{2,0,1:T(4,128)S(1)} %copy.259), channel_id=1, source_target_pairs={{1,0},{2,1},{3,2},{4,3},{5,4},{6,5},{7,6},{8,7},{9,8},{10,9},{11,1... | collective-permute-start | bytes 16208 | tf_op jit(solution)/shard_map/ppermute | solution.py:26
  91.3 3.6 %collective-permute-start.10 = (f32[3,1,450]{2,0,1:T(4,128)S(1)}, f32[3,1,450]{2,0,1:T(4,128)S(1)}, u32[]{:S(2)}, u32[]{:S(2)}) collective-permute-start(f32[3,1,450]{2,0,1:T(4,128)S(1)} %get-tuple-element.38), channel_id=1, source_target_pairs={{0,1},{1,2},{2,3},{3,4},{4,5},{5,6},{6,7},{7,8},{8,9},{9,10},{10,1... | collective-permute-start | bytes 16208 | tf_op jit(solution)/shard_map/ppermute | solution.py:25
  95.7 1.0 slice.634
  96.8 2.5 %collective-permute-done.10 = f32[3,1,450]{2,0,1:T(4,128)S(1)} collective-permute-done((f32[3,1,450]{2,0,1:T(4,128)S(1)}, f32[3,1,450]{2,0,1:T(4,128)S(1)}, u32[]{:S(2)}, u32[]{:S(2)}) %collective-permute-start.10) | collective-permute-done | bytes 5432 | tf_op jit(solution)/shard_map/ppermute | solution.py:25
  102.1 3.1 %collective-permute-start.15 = (f32[3,1,450]{2,1,0:T(1,128)S(1)}, f32[3,1,450]{2,1,0:T(1,128)S(1)}, u32[]{:S(2)}, u32[]{:S(2)}) collective-permute-start(f32[3,1,450]{2,1,0:T(1,128)S(1)} %slice.667), channel_id=1, source_target_pairs={{1,0},{2,1},{3,2},{4,3},{5,4},{6,5},{7,6},{8,7},{9,8},{10,9},{11,1... | collective-permute-start | bytes 16208 | tf_op jit(solution)/shard_map/ppermute | solution.py:26
  105.2 1.3 fusion.109
  106.5 2.2 %collective-permute-start.14 = (f32[3,1,450]{2,1,0:T(1,128)S(1)}, f32[3,1,450]{2,1,0:T(1,128)S(1)}, u32[]{:S(2)}, u32[]{:S(2)}) collective-permute-start(f32[3,1,450]{2,1,0:T(1,128)S(1)} %get-tuple-element.18), channel_id=1, source_target_pairs={{0,1},{1,2},{2,3},{3,4},{4,5},{5,6},{6,7},{7,8},{8,9},{9,10},{10,1... | collective-permute-start | bytes 16208 | tf_op jit(solution)/shard_map/ppermute | solution.py:25
  108.9 4.2 %collective-permute-start.12 = (f32[3,192,1]{2,1,0:T(8,128)S(1)}, f32[3,192,1]{2,1,0:T(8,128)S(1)}, u32[]{:S(2)}, u32[]{:S(2)}) collective-permute-start(f32[3,192,1]{2,1,0:T(8,128)S(1)} %get-tuple-element.19), channel_id=1, source_target_pairs={{16,0},{32,16},{48,32},{64,48},{80,64},{96,80},{112,96},{128,112},... | collective-permute-start | bytes 6920 | tf_op jit(solution)/shard_map/ppermute | solution.py:26
  113.1 1.4 collective-permute-done.14
  114.6 2.8 %collective-permute-done.12 = f32[3,192,1]{2,1,0:T(8,128)S(1)} collective-permute-done((f32[3,192,1]{2,1,0:T(8,128)S(1)}, f32[3,192,1]{2,1,0:T(8,128)S(1)}, u32[]{:S(2)}, u32[]{:S(2)}) %collective-permute-start.12) | collective-permute-done | bytes 2336 | tf_op jit(solution)/shard_map/ppermute | solution.py:26
  117.4 1.5 collective-permute-done.13
  119.4 0.9 fusion.75
  122.2 1.5 convolution_bitcast_fusion
  123.7 1.4 copy.240
  125.1 1.7 %reshape.471 = f32[16,1,4680]{2,1,0:T(1,128)} reshape(f32[192,3,130]{2,1,0:T(4,128)S(1)} %copy.240) | data formatting | bytes 599040
  126.8 13.7 %all_to_all.28 = f32[16,1,4680]{2,1,0:T(1,128)S(1)} all-to-all(f32[16,1,4680]{2,1,0:T(1,128)} %reshape.471), channel_id=1, replica_groups=mesh['lon'=16,'lat'=16] {'lon'}, dimensions={0} | all-to-all | bytes 599040 | tf_op jit(solution)/shard_map/all_to_all | solution.py:73
  140.5 2.1 %reduce.8 = f32[16,4680]{1,0:T(8,128)} reduce(f32[16,1,4680]{2,1,0:T(1,128)S(1)} %all_to_all.28, f32[]{:T(128)} %broadcast.434), dimensions={1}, to_apply=%all_to_all.22.reduce_sub_computation | reduce | bytes 599044 | tf_op jit(solution)/shard_map/all_to_all | solution.py:73
  142.5 1.9 %reshape.472 = f32[192,3,130]{2,1,0:T(4,128)S(1)} reshape(f32[16,4680]{1,0:T(8,128)} %reduce.8) | data formatting | bytes 599040
  144.9 10.7 %all_to_all.29 = f32[16,1,4680]{2,1,0:T(1,128)S(1)} all-to-all(f32[16,1,4680]{2,1,0:T(1,128)S(1)} %broadcast_in_dim.159), channel_id=1, replica_groups=mesh['lon'=16,'lat'=16] {'lon'}, dimensions={0} | all-to-all | bytes 599040 | tf_op jit(solution)/shard_map/all_to_all | solution.py:81
  155.6 1.5 reduce.3
  157.1 1.9 %reshape.461 = f32[16,12,3,130]{3,2,1,0:T(4,128)S(1)} reshape(f32[16,4680]{1,0:T(8,128)} %reduce.3) | data formatting | bytes 599040 | tf_op jit(solution)/shard_map/reshape | solution.py:83
  159.0 1.7 %convolution_select_fusion = f32[3,192,450]{2,1,0:T(8,128)S(1)} fusion(f32[3,192,130]{2,0,1:T(4,128)S(1)} %bitcast.205, pred[192]{0:T(512)(128)(4,1)S(1)} %copy-done.40, f32[192,130]{1,0:T(8,128)} %copy-done.13, f32[65,450]{1,0:T(8,128)S(1)} %copy-done.12, f32[65,450]{1,0:T(8,128)S(1)} %copy-done.10, f32[3,192,450]{2,1,0:T(8,128)S(1)} %slice_select_fusion, ...), kind=kOutput, calls=%fused_computation.16 | convolution fusion | flops 203605376 | bytes 3743952 | tf_op jit(solution)/shard_map/fnk,kw->fnw/dot_general | solution.py:63
  160.7 1.0 slice_bitcast_fusion
  (186 shorter events, 24.6 us)
Async XLA Ops:
  2.0 15.3 %copy-start.41 = (s32[512]{0:T(512)S(1)}, s32[512]{0:T(512)}, u32[]{:S(2)}) copy-start(s32[512]{0:T(512)} %param.12) | copy-start | bytes 6148
  2.0 21.3 %copy-start = (f32[192,450]{1,0:T(8,128)S(1)}, f32[192,450]{1,0:T(8,128)}, u32[]{:S(2)}) copy-start(f32[192,450]{1,0:T(8,128)} %param.11) | copy-start | bytes 1036804
  2.0 21.3 %copy-start.1 = (f32[192,450]{1,0:T(8,128)S(1)}, f32[192,450]{1,0:T(8,128)}, u32[]{:S(2)}) copy-start(f32[192,450]{1,0:T(8,128)} %param.10) | copy-start | bytes 1036804
  2.0 21.3 %copy-start.2 = (f32[192,450]{1,0:T(8,128)S(1)}, f32[192,450]{1,0:T(8,128)}, u32[]{:S(2)}) copy-start(f32[192,450]{1,0:T(8,128)} %param.9) | copy-start | bytes 1036804
  2.0 15.4 %collective-permute-start.4 = (f32[3,1,450]{2,0,1:T(4,128)S(1)}, f32[3,1,450]{2,0,1:T(4,128)S(1)}, u32[]{:S(2)}, u32[]{:S(2)}) collective-permute-start(f32[3,1,450]{2,0,1:T(4,128)S(1)} %copy.293), channel_id=1, source_target_pairs={{1,0},{2,1},{3,2},{4,3},{5,4},{6,5},{7,6},{8,7},{9,8},{10,9},{11,1... | collective-permute-start | bytes 16208 | tf_op jit(solution)/shard_map/ppermute | solution.py:26
  9.4 14.4 %collective-permute-start.2 = (f32[3,450]{1,0:T(4,128)S(1)}, f32[3,450]{1,0:T(4,128)S(1)}, u32[]{:S(2)}, u32[]{:S(2)}) collective-permute-start(f32[3,450]{1,0:T(4,128)S(1)} %bitcast.210), channel_id=1, source_target_pairs={{0,128},{16,144},{32,160},{48,176},{64,192},{80,208},{96,224},{112... | collective-permute-start | bytes 16208 | tf_op jit(solution)/shard_map/ppermute | solution.py:33
  12.4 10.9 %collective-permute-start = (f32[3,192,1]{2,1,0:T(8,128)S(1)}, f32[3,192,1]{2,1,0:T(8,128)S(1)}, u32[]{:S(2)}, u32[]{:S(2)}) collective-permute-start(f32[3,192,1]{2,1,0:T(8,128)S(1)} %get-tuple-element.31), channel_id=1, source_target_pairs={{16,0},{32,16},{48,32},{64,48},{80,64},{96,80},{112,96},{128,112},... | collective-permute-start | bytes 6920 | tf_op jit(solution)/shard_map/ppermute | solution.py:26
  13.7 9.5 %collective-permute-start.1 = (f32[3,192,1]{2,1,0:T(8,128)S(1)}, f32[3,192,1]{2,1,0:T(8,128)S(1)}, u32[]{:S(2)}, u32[]{:S(2)}) collective-permute-start(f32[3,192,1]{2,1,0:T(8,128)S(1)} %get-tuple-element.32), channel_id=1, source_target_pairs={{0,16},{16,32},{32,48},{48,64},{64,80},{80,96},{96,112},{112,128},... | collective-permute-start | bytes 6920 | tf_op jit(solution)/shard_map/ppermute | solution.py:25
  15.7 25.3 %copy-start.30 = (f32[192]{0:T(256)}, f32[192]{0:T(256)S(1)}, u32[]{:S(2)}) copy-start(f32[192]{0:T(256)S(1)} %get-tuple-element.60) | copy-start | bytes 2308
  15.7 25.3 %copy-start.33 = (f32[192]{0:T(256)}, f32[192]{0:T(256)S(1)}, u32[]{:S(2)}) copy-start(f32[192]{0:T(256)S(1)} %get-tuple-element.61) | copy-start | bytes 2308
  15.8 26.3 %copy-start.28 = (f32[192]{0:T(256)}, f32[192]{0:T(256)S(1)}, u32[]{:S(2)}) copy-start(f32[192]{0:T(256)S(1)} %get-tuple-element.10) | copy-start | bytes 2308
  15.8 27.1 %copy-start.16 = (f32[192]{0:T(256)}, f32[192]{0:T(256)S(1)}, u32[]{:S(2)}) copy-start(f32[192]{0:T(256)S(1)} %get-tuple-element.11) | copy-start | bytes 2308
  16.5 26.4 %copy-start.19 = (f32[192]{0:T(256)}, f32[192]{0:T(256)S(1)}, u32[]{:S(2)}) copy-start(f32[192]{0:T(256)S(1)} %get-tuple-element.58) | copy-start | bytes 2308
  16.5 26.4 %copy-start.21 = (f32[192]{0:T(256)}, f32[192]{0:T(256)S(1)}, u32[]{:S(2)}) copy-start(f32[192]{0:T(256)S(1)} %get-tuple-element.59) | copy-start | bytes 2308
  17.1 27.7 %copy-start.9 = (f32[65,450]{1,0:T(8,128)}, f32[65,450]{1,0:T(8,128)S(1)}, u32[]{:S(2)}) copy-start(f32[65,450]{1,0:T(8,128)S(1)} %get-tuple-element.53) | copy-start | bytes 351004
  17.1 27.7 %copy-start.11 = (f32[65,450]{1,0:T(8,128)}, f32[65,450]{1,0:T(8,128)S(1)}, u32[]{:S(2)}) copy-start(f32[65,450]{1,0:T(8,128)S(1)} %get-tuple-element.54) | copy-start | bytes 351004
  17.5 8.2 %copy-start.36 = (f32[3]{0:T(128)S(1)}, f32[3]{0:T(128)}, u32[]{:S(2)}) copy-start(f32[3]{0:T(128)} %constant.144.clone) | copy-start | bytes 40
  17.5 8.2 %collective-permute-start.3 = (f32[3,1,450]{2,0,1:T(4,128)S(1)}, f32[3,1,450]{2,0,1:T(4,128)S(1)}, u32[]{:S(2)}, u32[]{:S(2)}) collective-permute-start(f32[3,1,450]{2,0,1:T(4,128)S(1)} %get-tuple-element.45), channel_id=1, source_target_pairs={{0,1},{1,2},{2,3},{3,4},{4,5},{5,6},{6,7},{7,8},{8,9},{9,10},{10,1... | collective-permute-start | bytes 16208 | tf_op jit(solution)/shard_map/ppermute | solution.py:25
  25.8 10.4 %copy-start.26 = (f32[3,1,1]{2,0,1:T(4,128)}, f32[3,1,1]{2,0,1:T(4,128)S(1)}, u32[]{:S(2)}) copy-start(f32[3,1,1]{2,0,1:T(4,128)S(1)} %broadcast.385.clone) | copy-start | bytes 40
  27.7 4.7 %collective-permute-start.9 = (f32[3,1,450]{2,0,1:T(4,128)S(1)}, f32[3,1,450]{2,0,1:T(4,128)S(1)}, u32[]{:S(2)}, u32[]{:S(2)}) collective-permute-start(f32[3,1,450]{2,0,1:T(4,128)S(1)} %copy.294), channel_id=1, source_target_pairs={{1,0},{2,1},{3,2},{4,3},{5,4},{6,5},{7,6},{8,7},{9,8},{10,9},{11,1... | collective-permute-start | bytes 16208 | tf_op jit(solution)/shard_map/ppermute | solution.py:26
  29.8 6.4 %collective-permute-start.7 = (f32[3,450]{1,0:T(4,128)S(1)}, f32[3,450]{1,0:T(4,128)S(1)}, u32[]{:S(2)}, u32[]{:S(2)}) collective-permute-start(f32[3,450]{1,0:T(4,128)S(1)} %bitcast.211), channel_id=1, source_target_pairs={{0,128},{16,144},{32,160},{48,176},{64,192},{80,208},{96,224},{112... | collective-permute-start | bytes 16208 | tf_op jit(solution)/shard_map/ppermute | solution.py:33
  29.9 10.6 %collective-permute-start.5 = (f32[3,192,1]{2,1,0:T(8,128)S(1)}, f32[3,192,1]{2,1,0:T(8,128)S(1)}, u32[]{:S(2)}, u32[]{:S(2)}) collective-permute-start(f32[3,192,1]{2,1,0:T(8,128)S(1)} %get-tuple-element.25), channel_id=1, source_target_pairs={{16,0},{32,16},{48,32},{64,48},{80,64},{96,80},{112,96},{128,112},... | collective-permute-start | bytes 6920 | tf_op jit(solution)/shard_map/ppermute | solution.py:26
  32.3 8.3 %collective-permute-start.6 = (f32[3,192,1]{2,1,0:T(8,128)S(1)}, f32[3,192,1]{2,1,0:T(8,128)S(1)}, u32[]{:S(2)}, u32[]{:S(2)}) collective-permute-start(f32[3,192,1]{2,1,0:T(8,128)S(1)} %get-tuple-element.26), channel_id=1, source_target_pairs={{0,16},{16,32},{32,48},{48,64},{64,80},{80,96},{96,112},{112,128},... | collective-permute-start | bytes 6920 | tf_op jit(solution)/shard_map/ppermute | solution.py:25
  32.4 8.0 %collective-permute-start.8 = (f32[3,1,450]{2,0,1:T(4,128)S(1)}, f32[3,1,450]{2,0,1:T(4,128)S(1)}, u32[]{:S(2)}, u32[]{:S(2)}) collective-permute-start(f32[3,1,450]{2,0,1:T(4,128)S(1)} %get-tuple-element.40), channel_id=1, source_target_pairs={{0,1},{1,2},{2,3},{3,4},{4,5},{5,6},{6,7},{7,8},{8,9},{9,10},{10,1... | collective-permute-start | bytes 16208 | tf_op jit(solution)/shard_map/ppermute | solution.py:25
  42.1 1.6 copy-start.3
  49.4 14.7 %all-to-all-start = ((f32[16,1,4680]{2,1,0:T(1,128)}), f32[16,1,4680]{2,1,0:T(1,128)S(1)}, u32[]{:S(2)}, u32[]{:S(2)}) async-start(f32[16,1,4680]{2,1,0:T(1,128)} %reshape.469), calls=%async_computation | async-start | bytes 606208 | tf_op jit(solution)/shard_map/all_to_all | solution.py:73
  68.5 12.7 %all-to-all-start.1 = ((f32[16,1,6606]{2,1,0:T(1,128)}), f32[16,1,6606]{2,1,0:T(1,128)S(1)}, u32[]{:S(2)}, u32[]{:S(2)}) async-start(f32[16,1,6606]{2,1,0:T(1,128)} %all_to_all.19), calls=%async_computation.1 | async-start | bytes 851968 | tf_op jit(solution)/shard_map/all_to_all | solution.py:81
  74.9 10.9 %copy-start.13 = (f32[192,130]{1,0:T(8,128)}, f32[192,130]{1,0:T(8,128)S(1)}, u32[]{:S(2)}) copy-start(f32[192,130]{1,0:T(8,128)S(1)} %pad_maximum_fusion.45) | copy-start | bytes 299524
  86.6 3.8 %copy-start.25 = (f32[3,1,452]{2,1,0:T(1,128)S(1)}, f32[3,1,452]{2,1,0:T(1,128)}, u32[]{:S(2)}) copy-start(f32[3,1,452]{2,1,0:T(1,128)} %slice_multiply_fusion) | copy-start | bytes 16276
  86.6 12.7 %copy-start.37 = (f32[3]{0:T(128)S(1)}, f32[3]{0:T(128)}, u32[]{:S(2)}) copy-start(f32[3]{0:T(128)} %constant.144.clone) | copy-start | bytes 40
  86.6 12.7 %copy-start.39 = (pred[192]{0:T(512)(128)(4,1)S(1)}, pred[192]{0:T(512)(128)(4,1)}, u32[]{:S(2)}) copy-start(pred[192]{0:T(512)(128)(4,1)} %add_compare_fusion) | copy-start | bytes 580
  86.6 12.8 %copy-start.27 = (f32[3,1,1]{2,0,1:T(4,128)S(1)}, f32[3,1,1]{2,0,1:T(4,128)}, u32[]{:S(2)}) copy-start(f32[3,1,1]{2,0,1:T(4,128)} %copy-done.26) | copy-start | bytes 40
  86.6 12.9 %copy-start.17 = (f32[192]{0:T(256)S(1)}, f32[192]{0:T(256)}, u32[]{:S(2)}) copy-start(f32[192]{0:T(256)} %copy-done.16) | copy-start | bytes 2308
  86.7 12.9 %copy-start.31 = (f32[192]{0:T(256)S(1)}, f32[192]{0:T(256)}, u32[]{:S(2)}) copy-start(f32[192]{0:T(256)} %copy-done.30) | copy-start | bytes 2308
  86.7 12.9 %copy-start.34 = (f32[192]{0:T(256)S(1)}, f32[192]{0:T(256)}, u32[]{:S(2)}) copy-start(f32[192]{0:T(256)} %copy-done.33) | copy-start | bytes 2308
  86.7 4.5 %collective-permute-start.11 = (f32[3,1,450]{2,0,1:T(4,128)S(1)}, f32[3,1,450]{2,0,1:T(4,128)S(1)}, u32[]{:S(2)}, u32[]{:S(2)}) collective-permute-start(f32[3,1,450]{2,0,1:T(4,128)S(1)} %copy.259), channel_id=1, source_target_pairs={{1,0},{2,1},{3,2},{4,3},{5,4},{6,5},{7,6},{8,7},{9,8},{10,9},{11,1... | collective-permute-start | bytes 16208 | tf_op jit(solution)/shard_map/ppermute | solution.py:26
  91.3 8.0 %collective-permute-start.10 = (f32[3,1,450]{2,0,1:T(4,128)S(1)}, f32[3,1,450]{2,0,1:T(4,128)S(1)}, u32[]{:S(2)}, u32[]{:S(2)}) collective-permute-start(f32[3,1,450]{2,0,1:T(4,128)S(1)} %get-tuple-element.38), channel_id=1, source_target_pairs={{0,1},{1,2},{2,3},{3,4},{4,5},{5,6},{6,7},{7,8},{8,9},{9,10},{10,1... | collective-permute-start | bytes 16208 | tf_op jit(solution)/shard_map/ppermute | solution.py:25
  96.8 3.6 %copy-start.20 = (f32[192]{0:T(256)S(1)}, f32[192]{0:T(256)}, u32[]{:S(2)}) copy-start(f32[192]{0:T(256)} %copy-done.19) | copy-start | bytes 2308
  96.8 3.6 %copy-start.22 = (f32[192]{0:T(256)S(1)}, f32[192]{0:T(256)}, u32[]{:S(2)}) copy-start(f32[192]{0:T(256)} %copy-done.21) | copy-start | bytes 2308
  96.8 3.6 %copy-start.29 = (f32[192]{0:T(256)S(1)}, f32[192]{0:T(256)}, u32[]{:S(2)}) copy-start(f32[192]{0:T(256)} %copy-done.28) | copy-start | bytes 2308
  102.1 16.8 %copy-start.24 = (f32[3,1,1]{2,1,0:T(1,128)S(1)}, f32[3,1,1]{2,1,0:T(1,128)}, u32[]{:S(2)}) copy-start(f32[3,1,1]{2,1,0:T(1,128)} %copy-done.23) | copy-start | bytes 40
  102.1 4.4 %collective-permute-start.15 = (f32[3,1,450]{2,1,0:T(1,128)S(1)}, f32[3,1,450]{2,1,0:T(1,128)S(1)}, u32[]{:S(2)}, u32[]{:S(2)}) collective-permute-start(f32[3,1,450]{2,1,0:T(1,128)S(1)} %slice.667), channel_id=1, source_target_pairs={{1,0},{2,1},{3,2},{4,3},{5,4},{6,5},{7,6},{8,7},{9,8},{10,9},{11,1... | collective-permute-start | bytes 16208 | tf_op jit(solution)/shard_map/ppermute | solution.py:26
  106.5 8.0 %collective-permute-start.14 = (f32[3,1,450]{2,1,0:T(1,128)S(1)}, f32[3,1,450]{2,1,0:T(1,128)S(1)}, u32[]{:S(2)}, u32[]{:S(2)}) collective-permute-start(f32[3,1,450]{2,1,0:T(1,128)S(1)} %get-tuple-element.18), channel_id=1, source_target_pairs={{0,1},{1,2},{2,3},{3,4},{4,5},{5,6},{6,7},{7,8},{8,9},{9,10},{10,1... | collective-permute-start | bytes 16208 | tf_op jit(solution)/shard_map/ppermute | solution.py:25
  108.9 8.5 %collective-permute-start.12 = (f32[3,192,1]{2,1,0:T(8,128)S(1)}, f32[3,192,1]{2,1,0:T(8,128)S(1)}, u32[]{:S(2)}, u32[]{:S(2)}) collective-permute-start(f32[3,192,1]{2,1,0:T(8,128)S(1)} %get-tuple-element.19), channel_id=1, source_target_pairs={{16,0},{32,16},{48,32},{64,48},{80,64},{96,80},{112,96},{128,112},... | collective-permute-start | bytes 6920 | tf_op jit(solution)/shard_map/ppermute | solution.py:26
  113.1 5.8 %collective-permute-start.13 = (f32[3,192,1]{2,1,0:T(8,128)S(1)}, f32[3,192,1]{2,1,0:T(8,128)S(1)}, u32[]{:S(2)}, u32[]{:S(2)}) collective-permute-start(f32[3,192,1]{2,1,0:T(8,128)S(1)} %get-tuple-element.20), channel_id=1, source_target_pairs={{0,16},{16,32},{32,48},{48,64},{64,80},{80,96},{96,112},{112,128},... | collective-permute-start | bytes 6920 | tf_op jit(solution)/shard_map/ppermute | solution.py:25
  114.6 4.8 %copy-start.32 = (f32[192]{0:T(256)S(1)}, f32[192]{0:T(256)}, u32[]{:S(2)}) copy-start(f32[192]{0:T(256)} %copy-done.30) | copy-start | bytes 2308
  114.6 4.8 %copy-start.35 = (f32[192]{0:T(256)S(1)}, f32[192]{0:T(256)}, u32[]{:S(2)}) copy-start(f32[192]{0:T(256)} %copy-done.33) | copy-start | bytes 2308
  144.9 14.1 %copy-start.40 = (pred[192]{0:T(512)(128)(4,1)S(1)}, pred[192]{0:T(512)(128)(4,1)}, u32[]{:S(2)}) copy-start(pred[192]{0:T(512)(128)(4,1)} %add_compare_fusion) | copy-start | bytes 580
  (12 other events, 12.5 us)
